TPU v7x, 256 devices: a whole 4x4x8 slice. The times are simulated.
256 devices in a mesh: tile: 16 (over z, x_lo), obj: 16 (over x_hi, y, core).
Axes of the slice: x: 4 (x_hi: 2, x_lo: 2; x = x_hi * 2 + x_lo), y: 4, z: 8, core: 2. Of those that a mesh axis runs over, the one named last changes fastest.
Arguments:
- adjoint_in: float32 [256, 2, 256, 1024], P('obj', None, 'tile'), may hold values from -6 to 6
- checkpoint_store: float32 [64, 2, 256, 1024], P('obj', None, 'tile'), may hold values from 1900 to 2500, as said below
- interval: int32 [1], replicated, may hold values from 0 to 63
- sea_mask: int32 [256, 1024], P('tile'), may hold values 0 or 1
- zonal_speed: float32 [256, 1024], P('tile'), may hold values from -0.45 to 0.45
- mixing: float32 [256, 1024], P('tile'), may hold values from 0.02 to 0.2
- piston: float32 [256, 32], P('tile'), may hold values from 0.1 to 0.9
- cell_area: float32 [256, 32], P('tile'), may hold values from 5 to 50
- region: int32 [256, 32], P('tile'), may hold values from 0 to 255
Outputs:
- adjoint_out: float32 [256, 2, 256, 1024], P('obj', None, 'tile')
Inputs may be any that keep to these rules, and one draw needn't show every extreme that they name: region numbers name objectives. `checkpoint_store`: dissolved carbon lies in 1900 to 2100 and alkalinity exceeds it by 200 to 400 in every cell.
All inputs are finite; a program needn't handle non-finite values. No bound on the sum of `sea_mask` on one device may be relied on, other than what follows from the above.
Results may differ from a plain program's by a relative error of at most 0.0003.
Values sent between devices are 32-bit elements; how exact they have to be, the bound alone decides.
No kernel may reach another device: no remote copies, remote signals or barrier semaphores. Data moves between devices by JAX's collectives and lax.ppermute only.
A program may use at most 64 MiB of HBM per device.

v0:
```python
import jax
import jax.numpy as jnp
from jax import lax
from jax.sharding import PartitionSpec as P

ROWS = 32
LEVELS = 32
NEWTON = 4


DISSOCIATION_ONE = 1400.0
DISSOCIATION_TWO = 1.1
BORATE_CONSTANT = 2.5
BORON_TOTAL = 416.0
AIR_CARBON = 14.0
START_HYDROGEN = 2.0
ROW_DIFFUSION = 0.1


def padded(cells, sides, width):
    for axis, dim in sides:
        count = lax.axis_size(axis)
        head = lax.slice_in_dim(cells, 0, width, axis=dim)
        tail = lax.slice_in_dim(cells, cells.shape[dim] - width, cells.shape[dim], axis=dim)
        cells = jnp.concatenate(
            [
                lax.ppermute(tail, axis, [(i, (i + 1) % count) for i in range(count)]),
                cells,
                lax.ppermute(head, axis, [((i + 1) % count, i) for i in range(count)]),
            ],
            axis=dim,
        )
    return cells


def spread(value, axis, source):
    kept = jnp.where(lax.axis_index(axis) == source, value, 0).astype(value.dtype)
    return lax.psum(kept, axis)


def chemistry(carbon, alkalinity, piston, surface_sea):
    hydrogen = jnp.full_like(carbon, START_HYDROGEN)
    for iteration in range(NEWTON):
        square = hydrogen * hydrogen
        denominator = square + DISSOCIATION_ONE * hydrogen + DISSOCIATION_ONE * DISSOCIATION_TWO
        carbonate = carbon * DISSOCIATION_ONE * (hydrogen + 2.0 * DISSOCIATION_TWO) / denominator
        borate = BORON_TOTAL * BORATE_CONSTANT / (hydrogen + BORATE_CONSTANT)
        derivative = -carbon * DISSOCIATION_ONE * (
            square + 4.0 * DISSOCIATION_TWO * hydrogen + DISSOCIATION_ONE * DISSOCIATION_TWO
        ) / (denominator * denominator) - borate / (hydrogen + BORATE_CONSTANT)
        hydrogen = hydrogen - (carbonate + borate - alkalinity) / derivative
    square = hydrogen * hydrogen
    denominator = square + DISSOCIATION_ONE * hydrogen + DISSOCIATION_ONE * DISSOCIATION_TWO
    dissolved = carbon * square / denominator
    return surface_sea * piston * (AIR_CARBON - dissolved)


def forward_shift(source, offset):
    padding = jnp.zeros(source.shape[:-1] + (offset,), source.dtype)
    return jnp.concatenate([source[..., offset:], padding], axis=-1)


def backward_shift(source, offset):
    padding = jnp.zeros(source.shape[:-1] + (offset,), source.dtype)
    return jnp.concatenate([padding, source[..., :-offset]], axis=-1)


def column_weights(sea_float, mixing):
    cell_index = jnp.arange(LEVELS * ROWS, dtype=jnp.int32)
    row_open = (cell_index % ROWS < ROWS - 1).astype(jnp.float32)
    level_open = (cell_index // ROWS < LEVELS - 1).astype(jnp.float32)
    row_weight = ROW_DIFFUSION * row_open * sea_float * forward_shift(sea_float, 1)
    level_weight = mixing * level_open * sea_float * forward_shift(sea_float, ROWS)
    return (row_weight, level_weight)


def column_mix(source, row_weight, level_weight):
    row_flux = row_weight * (forward_shift(source, 1) - source)
    level_flux = level_weight * (forward_shift(source, ROWS) - source)
    return row_flux - backward_shift(row_flux, 1) + level_flux - backward_shift(level_flux, ROWS)


def zonal_weights(sea_float, sea_east, velocity):
    opened = sea_float * sea_east
    magnitude = jnp.abs(velocity)
    return jnp.stack(
        [
            opened * (-velocity - magnitude) / 12.0,
            opened * (7.0 * velocity + 3.0 * magnitude) / 12.0,
            opened * (7.0 * velocity - 3.0 * magnitude) / 12.0,
            opened * (magnitude - velocity) / 12.0,
        ]
    )


def trim_rim(source, keep_rim, outer_rim, dimension):
    length = source.shape[dimension] - 2 * outer_rim
    return lax.slice_in_dim(
        source, outer_rim - keep_rim, outer_rim + length + keep_rim, axis=dimension
    )


def surface_slopes(carbon, alkalinity, piston, surface_sea):

    def uptake_of(carbon_in, alkalinity_in):
        return chemistry(carbon_in, alkalinity_in, piston, surface_sea)

    uptake, pullback = jax.vjp(uptake_of, carbon, alkalinity)
    by_carbon, by_alkalinity = pullback(jnp.ones_like(carbon))
    return (uptake, jnp.stack([by_carbon, by_alkalinity]))


def advance_rim(extended, weights, row_weight, level_weight, uptake):
    length = extended.shape[1]
    face_flux = (
        weights[0, 1 : length - 2] * extended[:, 0 : length - 3]
        + weights[1, 1 : length - 2] * extended[:, 1 : length - 2]
        + weights[2, 1 : length - 2] * extended[:, 2 : length - 1]
        + weights[3, 1 : length - 2] * extended[:, 3:length]
    )
    interior = extended[:, 2 : length - 2]
    zonal_term = -(face_flux[:, 1:] - face_flux[:, :-1])
    transported = interior + zonal_term + column_mix(interior, row_weight, level_weight)
    surface_row = transported[0, :, :ROWS] + uptake
    carbon = jnp.concatenate([surface_row, transported[0, :, ROWS:]], axis=-1)
    return jnp.stack([carbon, transported[1]])


def retreat(extended, weights, row_weight, level_weight, slopes, objective_seeds):
    length = extended.shape[2]
    difference = extended[:, :, 1:] - extended[:, :, :-1]
    zonal_term = (
        weights[0, 3 : length - 1] * difference[:, :, 3 : length - 1]
        + weights[1, 2 : length - 2] * difference[:, :, 2 : length - 2]
        + weights[2, 1 : length - 3] * difference[:, :, 1 : length - 3]
        + weights[3, 0 : length - 4] * difference[:, :, 0 : length - 4]
    )
    interior = extended[:, :, 2 : length - 2]
    adjoint = interior + zonal_term + column_mix(interior, row_weight, level_weight)
    forcing = interior[:, 0, :, :ROWS] + objective_seeds
    surface = adjoint[..., :ROWS] + slopes[None] * forcing[:, None]
    return jnp.concatenate([surface, adjoint[..., ROWS:]], axis=-1)


def body(
    adjoint_in, checkpoint_store, interval, sea_mask, zonal_speed, mixing, piston, cell_area, region
):
    groups = adjoint_in.shape[0]
    cell_count = adjoint_in.shape[3]
    rim_depth = 2
    statics = jnp.concatenate(
        [
            sea_mask.astype(jnp.float32),
            zonal_speed,
            mixing,
            piston,
            cell_area,
            region.astype(jnp.float32),
        ],
        axis=1,
    )
    widened = padded(statics, (("tile", 0),), rim_depth)
    sea_wide = widened[:, :cell_count]
    speed_wide = widened[:, cell_count : 2 * cell_count]
    mixing_wide = widened[:, 2 * cell_count : 3 * cell_count]
    offset = 3 * cell_count
    piston_wide = widened[:, offset : offset + ROWS]
    area_wide = widened[:, offset + ROWS : offset + 2 * ROWS]
    region_wide = widened[:, offset + 2 * ROWS : offset + 3 * ROWS]
    sea_east = jnp.concatenate([sea_wide[1:], jnp.zeros_like(sea_wide[:1])], axis=0)
    weights = zonal_weights(sea_wide, sea_east, speed_wide)
    row_weight, level_weight = column_weights(sea_wide, mixing_wide)
    surface_sea = sea_wide[:, :ROWS]
    targets = (lax.axis_index("obj") * groups + jnp.arange(groups, dtype=jnp.int32)).astype(
        jnp.float32
    )
    objective_seeds = area_wide[None] * (region_wide[None] == targets[:, None, None]).astype(
        jnp.float32
    )
    owners = lax.axis_size("obj")
    owner_index = interval[0] % owners
    stored = lax.dynamic_index_in_dim(checkpoint_store, interval[0] // owners, 0, keepdims=False)
    linearize_extended = padded(spread(stored, "obj", owner_index), (("tile", 1),), rim_depth)
    inner_rim = rim_depth - 2
    piston_inner = trim_rim(piston_wide, inner_rim, rim_depth, 0)
    sea_inner = trim_rim(surface_sea, inner_rim, rim_depth, 0)
    initial_inner = trim_rim(linearize_extended, inner_rim, rim_depth, 1)
    uptake_first, slopes_first = surface_slopes(
        initial_inner[0, :, :ROWS], initial_inner[1, :, :ROWS], piston_inner, sea_inner
    )
    following = advance_rim(
        linearize_extended,
        weights,
        trim_rim(row_weight, inner_rim, rim_depth, 0),
        trim_rim(level_weight, inner_rim, rim_depth, 0),
        uptake_first,
    )
    _, slopes_second = surface_slopes(
        following[0, :, :ROWS], following[1, :, :ROWS], piston_inner, sea_inner
    )
    slopes = jnp.stack([slopes_first, slopes_second])
    adjoint = adjoint_in
    for substep in (1, 0):
        extended = padded(adjoint, (("tile", 2),), 2)
        rim_in = 0 + 2
        adjoint = retreat(
            extended,
            trim_rim(weights, rim_in, rim_depth, 1),
            trim_rim(row_weight, 0, rim_depth, 0),
            trim_rim(level_weight, 0, rim_depth, 0),
            trim_rim(slopes[substep], 0, rim_depth - 2, 1),
            trim_rim(objective_seeds, 0, rim_depth, 1),
        )
    return adjoint


def solution(mesh):
    placed = (
        P("obj", None, "tile", None),
        P("obj", None, "tile", None),
        P(),
        P("tile", None),
        P("tile", None),
        P("tile", None),
        P("tile", None),
        P("tile", None),
        P("tile", None),
    )
    return jax.shard_map(
        body, mesh=mesh, in_specs=placed, out_specs=P("obj", None, "tile", None), check_vma=False
    )
```

profile of v0, /device:TPU:1, one launch (start us, length us, event | category | flops | bytes accessed | tf_op | source)
XLA Modules:
  0.0 209.7 jit_solution(15050452365637785768)
XLA Ops:
  7.2 1.6 select_bitcast_fusion
  10.4 1.0 concatenate.75
  11.3 2.1 %collective-permute-start = (f32[2,3168]{1,0:T(2,128)S(1)}, f32[2,3168]{1,0:T(2,128)S(1)}, u32[]{:S(2)}, u32[]{:S(2)}) collective-permute-start(f32[2,3168]{1,0:T(2,128)S(1)} %get-tuple-element.39), channel_id=1, source_target_pairs={{0,16},{16,32},{32,48},{48,64},{64,80},{80,96},{96,112},{112,128},... | collective-permute-start | bytes 76040 | tf_op jit(solution)/shard_map/ppermute | solution.py:27
  13.4 5.4 %collective-permute-start.1 = (f32[2,3168]{1,0:T(2,128)S(1)}, f32[2,3168]{1,0:T(2,128)S(1)}, u32[]{:S(2)}, u32[]{:S(2)}) collective-permute-start(f32[2,3168]{1,0:T(2,128)S(1)} %get-tuple-element.40), channel_id=1, source_target_pairs={{16,0},{32,16},{48,32},{64,48},{80,64},{96,80},{112,96},{128,112},... | collective-permute-start | bytes 76040 | tf_op jit(solution)/shard_map/ppermute | solution.py:29
  18.8 2.8 %copy.14 = f32[16,2,16,1024]{3,0,2,1:T(8,128)S(1)} copy(f32[16,2,16,1024]{3,2,1,0:T(8,128)} %param.9) | data formatting | bytes 4194304 | tf_op args[0]
  22.5 1.4 collective-permute-start.3
  24.0 2.0 slice.328
  25.9 1.9 slice.322
  28.6 133.8 %all-reduce.17.cloned.1.call-done = f32[2,16,1024]{2,1,0:T(8,128)} async-done(((f32[2,16,1024]{2,1,0:T(8,128)}), f32[2,16,1024]{2,1,0:T(8,128)}) %all-reduce.17.cloned.1.call-update) | async-done | bytes 131088 | tf_op jit(solution)/shard_map/psum | solution.py:38
  162.3 0.9 fusion.65
  163.6 3.3 %collective-permute-start.5 = (f32[2,2,1024]{2,1,0:T(2,128)S(1)}, f32[2,2,1024]{2,1,0:T(2,128)S(1)}, u32[]{:S(2)}, u32[]{:S(2)}) collective-permute-start(f32[2,2,1024]{2,1,0:T(2,128)S(1)} %get-tuple-element.47), channel_id=1, source_target_pairs={{16,0},{32,16},{48,32},{64,48},{80,64},{96,80},{112,96},{128,112},... | collective-permute-start | bytes 49160 | tf_op jit(solution)/shard_map/ppermute | solution.py:29
  166.9 1.0 slice.346
  167.9 1.0 slice.344
  168.9 1.1 subtract_multiply_fusion.5
  170.1 1.1 add_bitcast_fusion.1
  171.2 1.1 fusion.13
  172.9 3.5 %subtract_multiply_fusion.3 = (f32[16,2,16,1024]{3,0,2,1:T(8,128)S(1)}, f32[16,2,20,1024]{3,0,2,1:T(8,128)S(1)}, f32[16,2,16,1024]{3,0,2,1:T(8,128)S(1)}) fusion(f32[16,2,16,1023]{3,0,2,1:T(8,128)} %slice.322, f32[16,1024]{1,0:T(8,128)S(1)} %get-tuple-element.48, f32[16,2,16,1024]{3,2,1,0:T(8,128)S(1)} %copy-done, ...), kind=kLoop, calls=%fused_computation.30 | loop fusion | flops 2097152 | bytes 12711936 | tf_op jit(solution)/shard_map/mul | solution.py:78
  176.8 4.4 %fusion.8 = f32[16,2,16,1024]{3,0,2,1:T(8,128)S(1)} fusion(f32[16,2,19,1024]{3,0,2,1:T(8,128)S(1)} %slice_subtract_fusion.1, f32[16,2,16,992]{3,0,2,1:T(8,128)S(1)} %bitcast.349, f32[16,2,16,1024]{3,0,2,1:T(8,128)S(1)} %get-tuple-element.29, f32[16,2,16,1024]{3,0,2,1:T(8,128)S(1)} %get-tuple-element.27, f32[16,2,16,1023]{3,0,2,1:T(8,128)S(1)} %bitcast.348, ...), kind=kLoop, calls=%fused_computation.20 | loop fusion | flops 6291456 | bytes 21166080 | tf_op jit(solution)/shard_map/add | solution.py:139
  182.8 3.6 %collective-permute-start.7 = (f32[16,2,2,1024]{3,0,2,1:T(8,128)S(1)}, f32[16,2,2,1024]{3,0,2,1:T(8,128)S(1)}, u32[]{:S(2)}, u32[]{:S(2)}) collective-permute-start(f32[16,2,2,1024]{3,0,2,1:T(8,128)S(1)} %get-tuple-element.26), channel_id=1, source_target_pairs={{16,0},{32,16},{48,32},{64,48},{80,64},{96,80},{112,96},{128,112},... | collective-permute-start | bytes 786440 | tf_op jit(solution)/shard_map/ppermute | solution.py:29
  186.4 1.2 subtract_multiply_fusion.1
  187.7 5.3 %collective-permute-done.6 = f32[16,2,2,1024]{3,0,2,1:T(8,128)S(1)} collective-permute-done((f32[16,2,2,1024]{3,0,2,1:T(8,128)S(1)}, f32[16,2,2,1024]{3,0,2,1:T(8,128)S(1)}, u32[]{:S(2)}, u32[]{:S(2)}) %collective-permute-start.6) | collective-permute-done | bytes 262176 | tf_op jit(solution)/shard_map/ppermute | solution.py:27
  193.1 2.2 %collective-permute-done.7 = f32[16,2,2,1024]{3,0,2,1:T(8,128)S(1)} collective-permute-done((f32[16,2,2,1024]{3,0,2,1:T(8,128)S(1)}, f32[16,2,2,1024]{3,0,2,1:T(8,128)S(1)}, u32[]{:S(2)}, u32[]{:S(2)}) %collective-permute-start.7) | collective-permute-done | bytes 262176 | tf_op jit(solution)/shard_map/ppermute | solution.py:29
  196.1 2.9 %fusion.3 = f32[16,2,16,1024]{3,0,2,1:T(8,128)S(1)} fusion(f32[16,2,19,1024]{3,0,2,1:T(8,128)S(1)} %slice_subtract_fusion, f32[16,2,16,992]{3,0,2,1:T(8,128)S(1)} %bitcast.350, f32[16,2,16,1024]{3,0,2,1:T(8,128)S(1)} %get-tuple-element.23, f32[16,2,16,1023]{3,0,2,1:T(8,128)S(1)} %bitcast.347, f32[16,2,16,992]{3,0,2,1:T(8,128)S(1)} %slice.357, ...), kind=kLoop, calls=%fused_computation.11 | loop fusion | flops 7864320 | bytes 19134464 | tf_op jit(solution)/shard_map/add | solution.py:139
  200.4 2.5 %copy.20 = f32[16,2,16,1024]{3,2,1,0:T(8,128)} copy(f32[16,2,16,1024]{3,0,2,1:T(8,128)S(1)} %pad_maximum_fusion.2) | data formatting | bytes 4194304 | tf_op jit(solution)/shard_map/concatenate | solution.py:142
  (63 shorter events, 8.3 us)
Async XLA Ops:
  6.5 155.8 %all-reduce.17.cloned.1.call-start = ((), (), s32[]{:S(2)}) async-start(), calls=%async_computation | async-start | bytes 262144 | tf_op jit(solution)/shard_map/psum | solution.py:38
  11.3 16.5 %collective-permute-start = (f32[2,3168]{1,0:T(2,128)S(1)}, f32[2,3168]{1,0:T(2,128)S(1)}, u32[]{:S(2)}, u32[]{:S(2)}) collective-permute-start(f32[2,3168]{1,0:T(2,128)S(1)} %get-tuple-element.39), channel_id=1, source_target_pairs={{0,16},{16,32},{32,48},{48,64},{64,80},{80,96},{96,112},{112,128},... | collective-permute-start | bytes 76040 | tf_op jit(solution)/shard_map/ppermute | solution.py:27
  13.4 14.4 %collective-permute-start.1 = (f32[2,3168]{1,0:T(2,128)S(1)}, f32[2,3168]{1,0:T(2,128)S(1)}, u32[]{:S(2)}, u32[]{:S(2)}) collective-permute-start(f32[2,3168]{1,0:T(2,128)S(1)} %get-tuple-element.40), channel_id=1, source_target_pairs={{16,0},{32,16},{48,32},{64,48},{80,64},{96,80},{112,96},{128,112},... | collective-permute-start | bytes 76040 | tf_op jit(solution)/shard_map/ppermute | solution.py:29
  22.5 153.9 %collective-permute-start.3 = (f32[16,2,2,1024]{3,0,2,1:T(8,128)}, f32[16,2,2,1024]{3,0,2,1:T(8,128)S(1)}, u32[]{:S(2)}, u32[]{:S(2)}) collective-permute-start(f32[16,2,2,1024]{3,0,2,1:T(8,128)} %get-tuple-element.30), channel_id=1, source_target_pairs={{16,0},{32,16},{48,32},{64,48},{80,64},{96,80},{112,96},{128,112},... | collective-permute-start | bytes 786440 | tf_op jit(solution)/shard_map/ppermute | solution.py:29
  23.9 149.0 %collective-permute-start.2 = (f32[16,2,2,1024]{3,0,2,1:T(8,128)}, f32[16,2,2,1024]{3,0,2,1:T(8,128)S(1)}, u32[]{:S(2)}, u32[]{:S(2)}) collective-permute-start(f32[16,2,2,1024]{3,0,2,1:T(8,128)} %get-tuple-element.31), channel_id=1, source_target_pairs={{0,16},{16,32},{32,48},{48,64},{64,80},{80,96},{96,112},{112,128},... | collective-permute-start | bytes 786440 | tf_op jit(solution)/shard_map/ppermute | solution.py:27
  28.2 141.8 %copy-start.3 = (f32[16,32]{1,0:T(8,128)S(1)}, f32[16,32]{1,0:T(8,128)}, u32[]{:S(2)}) copy-start(f32[16,32]{1,0:T(8,128)} %param.15) | copy-start | bytes 6148
  162.3 9.9 %copy-start.2 = (f32[2,16,1024]{2,1,0:T(8,128)S(1)}, f32[2,16,1024]{2,1,0:T(8,128)}, u32[]{:S(2)}) copy-start(f32[2,16,1024]{2,1,0:T(8,128)} %all-reduce.17.cloned.1.call-done) | copy-start | bytes 393220
  163.3 7.9 %collective-permute-start.4 = (f32[2,2,1024]{2,1,0:T(2,128)S(1)}, f32[2,2,1024]{2,1,0:T(2,128)S(1)}, u32[]{:S(2)}, u32[]{:S(2)}) collective-permute-start(f32[2,2,1024]{2,1,0:T(2,128)S(1)} %get-tuple-element.46), channel_id=1, source_target_pairs={{0,16},{16,32},{32,48},{48,64},{64,80},{80,96},{96,112},{112,128},... | collective-permute-start | bytes 49160 | tf_op jit(solution)/shard_map/ppermute | solution.py:27
  163.6 7.5 %collective-permute-start.5 = (f32[2,2,1024]{2,1,0:T(2,128)S(1)}, f32[2,2,1024]{2,1,0:T(2,128)S(1)}, u32[]{:S(2)}, u32[]{:S(2)}) collective-permute-start(f32[2,2,1024]{2,1,0:T(2,128)S(1)} %get-tuple-element.47), channel_id=1, source_target_pairs={{16,0},{32,16},{48,32},{64,48},{80,64},{96,80},{112,96},{128,112},... | collective-permute-start | bytes 49160 | tf_op jit(solution)/shard_map/ppermute | solution.py:29
  168.9 4.0 %copy-start = (f32[16,2,16,1024]{3,2,1,0:T(8,128)S(1)}, f32[16,2,16,1024]{3,2,1,0:T(8,128)}, u32[]{:S(2)}) copy-start(f32[16,2,16,1024]{3,2,1,0:T(8,128)} %param.9) | copy-start | bytes 6291460
  168.9 3.9 %copy-start.1 = (f32[16,2,16,992]{3,0,2,1:T(8,128)S(1)}, f32[16,2,16,992]{3,0,2,1:T(8,128)}, u32[]{:S(2)}) copy-start(f32[16,2,16,992]{3,0,2,1:T(8,128)} %slice.328) | copy-start | bytes 6094852
  182.8 10.3 %collective-permute-start.6 = (f32[16,2,2,1024]{3,0,2,1:T(8,128)S(1)}, f32[16,2,2,1024]{3,0,2,1:T(8,128)S(1)}, u32[]{:S(2)}, u32[]{:S(2)}) collective-permute-start(f32[16,2,2,1024]{3,0,2,1:T(8,128)S(1)} %get-tuple-element.25), channel_id=1, source_target_pairs={{0,16},{16,32},{32,48},{48,64},{64,80},{80,96},{96,112},{112,128},... | collective-permute-start | bytes 786440 | tf_op jit(solution)/shard_map/ppermute | solution.py:27
  182.8 12.4 %collective-permute-start.7 = (f32[16,2,2,1024]{3,0,2,1:T(8,128)S(1)}, f32[16,2,2,1024]{3,0,2,1:T(8,128)S(1)}, u32[]{:S(2)}, u32[]{:S(2)}) collective-permute-start(f32[16,2,2,1024]{3,0,2,1:T(8,128)S(1)} %get-tuple-element.26), channel_id=1, source_target_pairs={{16,0},{32,16},{48,32},{64,48},{80,64},{96,80},{112,96},{128,112},... | collective-permute-start | bytes 786440 | tf_op jit(solution)/shard_map/ppermute | solution.py:29
Sparse Core Ops, SparseCore 0:
  9.9 152.3 all-reduce.16
where the time goes:
time: 210 us
  waiting for transfers between devices  141 us (67%)
  other arithmetic  22.1 us (11%)
  starting transfers between devices  16.3 us (8%)
  local copies, waits for them, and re-layouts  15.6 us (7%)
  between operations  14.4 us (7%)
    psum x1, waiting for transfers between devices, spread(): return lax.psum(kept, axis)  134 us
    ppermute x4, starting transfers between devices, padded(): lax.ppermute(head, axis, [((i + 1) % count, i) for i in range(count)])  13.6 us
    add x2, other arithmetic, retreat(): interior + zonal_term + column_mix(interior, row_weight, level_weight)  7.35 us
    slice x6, local copies, waits for them, and re-layouts, forward_shift(): return jnp.concatenate([source[..., offset:], padding], axis=-1)  6.04 us
    mul x3, other arithmetic, column_mix(): row_flux = row_weight * (forward_shift(source, 1) - source)  5.84 us
    ppermute x4, waiting for transfers between devices, padded(): lax.ppermute(tail, axis, [(i, (i + 1) % count) for i in range(count)])  5.32 us
  transfers between devices with their start and end apart: 9, of which 3 were waited for; matrix products, arithmetic and copies ran while one was open for 11% of the time, Pallas kernels for 0%

commit v1 on v0

--- a/solution.py
+++ b/solution.py
@@ -147,7 +147,7 @@
 ):
     groups = adjoint_in.shape[0]
     cell_count = adjoint_in.shape[3]
-    rim_depth = 2
+    rim_depth = 4
     statics = jnp.concatenate(
         [
             sea_mask.astype(jnp.float32),
@@ -179,39 +179,44 @@
     )
     owners = lax.axis_size("obj")
     owner_index = interval[0] % owners
+    band = 2 * ROWS
     stored = lax.dynamic_index_in_dim(checkpoint_store, interval[0] // owners, 0, keepdims=False)
-    linearize_extended = padded(spread(stored, "obj", owner_index), (("tile", 1),), rim_depth)
-    inner_rim = rim_depth - 2
+    stored = spread(stored[:, :, :band], "obj", owner_index)
+    initial_wide = padded(stored, (("tile", 1),), rim_depth)
+    inner_rim = 2
     piston_inner = trim_rim(piston_wide, inner_rim, rim_depth, 0)
     sea_inner = trim_rim(surface_sea, inner_rim, rim_depth, 0)
-    initial_inner = trim_rim(linearize_extended, inner_rim, rim_depth, 1)
+    initial_inner = trim_rim(initial_wide, inner_rim, rim_depth, 1)
     uptake_first, slopes_first = surface_slopes(
         initial_inner[0, :, :ROWS], initial_inner[1, :, :ROWS], piston_inner, sea_inner
     )
     following = advance_rim(
-        linearize_extended,
+        initial_wide,
+        weights[:, :, :band],
+        trim_rim(row_weight, inner_rim, rim_depth, 0)[:, :band],
+        trim_rim(level_weight, inner_rim, rim_depth, 0)[:, :band],
+        uptake_first,
+    )
+    _, slopes_second = surface_slopes(
+        following[0, :, :ROWS], following[1, :, :ROWS], piston_inner, sea_inner
+    )
+    extended = padded(adjoint_in, (("tile", 2),), rim_depth)
+    middle = retreat(
+        extended,
         weights,
         trim_rim(row_weight, inner_rim, rim_depth, 0),
         trim_rim(level_weight, inner_rim, rim_depth, 0),
-        uptake_first,
-    )
-    _, slopes_second = surface_slopes(
-        following[0, :, :ROWS], following[1, :, :ROWS], piston_inner, sea_inner
-    )
-    slopes = jnp.stack([slopes_first, slopes_second])
-    adjoint = adjoint_in
-    for substep in (1, 0):
-        extended = padded(adjoint, (("tile", 2),), 2)
-        rim_in = 0 + 2
-        adjoint = retreat(
-            extended,
-            trim_rim(weights, rim_in, rim_depth, 1),
-            trim_rim(row_weight, 0, rim_depth, 0),
-            trim_rim(level_weight, 0, rim_depth, 0),
-            trim_rim(slopes[substep], 0, rim_depth - 2, 1),
-            trim_rim(objective_seeds, 0, rim_depth, 1),
-        )
-    return adjoint
+        slopes_second,
+        trim_rim(objective_seeds, inner_rim, rim_depth, 1),
+    )
+    return retreat(
+        middle,
+        trim_rim(weights, inner_rim, rim_depth, 1),
+        trim_rim(row_weight, 0, rim_depth, 0),
+        trim_rim(level_weight, 0, rim_depth, 0),
+        trim_rim(slopes_first, 0, inner_rim, 1),
+        trim_rim(objective_seeds, 0, rim_depth, 1),
+    )
 
 
 def solution(mesh):

time: 210 us -> 127 us (0.60)
  waiting for transfers between devices: 141 us -> 15.4 us
  blocking collectives: 0 us -> 65.3 us
  between operations: 14.4 us -> 1.15 us
  other arithmetic: 22.1 us -> 18.5 us
  starting transfers between devices: 16.3 us -> 12.9 us
    psum x1 -> x0, waiting for transfers between devices: 134 us -> none  [spread(): return lax.psum(kept, axis)]
    psum x0 -> x1, blocking collectives: none -> 65.3 us  [spread(): return lax.psum(kept, axis)]
    ppermute x4 -> x3, waiting for transfers between devices: 5.32 us -> 13.3 us  [padded(): lax.ppermute(tail, axis, [(i, (i + 1) % count) for i in range(count)])]
    mul x3 -> x2, other arithmetic: 5.84 us -> 1.9 us  [column_mix(): row_flux = row_weight * (forward_shift(source, 1) - source)]
    concatenate x3 -> x0, local copies, waits for them, and re-layouts: 2.57 us -> none  [the longest x1 2.54 us: retreat(): return jnp.concatenate([surface, adjoint[..., ROWS:]], axis=-1)]
    unnamed x10 -> x22, local copies, waits for them, and re-layouts: 2.85 us -> 0.36 us
    ppermute x4 -> x3, starting transfers between devices: 2.64 us -> 0.48 us  [padded(): lax.ppermute(tail, axis, [(i, (i + 1) % count) for i in range(count)])]
    add x2 -> x3, other arithmetic: 7.35 us -> 9.16 us  [retreat(): interior + zonal_term + column_mix(interior, row_weight, level_weight)]
  transfers between devices with their start and end apart: 9 -> 6, of which waited for: 3 -> 2; matrix products, arithmetic and copies ran while one was open for 11% -> 8% of each run, Pallas kernels for 0% -> 0%
where the time goes in v1:
time: 127 us
  blocking collectives  65.3 us (51%)
  other arithmetic  18.5 us (15%)
  waiting for transfers between devices  15.4 us (12%)
  local copies, waits for them, and re-layouts  13.8 us (11%)
  starting transfers between devices  12.9 us (10%)
    psum x1, blocking collectives, spread(): return lax.psum(kept, axis)  65.3 us
    ppermute x3, waiting for transfers between devices, padded(): lax.ppermute(tail, axis, [(i, (i + 1) % count) for i in range(count)])  13.3 us
    ppermute x3, starting transfers between devices, padded(): lax.ppermute(head, axis, [((i + 1) % count, i) for i in range(count)])  12.5 us
    add x3, other arithmetic, retreat(): interior + zonal_term + column_mix(interior, row_weight, level_weight)  9.16 us
    slice x7, local copies, waits for them, and re-layouts, forward_shift(): return jnp.concatenate([source[..., offset:], padding], axis=-1)  5.15 us
  transfers between devices with their start and end apart: 6, of which 2 were waited for; matrix products, arithmetic and copies ran while one was open for 8% of the time, Pallas kernels for 0%

profile of v1, /device:TPU:1, one launch (start us, length us, event | category | flops | bytes accessed | tf_op | source)
XLA Modules:
  0.0 127.1 jit_solution(1453807047856551090)
XLA Ops:
  1.1 65.3 %psum.7 = f32[2,16,64]{2,1,0:T(8,128)S(1)} all-reduce(f32[2,16,64]{2,1,0:T(8,128)S(1)} %slice_select_fusion), channel_id=1, replica_groups=mesh['tile'=16,'obj'=16] {'obj'}, use_global_device_ids=true, to_apply=%region_0.1 | all-reduce | flops 2048 | bytes 16384 | tf_op jit(solution)/shard_map/psum | solution.py:38
  66.7 5.3 %collective-permute-start.5 = (f32[2,4,64]{2,1,0:T(4,128)S(1)}, f32[2,4,64]{2,1,0:T(4,128)S(1)}, u32[]{:S(2)}, u32[]{:S(2)}) collective-permute-start(f32[2,4,64]{2,1,0:T(4,128)S(1)} %get-tuple-element.44), channel_id=1, source_target_pairs={{16,0},{32,16},{48,32},{64,48},{80,64},{96,80},{112,96},{128,112},... | collective-permute-start | bytes 6152 | tf_op jit(solution)/shard_map/ppermute | solution.py:29
  72.0 0.7 convert_element_type.25
  72.7 0.8 convert_element_type.24
  73.5 1.0 concatenate.67
  74.6 3.6 %collective-permute-start.3 = (f32[4,3168]{1,0:T(4,128)S(1)}, f32[4,3168]{1,0:T(4,128)S(1)}, u32[]{:S(2)}, u32[]{:S(2)}) collective-permute-start(f32[4,3168]{1,0:T(4,128)S(1)} %get-tuple-element.38), channel_id=1, source_target_pairs={{16,0},{32,16},{48,32},{64,48},{80,64},{96,80},{112,96},{128,112},... | collective-permute-start | bytes 152072 | tf_op jit(solution)/shard_map/ppermute | solution.py:29
  78.1 1.8 %fusion.65 = (f32[16,2,4,1024]{3,2,0,1:T(4,128)S(1)}, f32[16,2,4,1024]{3,2,0,1:T(4,128)S(1)}) fusion(f32[16,2,16,1024]{3,2,1,0:T(8,128)} %param.9), kind=kLoop, calls=%fused_computation.232 | loop fusion | bytes 2097152 | tf_op jit(solution)/shard_map/slice | solution.py:24
  80.1 3.6 %collective-permute-start.1 = (f32[16,2,4,1024]{3,2,0,1:T(4,128)S(1)}, f32[16,2,4,1024]{3,2,0,1:T(4,128)S(1)}, u32[]{:S(2)}, u32[]{:S(2)}) collective-permute-start(f32[16,2,4,1024]{3,2,0,1:T(4,128)S(1)} %get-tuple-element.29), channel_id=1, source_target_pairs={{16,0},{32,16},{48,32},{64,48},{80,64},{96,80},{112,96},{128,112},... | collective-permute-start | bytes 1572872 | tf_op jit(solution)/shard_map/ppermute | solution.py:29
  84.2 0.7 slice_bitcast_fusion.7
  84.9 0.7 slice_bitcast_fusion.5
  87.9 0.7 slice_bitcast_fusion.3
  88.5 0.7 slice_bitcast_fusion.1
  89.2 13.3 %collective-permute-done = f32[16,2,4,1024]{3,2,0,1:T(4,128)S(1)} collective-permute-done((f32[16,2,4,1024]{3,2,0,1:T(4,128)S(1)}, f32[16,2,4,1024]{3,2,0,1:T(4,128)S(1)}, u32[]{:S(2)}, u32[]{:S(2)}) %collective-permute-start) | collective-permute-done | bytes 524320 | tf_op jit(solution)/shard_map/ppermute | solution.py:27
  102.5 2.1 %collective-permute-done.1 = f32[16,2,4,1024]{3,2,0,1:T(4,128)S(1)} collective-permute-done((f32[16,2,4,1024]{3,2,0,1:T(4,128)S(1)}, f32[16,2,4,1024]{3,2,0,1:T(4,128)S(1)}, u32[]{:S(2)}, u32[]{:S(2)}) %collective-permute-start.1) | collective-permute-done | bytes 524320 | tf_op jit(solution)/shard_map/ppermute | solution.py:29
  105.2 1.2 slice.398
  106.9 2.9 %slice.403 = f32[16,2,20,992]{3,2,0,1:T(8,128)} slice(f32[16,2,24,1024]{3,2,0,1:T(8,128)S(1)} %pad_maximum_fusion), slice={[0:16], [0:2], [2:22], [32:1024]} | slice | bytes 5079040 | tf_op jit(solution)/shard_map/slice | solution.py:60
  109.8 4.3 %fusion.4 = (f32[16,2,20,1024]{3,2,0,1:T(8,128)S(1)}, f32[16,2,20,1024]{3,2,0,1:T(8,128)S(1)}, f32[16,2,20,1024]{3,2,0,1:T(8,128)S(1)}) fusion(f32[16,2,23,1024]{3,2,0,1:T(8,128)S(1)} %slice_subtract_fusion, f32[16,2,24,1024]{3,2,0,1:T(8,128)S(1)} %pad_maximum_fusion, f32[20,1024]{1,0:T(8,128)S(1)} %copy-done.3, f32[20,1024]{1,0:T(8,128)S(1)} %copy-done.4, ...), kind=kLoop, calls=%fused_computation.8 | loop fusion | flops 7864320 | bytes 26621440 | tf_op jit(solution)/shard_map/add | solution.py:139
  114.1 2.4 %copy_add_fusion = f32[16,2,20,1024]{3,2,1,0:T(8,128)S(1)} fusion(f32[16,2,20,1024]{3,2,0,1:T(8,128)S(1)} %get-tuple-element.25, f32[16,2,20,992]{3,2,0,1:T(8,128)S(1)} %bitcast.356, f32[16,2,20,1024]{3,2,0,1:T(8,128)S(1)} %get-tuple-element.27, f32[16,2,20,1024]{3,2,0,1:T(8,128)S(1)} %get-tuple-element.26, f32[16,2,20,1023]{3,2,0,1:T(8,128)S(1)} %bitcast.355), kind=kLoop, calls=%fused_computation.16 | loop fusion | flops 2621440 | bytes 15644160 | tf_op jit(solution)/shard_map/add | solution.py:139
  116.5 0.8 slice.451
  117.3 0.9 slice.433
  118.4 1.7 %fusion.1 = f32[16,2,19,1024]{3,2,1,0:T(8,128)S(1)} fusion(f32[16,2,20,32]{3,2,1,0:T(8,128)S(1)} %slice_add_fusion, f32[16,2,20,992]{3,2,1,0:T(8,128)S(1)} %slice.433), kind=kLoop, calls=%fused_computation.4 | loop fusion | flops 1867776 | bytes 5111808 | tf_op jit(solution)/shard_map/sub | solution.py:131
  120.2 1.9 %fusion.9 = (f32[16,2,16,1024]{3,2,1,0:T(8,128)S(1)}, f32[16,2,16,1024]{3,2,1,0:T(8,128)S(1)}) fusion(f32[16,2,20,992]{3,2,1,0:T(8,128)S(1)} %slice.433, f32[16,2,20,32]{3,2,1,0:T(8,128)S(1)} %slice_add_fusion, f32[16,1024]{1,0:T(8,128)S(1)} %copy-done.5, f32[16,2,16,992]{3,2,1,0:T(8,128)S(1)} %slice.451, f32[16,1024]{1,0:T(8,128)S(1)} %copy-done.6), kind=kLoop, calls=%fused_computation.24 | loop fusion | flops 5242880 | bytes 8978432 | tf_op jit(solution)/shard_map/mul | solution.py:78
  122.1 2.4 %fusion.12 = f32[16,2,16,1024]{3,2,1,0:T(8,128)S(1)} fusion(f32[16,2,19,1024]{3,2,1,0:T(8,128)S(1)} %fusion.1, f32[16,2,16,992]{3,2,1,0:T(8,128)S(1)} %bitcast.358, f32[16,2,16,1024]{3,2,1,0:T(8,128)S(1)} %get-tuple-element.24, f32[16,2,16,1024]{3,2,1,0:T(8,128)S(1)} %get-tuple-element.23, f32[16,2,16,1023]{3,2,1,0:T(8,128)S(1)} %bitcast.357, ...), kind=kLoop, calls=%fused_computation.29 | loop fusion | flops 6815744 | bytes 21690368 | tf_op jit(solution)/shard_map/add | solution.py:139
  125.2 1.9 %pad_maximum_fusion.1 = f32[16,2,16,1024]{3,2,1,0:T(8,128)} fusion(f32[16,2,16,992]{3,2,1,0:T(8,128)S(1)} %slice.456, f32[16,2,16,32]{3,2,1,0:T(8,128)S(1)} %slice_add_fusion.1), kind=kLoop, calls=%fused_computation.35 | loop fusion | flops 524288 | bytes 4194304 | tf_op jit(solution)/shard_map/concatenate | solution.py:142
  (73 shorter events, 5.4 us)
Async XLA Ops:
  0.0 1.1 copy-start
  66.3 13.7 %collective-permute-start.4 = (f32[2,4,64]{2,1,0:T(4,128)S(1)}, f32[2,4,64]{2,1,0:T(4,128)S(1)}, u32[]{:S(2)}, u32[]{:S(2)}) collective-permute-start(f32[2,4,64]{2,1,0:T(4,128)S(1)} %get-tuple-element.43), channel_id=1, source_target_pairs={{0,16},{16,32},{32,48},{48,64},{64,80},{80,96},{96,112},{112,128},... | collective-permute-start | bytes 6152 | tf_op jit(solution)/shard_map/ppermute | solution.py:27
  66.7 17.0 %collective-permute-start.5 = (f32[2,4,64]{2,1,0:T(4,128)S(1)}, f32[2,4,64]{2,1,0:T(4,128)S(1)}, u32[]{:S(2)}, u32[]{:S(2)}) collective-permute-start(f32[2,4,64]{2,1,0:T(4,128)S(1)} %get-tuple-element.44), channel_id=1, source_target_pairs={{16,0},{32,16},{48,32},{64,48},{80,64},{96,80},{112,96},{128,112},... | collective-permute-start | bytes 6152 | tf_op jit(solution)/shard_map/ppermute | solution.py:29
  74.5 9.4 %collective-permute-start.2 = (f32[4,3168]{1,0:T(4,128)S(1)}, f32[4,3168]{1,0:T(4,128)S(1)}, u32[]{:S(2)}, u32[]{:S(2)}) collective-permute-start(f32[4,3168]{1,0:T(4,128)S(1)} %get-tuple-element.37), channel_id=1, source_target_pairs={{0,16},{16,32},{32,48},{48,64},{64,80},{80,96},{96,112},{112,128},... | collective-permute-start | bytes 152072 | tf_op jit(solution)/shard_map/ppermute | solution.py:27
  74.6 9.3 %collective-permute-start.3 = (f32[4,3168]{1,0:T(4,128)S(1)}, f32[4,3168]{1,0:T(4,128)S(1)}, u32[]{:S(2)}, u32[]{:S(2)}) collective-permute-start(f32[4,3168]{1,0:T(4,128)S(1)} %get-tuple-element.38), channel_id=1, source_target_pairs={{16,0},{32,16},{48,32},{64,48},{80,64},{96,80},{112,96},{128,112},... | collective-permute-start | bytes 152072 | tf_op jit(solution)/shard_map/ppermute | solution.py:29
  79.9 22.6 %collective-permute-start = (f32[16,2,4,1024]{3,2,0,1:T(4,128)S(1)}, f32[16,2,4,1024]{3,2,0,1:T(4,128)S(1)}, u32[]{:S(2)}, u32[]{:S(2)}) collective-permute-start(f32[16,2,4,1024]{3,2,0,1:T(4,128)S(1)} %get-tuple-element.28), channel_id=1, source_target_pairs={{0,16},{16,32},{32,48},{48,64},{64,80},{80,96},{96,112},{112,128},... | collective-permute-start | bytes 1572872 | tf_op jit(solution)/shard_map/ppermute | solution.py:27
  80.1 24.6 %collective-permute-start.1 = (f32[16,2,4,1024]{3,2,0,1:T(4,128)S(1)}, f32[16,2,4,1024]{3,2,0,1:T(4,128)S(1)}, u32[]{:S(2)}, u32[]{:S(2)}) collective-permute-start(f32[16,2,4,1024]{3,2,0,1:T(4,128)S(1)} %get-tuple-element.29), channel_id=1, source_target_pairs={{16,0},{32,16},{48,32},{64,48},{80,64},{96,80},{112,96},{128,112},... | collective-permute-start | bytes 1572872 | tf_op jit(solution)/shard_map/ppermute | solution.py:29
  84.0 20.7 %copy-start.1 = (f32[16,2,16,1024]{3,2,1,0:T(8,128)S(1)}, f32[16,2,16,1024]{3,2,1,0:T(8,128)}, u32[]{:S(2)}) copy-start(f32[16,2,16,1024]{3,2,1,0:T(8,128)} %param.9) | copy-start | bytes 6291460
  106.9 2.9 %copy-start.2 = (f32[20,1024]{1,0:T(8,128)S(1)}, f32[20,1024]{1,0:T(8,128)}, u32[]{:S(2)}) copy-start(f32[20,1024]{1,0:T(8,128)} %get-tuple-element.52) | copy-start | bytes 245764
  106.9 2.9 %copy-start.3 = (f32[20,1024]{1,0:T(8,128)S(1)}, f32[20,1024]{1,0:T(8,128)}, u32[]{:S(2)}) copy-start(f32[20,1024]{1,0:T(8,128)} %get-tuple-element.45) | copy-start | bytes 245764
  106.9 2.9 %copy-start.4 = (f32[20,1024]{1,0:T(8,128)S(1)}, f32[20,1024]{1,0:T(8,128)}, u32[]{:S(2)}) copy-start(f32[20,1024]{1,0:T(8,128)} %get-tuple-element.46) | copy-start | bytes 245764
  118.3 1.8 %copy-start.5 = (f32[16,1024]{1,0:T(8,128)S(1)}, f32[16,1024]{1,0:T(8,128)}, u32[]{:S(2)}) copy-start(f32[16,1024]{1,0:T(8,128)} %slice.448) | copy-start | bytes 196612
  118.4 1.8 %copy-start.6 = (f32[16,1024]{1,0:T(8,128)S(1)}, f32[16,1024]{1,0:T(8,128)}, u32[]{:S(2)}) copy-start(f32[16,1024]{1,0:T(8,128)} %slice.450) | copy-start | bytes 196612
  120.1 1.9 %copy-start.7 = (f32[16,1024]{1,0:T(8,128)S(1)}, f32[16,1024]{1,0:T(8,128)}, u32[]{:S(2)}) copy-start(f32[16,1024]{1,0:T(8,128)} %get-tuple-element.55) | copy-start | bytes 196612
  120.1 1.9 %copy-start.8 = (f32[16,1024]{1,0:T(8,128)S(1)}, f32[16,1024]{1,0:T(8,128)}, u32[]{:S(2)}) copy-start(f32[16,1024]{1,0:T(8,128)} %get-tuple-element.56) | copy-start | bytes 196612
  120.2 1.9 %copy-start.9 = (f32[16,1024]{1,0:T(8,128)S(1)}, f32[16,1024]{1,0:T(8,128)}, u32[]{:S(2)}) copy-start(f32[16,1024]{1,0:T(8,128)} %get-tuple-element.47) | copy-start | bytes 196612
  120.2 1.9 %copy-start.10 = (f32[16,1024]{1,0:T(8,128)S(1)}, f32[16,1024]{1,0:T(8,128)}, u32[]{:S(2)}) copy-start(f32[16,1024]{1,0:T(8,128)} %get-tuple-element.48) | copy-start | bytes 196612

commit v2 on v1

--- a/solution.py
+++ b/solution.py
@@ -34,8 +34,19 @@
 
 
 def spread(value, axis, source):
-    kept = jnp.where(lax.axis_index(axis) == source, value, 0).astype(value.dtype)
-    return lax.psum(kept, axis)
+    count = lax.axis_size(axis)
+    rank = (lax.axis_index(axis) - source) % count
+    reach = 1
+    while reach < count:
+        fan = min(4, -(-count // reach))
+        received = value
+        for k in range(1, fan):
+            shift = k * reach
+            moved = lax.ppermute(value, axis, [(i, (i + shift) % count) for i in range(count)])
+            received = jnp.where((rank >= shift) & (rank < shift + reach), moved, received)
+        value = received
+        reach *= fan
+    return value
 
 
 def chemistry(carbon, alkalinity, piston, surface_sea):
@@ -148,8 +159,14 @@
     groups = adjoint_in.shape[0]
     cell_count = adjoint_in.shape[3]
     rim_depth = 4
+    owners = lax.axis_size("obj")
+    owner_index = interval[0] % owners
+    band = 2 * ROWS
+    stored = lax.dynamic_index_in_dim(checkpoint_store, interval[0] // owners, 0, keepdims=False)
     statics = jnp.concatenate(
         [
+            stored[0, :, :band],
+            stored[1, :, :band],
             sea_mask.astype(jnp.float32),
             zonal_speed,
             mixing,
@@ -160,6 +177,10 @@
         axis=1,
     )
     widened = padded(statics, (("tile", 0),), rim_depth)
+    initial_wide = spread(
+        jnp.stack([widened[:, :band], widened[:, band : 2 * band]]), "obj", owner_index
+    )
+    widened = widened[:, 2 * band :]
     sea_wide = widened[:, :cell_count]
     speed_wide = widened[:, cell_count : 2 * cell_count]
     mixing_wide = widened[:, 2 * cell_count : 3 * cell_count]
@@ -177,12 +198,6 @@
     objective_seeds = area_wide[None] * (region_wide[None] == targets[:, None, None]).astype(
         jnp.float32
     )
-    owners = lax.axis_size("obj")
-    owner_index = interval[0] % owners
-    band = 2 * ROWS
-    stored = lax.dynamic_index_in_dim(checkpoint_store, interval[0] // owners, 0, keepdims=False)
-    stored = spread(stored[:, :, :band], "obj", owner_index)
-    initial_wide = padded(stored, (("tile", 1),), rim_depth)
     inner_rim = 2
     piston_inner = trim_rim(piston_wide, inner_rim, rim_depth, 0)
     sea_inner = trim_rim(surface_sea, inner_rim, rim_depth, 0)

time: 127 us -> 76.1 us (0.60)
  the two profiles are of different devices: /device:TPU:1 before, /device:TPU:24 now
where the time goes in v2:
time: 76.1 us; the launch traced here: 75.9 us
  starting transfers between devices  25.9 us (34%)
  other arithmetic  18.4 us (24%)
  waiting for transfers between devices  16.9 us (22%)
  local copies, waits for them, and re-layouts  13.5 us (18%)
  between operations  1.25 us (2%)
    ppermute x6, waiting for transfers between devices, spread(): lax.ppermute(value, axis, [(i, (i + shift) % count) for i in range(count)])  16.9 us
    ppermute x6, starting transfers between devices, spread(): lax.ppermute(value, axis, [(i, (i + shift) % count) for i in range(count)])  14.7 us
    ppermute x2, starting transfers between devices, padded(): lax.ppermute(head, axis, [((i + 1) % count, i) for i in range(count)])  9.5 us
    add x3, other arithmetic, retreat(): interior + zonal_term + column_mix(interior, row_weight, level_weight)  8.98 us
    slice x7, local copies, waits for them, and re-layouts, forward_shift(): return jnp.concatenate([source[..., offset:], padding], axis=-1)  5.15 us
    sub x2, other arithmetic, retreat(): difference = extended[:, :, 1:] - extended[:, :, :-1]  2.24 us
    concatenate x1, other arithmetic, retreat(): return jnp.concatenate([surface, adjoint[..., ROWS:]], axis=-1)  1.93 us
    mul x2, other arithmetic, column_mix(): row_flux = row_weight * (forward_shift(source, 1) - source)  1.9 us
  transfers between devices with their start and end apart: 10, of which 4 were waited for; matrix products, arithmetic and copies ran while one was open for 10% of the time, Pallas kernels for 0%

profile of v2, /device:TPU:24, one launch (start us, length us, event | category | flops | bytes accessed | tf_op | source)
XLA Modules:
  0.0 75.9 jit_solution(15758259054470484026)
XLA Ops:
  0.7 0.7 convert_element_type.23
  1.4 0.8 %convert_element_type.22 = f32[16,1024]{1,0:T(8,128)S(1)} convert(s32[16,1024]{1,0:T(8,128)} %param.12) | non-fusion elementwise | flops 16384 | bytes 131072 | tf_op jit(solution)/shard_map/convert_element_type | solution.py:170
  2.3 1.0 %concatenate.64 = f32[16,3296]{1,0:T(8,128)S(1)} concatenate(f32[16,64]{1,0:T(8,128)S(1)} %get-tuple-element.42, f32[16,64]{1,0:T(8,128)S(1)} %get-tuple-element.41, f32[16,1024]{1,0:T(8,128)S(1)} %convert_element_type.22, f32[16,1024]{1,0:T(8,128)} %param.13, f32[16,1024]{1,0:T(8,128)} %param.14, f32[16,32]{1,0:T(8,128)} %param.15, f32[16,32]{1,0:T(8,128)} %param.16, ...), dimensions={1} | concatenate | bytes 421888 | tf_op jit(solution)/shard_map/concatenate | solution.py:166
  3.3 1.6 %collective-permute-start.2 = (f32[4,3296]{1,0:T(4,128)S(1)}, f32[4,3296]{1,0:T(4,128)S(1)}, u32[]{:S(2)}, u32[]{:S(2)}) collective-permute-start(f32[4,3296]{1,0:T(4,128)S(1)} %get-tuple-element.39), channel_id=1, source_target_pairs={{0,16},{16,32},{32,48},{48,64},{64,80},{80,96},{96,112},{112,128},... | collective-permute-start | bytes 158216 | tf_op jit(solution)/shard_map/ppermute | solution.py:27
  4.9 5.4 %collective-permute-start.3 = (f32[4,3296]{1,0:T(4,128)S(1)}, f32[4,3296]{1,0:T(4,128)S(1)}, u32[]{:S(2)}, u32[]{:S(2)}) collective-permute-start(f32[4,3296]{1,0:T(4,128)S(1)} %get-tuple-element.40), channel_id=1, source_target_pairs={{16,0},{32,16},{48,32},{64,48},{80,64},{96,80},{112,96},{128,112},... | collective-permute-start | bytes 158216 | tf_op jit(solution)/shard_map/ppermute | solution.py:29
  10.3 1.8 %fusion.65 = (f32[16,2,4,1024]{3,2,0,1:T(4,128)S(1)}, f32[16,2,4,1024]{3,2,0,1:T(4,128)S(1)}) fusion(f32[16,2,16,1024]{3,2,1,0:T(8,128)} %param.9), kind=kLoop, calls=%fused_computation.237 | loop fusion | bytes 2097152 | tf_op jit(solution)/shard_map/slice | solution.py:24
  12.1 4.1 %collective-permute-start.1 = (f32[16,2,4,1024]{3,2,0,1:T(4,128)S(1)}, f32[16,2,4,1024]{3,2,0,1:T(4,128)S(1)}, u32[]{:S(2)}, u32[]{:S(2)}) collective-permute-start(f32[16,2,4,1024]{3,2,0,1:T(4,128)S(1)} %get-tuple-element.29), channel_id=1, source_target_pairs={{16,0},{32,16},{48,32},{64,48},{80,64},{96,80},{112,96},{128,112},... | collective-permute-start | bytes 1572872 | tf_op jit(solution)/shard_map/ppermute | solution.py:29
  16.5 2.5 %collective-permute-start.5 = (f32[2,24,64]{2,1,0:T(8,128)S(1)}, f32[2,24,64]{2,1,0:T(8,128)S(1)}, u32[]{:S(2)}, u32[]{:S(2)}) collective-permute-start(f32[2,24,64]{2,1,0:T(8,128)S(1)} %pad_maximum_fusion.3), channel_id=1, source_target_pairs={{0,2},{1,3},{2,4},{3,5},{4,6},{5,7},{6,8},{7,9},{8,10},{9,11},{10,... | collective-permute-start | bytes 36872 | tf_op jit(solution)/shard_map/ppermute | solution.py:45
  19.0 2.5 %collective-permute-start.4 = (f32[2,24,64]{2,1,0:T(8,128)S(1)}, f32[2,24,64]{2,1,0:T(8,128)S(1)}, u32[]{:S(2)}, u32[]{:S(2)}) collective-permute-start(f32[2,24,64]{2,1,0:T(8,128)S(1)} %pad_maximum_fusion.3), channel_id=1, source_target_pairs={{0,3},{1,4},{2,5},{3,6},{4,7},{5,8},{6,9},{7,10},{8,11},{9,12},{10... | collective-permute-start | bytes 36872 | tf_op jit(solution)/shard_map/ppermute | solution.py:45
  24.7 9.9 %collective-permute-done.5 = f32[2,24,64]{2,1,0:T(8,128)S(1)} collective-permute-done((f32[2,24,64]{2,1,0:T(8,128)S(1)}, f32[2,24,64]{2,1,0:T(8,128)S(1)}, u32[]{:S(2)}, u32[]{:S(2)}) %collective-permute-start.5) | collective-permute-done | bytes 12320 | tf_op jit(solution)/shard_map/ppermute | solution.py:45
  35.2 6.6 %collective-permute-start.9 = (f32[2,24,64]{2,1,0:T(8,128)S(1)}, f32[2,24,64]{2,1,0:T(8,128)S(1)}, u32[]{:S(2)}, u32[]{:S(2)}) collective-permute-start(f32[2,24,64]{2,1,0:T(8,128)S(1)} %select_select_fusion.1), channel_id=1, source_target_pairs={{0,4},{1,5},{2,6},{3,7},{4,8},{5,9},{6,10},{7,11},{8,12},{9,13},{1... | collective-permute-start | bytes 36872 | tf_op jit(solution)/shard_map/ppermute | solution.py:45
  41.8 3.0 %collective-permute-start.8 = (f32[2,24,64]{2,1,0:T(8,128)S(1)}, f32[2,24,64]{2,1,0:T(8,128)S(1)}, u32[]{:S(2)}, u32[]{:S(2)}) collective-permute-start(f32[2,24,64]{2,1,0:T(8,128)S(1)} %select_select_fusion.1), channel_id=1, source_target_pairs={{0,8},{1,9},{2,10},{3,11},{4,12},{5,13},{6,14},{7,15},{8,0},{9,1},... | collective-permute-start | bytes 36872 | tf_op jit(solution)/shard_map/ppermute | solution.py:45
  46.2 1.0 %collective-permute-done.8 = f32[2,24,64]{2,1,0:T(8,128)S(1)} collective-permute-done((f32[2,24,64]{2,1,0:T(8,128)S(1)}, f32[2,24,64]{2,1,0:T(8,128)S(1)}, u32[]{:S(2)}, u32[]{:S(2)}) %collective-permute-start.8) | collective-permute-done | bytes 12320 | tf_op jit(solution)/shard_map/ppermute | solution.py:45
  47.2 5.4 %collective-permute-done.7 = f32[2,24,64]{2,1,0:T(8,128)S(1)} collective-permute-done((f32[2,24,64]{2,1,0:T(8,128)S(1)}, f32[2,24,64]{2,1,0:T(8,128)S(1)}, u32[]{:S(2)}, u32[]{:S(2)}) %collective-permute-start.7) | collective-permute-done | bytes 12320 | tf_op jit(solution)/shard_map/ppermute | solution.py:45
  54.1 1.2 %slice.411 = f32[16,2,20,1023]{3,2,0,1:T(8,128)S(1)} slice(f32[16,2,24,1024]{3,2,0,1:T(8,128)S(1)} %pad_maximum_fusion), slice={[0:16], [0:2], [2:22], [1:1024]} | slice | bytes 5237760 | tf_op jit(solution)/shard_map/slice | solution.py:71
  55.8 2.9 %slice.416 = f32[16,2,20,992]{3,2,0,1:T(8,128)} slice(f32[16,2,24,1024]{3,2,0,1:T(8,128)S(1)} %pad_maximum_fusion), slice={[0:16], [0:2], [2:22], [32:1024]} | slice | bytes 5079040 | tf_op jit(solution)/shard_map/slice | solution.py:71
  58.7 4.1 %fusion.4 = (f32[16,2,20,1024]{3,2,0,1:T(8,128)S(1)}, f32[16,2,20,1024]{3,2,0,1:T(8,128)S(1)}, f32[16,2,20,1024]{3,2,0,1:T(8,128)S(1)}) fusion(f32[16,2,23,1024]{3,2,0,1:T(8,128)S(1)} %slice_subtract_fusion, f32[16,2,24,1024]{3,2,0,1:T(8,128)S(1)} %pad_maximum_fusion, f32[20,1024]{1,0:T(8,128)S(1)} %copy-done.3, f32[20,1024]{1,0:T(8,128)S(1)} %copy-done.4, ...), kind=kLoop, calls=%fused_computation.8 | loop fusion | flops 7864320 | bytes 26621440 | tf_op jit(solution)/shard_map/add | solution.py:150
  62.8 2.4 %copy_add_fusion = f32[16,2,20,1024]{3,2,1,0:T(8,128)S(1)} fusion(f32[16,2,20,1024]{3,2,0,1:T(8,128)S(1)} %get-tuple-element.25, f32[16,2,20,992]{3,2,0,1:T(8,128)S(1)} %bitcast.364, f32[16,2,20,1024]{3,2,0,1:T(8,128)S(1)} %get-tuple-element.27, f32[16,2,20,1024]{3,2,0,1:T(8,128)S(1)} %get-tuple-element.26, f32[16,2,20,1023]{3,2,0,1:T(8,128)S(1)} %bitcast.363), kind=kLoop, calls=%fused_computation.16 | loop fusion | flops 2621440 | bytes 15644160 | tf_op jit(solution)/shard_map/add | solution.py:150
  65.3 0.8 %slice.461 = f32[16,2,16,992]{3,2,1,0:T(8,128)S(1)} slice(f32[16,2,20,1024]{3,2,1,0:T(8,128)S(1)} %copy_add_fusion), slice={[0:16], [0:2], [2:18], [32:1024]} | slice | bytes 4063232 | tf_op jit(solution)/shard_map/slice | solution.py:71
  66.0 0.9 %slice.443 = f32[16,2,20,992]{3,2,1,0:T(8,128)S(1)} slice(f32[16,2,20,1024]{3,2,1,0:T(8,128)S(1)} %copy_add_fusion), slice={[0:16], [0:2], [0:20], [32:1024]} | slice | bytes 5079040 | tf_op jit(solution)/shard_map/slice | solution.py:153
  67.1 1.7 %fusion.1 = f32[16,2,19,1024]{3,2,1,0:T(8,128)S(1)} fusion(f32[16,2,20,32]{3,2,1,0:T(8,128)S(1)} %slice_add_fusion, f32[16,2,20,992]{3,2,1,0:T(8,128)S(1)} %slice.443), kind=kLoop, calls=%fused_computation.4 | loop fusion | flops 1867776 | bytes 5111808 | tf_op jit(solution)/shard_map/sub | solution.py:142
  68.9 1.9 %fusion.9 = (f32[16,2,16,1024]{3,2,1,0:T(8,128)S(1)}, f32[16,2,16,1024]{3,2,1,0:T(8,128)S(1)}) fusion(f32[16,2,20,992]{3,2,1,0:T(8,128)S(1)} %slice.443, f32[16,2,20,32]{3,2,1,0:T(8,128)S(1)} %slice_add_fusion, f32[16,1024]{1,0:T(8,128)S(1)} %copy-done.5, f32[16,2,16,992]{3,2,1,0:T(8,128)S(1)} %slice.461, f32[16,1024]{1,0:T(8,128)S(1)} %copy-done.6), kind=kLoop, calls=%fused_computation.24 | loop fusion | flops 5242880 | bytes 8978432 | tf_op jit(solution)/shard_map/mul | solution.py:89
  70.8 2.4 %fusion.12 = f32[16,2,16,1024]{3,2,1,0:T(8,128)S(1)} fusion(f32[16,2,19,1024]{3,2,1,0:T(8,128)S(1)} %fusion.1, f32[16,2,16,992]{3,2,1,0:T(8,128)S(1)} %bitcast.366, f32[16,2,16,1024]{3,2,1,0:T(8,128)S(1)} %get-tuple-element.24, f32[16,2,16,1024]{3,2,1,0:T(8,128)S(1)} %get-tuple-element.23, f32[16,2,16,1023]{3,2,1,0:T(8,128)S(1)} %bitcast.365, ...), kind=kLoop, calls=%fused_computation.29 | loop fusion | flops 6815744 | bytes 21690368 | tf_op jit(solution)/shard_map/add | solution.py:150
  73.9 1.9 %pad_maximum_fusion.1 = f32[16,2,16,1024]{3,2,1,0:T(8,128)} fusion(f32[16,2,16,992]{3,2,1,0:T(8,128)S(1)} %slice.466, f32[16,2,16,32]{3,2,1,0:T(8,128)S(1)} %slice_add_fusion.1), kind=kLoop, calls=%fused_computation.35 | loop fusion | flops 524288 | bytes 4194304 | tf_op jit(solution)/shard_map/concatenate | solution.py:153
  (82 shorter events, 8.1 us)
Async XLA Ops:
  0.0 2.3 %copy-start = (f32[4,2,16,1024]{3,2,1,0:T(8,128)S(1)}, f32[4,2,16,1024]{3,2,1,0:T(8,128)}, u32[]{:S(2)}) copy-start(f32[4,2,16,1024]{3,2,1,0:T(8,128)} %param.10) | copy-start | bytes 1572868
  3.3 13.0 %collective-permute-start.2 = (f32[4,3296]{1,0:T(4,128)S(1)}, f32[4,3296]{1,0:T(4,128)S(1)}, u32[]{:S(2)}, u32[]{:S(2)}) collective-permute-start(f32[4,3296]{1,0:T(4,128)S(1)} %get-tuple-element.39), channel_id=1, source_target_pairs={{0,16},{16,32},{32,48},{48,64},{64,80},{80,96},{96,112},{112,128},... | collective-permute-start | bytes 158216 | tf_op jit(solution)/shard_map/ppermute | solution.py:27
  4.9 11.5 %collective-permute-start.3 = (f32[4,3296]{1,0:T(4,128)S(1)}, f32[4,3296]{1,0:T(4,128)S(1)}, u32[]{:S(2)}, u32[]{:S(2)}) collective-permute-start(f32[4,3296]{1,0:T(4,128)S(1)} %get-tuple-element.40), channel_id=1, source_target_pairs={{16,0},{32,16},{48,32},{64,48},{80,64},{96,80},{112,96},{128,112},... | collective-permute-start | bytes 158216 | tf_op jit(solution)/shard_map/ppermute | solution.py:29
  12.0 41.5 %collective-permute-start = (f32[16,2,4,1024]{3,2,0,1:T(4,128)S(1)}, f32[16,2,4,1024]{3,2,0,1:T(4,128)S(1)}, u32[]{:S(2)}, u32[]{:S(2)}) collective-permute-start(f32[16,2,4,1024]{3,2,0,1:T(4,128)S(1)} %get-tuple-element.28), channel_id=1, source_target_pairs={{0,16},{16,32},{32,48},{48,64},{64,80},{80,96},{96,112},{112,128},... | collective-permute-start | bytes 1572872 | tf_op jit(solution)/shard_map/ppermute | solution.py:27
  12.1 41.4 %collective-permute-start.1 = (f32[16,2,4,1024]{3,2,0,1:T(4,128)S(1)}, f32[16,2,4,1024]{3,2,0,1:T(4,128)S(1)}, u32[]{:S(2)}, u32[]{:S(2)}) collective-permute-start(f32[16,2,4,1024]{3,2,0,1:T(4,128)S(1)} %get-tuple-element.29), channel_id=1, source_target_pairs={{16,0},{32,16},{48,32},{64,48},{80,64},{96,80},{112,96},{128,112},... | collective-permute-start | bytes 1572872 | tf_op jit(solution)/shard_map/ppermute | solution.py:29
  16.4 8.3 %collective-permute-start.6 = (f32[2,24,64]{2,1,0:T(8,128)S(1)}, f32[2,24,64]{2,1,0:T(8,128)S(1)}, u32[]{:S(2)}, u32[]{:S(2)}) collective-permute-start(f32[2,24,64]{2,1,0:T(8,128)S(1)} %pad_maximum_fusion.3), channel_id=1, source_target_pairs={{0,1},{1,2},{2,3},{3,4},{4,5},{5,6},{6,7},{7,8},{8,9},{9,10},{10,1... | collective-permute-start | bytes 36872 | tf_op jit(solution)/shard_map/ppermute | solution.py:45
  16.5 18.1 %collective-permute-start.5 = (f32[2,24,64]{2,1,0:T(8,128)S(1)}, f32[2,24,64]{2,1,0:T(8,128)S(1)}, u32[]{:S(2)}, u32[]{:S(2)}) collective-permute-start(f32[2,24,64]{2,1,0:T(8,128)S(1)} %pad_maximum_fusion.3), channel_id=1, source_target_pairs={{0,2},{1,3},{2,4},{3,5},{4,6},{5,7},{6,8},{7,9},{8,10},{9,11},{10,... | collective-permute-start | bytes 36872 | tf_op jit(solution)/shard_map/ppermute | solution.py:45
  19.0 16.2 %collective-permute-start.4 = (f32[2,24,64]{2,1,0:T(8,128)S(1)}, f32[2,24,64]{2,1,0:T(8,128)S(1)}, u32[]{:S(2)}, u32[]{:S(2)}) collective-permute-start(f32[2,24,64]{2,1,0:T(8,128)S(1)} %pad_maximum_fusion.3), channel_id=1, source_target_pairs={{0,3},{1,4},{2,5},{3,6},{4,7},{5,8},{6,9},{7,10},{8,11},{9,12},{10... | collective-permute-start | bytes 36872 | tf_op jit(solution)/shard_map/ppermute | solution.py:45
  21.7 31.8 %copy-start.1 = (f32[16,2,16,1024]{3,2,1,0:T(8,128)S(1)}, f32[16,2,16,1024]{3,2,1,0:T(8,128)}, u32[]{:S(2)}) copy-start(f32[16,2,16,1024]{3,2,1,0:T(8,128)} %param.9) | copy-start | bytes 6291460
  35.2 11.0 %collective-permute-start.9 = (f32[2,24,64]{2,1,0:T(8,128)S(1)}, f32[2,24,64]{2,1,0:T(8,128)S(1)}, u32[]{:S(2)}, u32[]{:S(2)}) collective-permute-start(f32[2,24,64]{2,1,0:T(8,128)S(1)} %select_select_fusion.1), channel_id=1, source_target_pairs={{0,4},{1,5},{2,6},{3,7},{4,8},{5,9},{6,10},{7,11},{8,12},{9,13},{1... | collective-permute-start | bytes 36872 | tf_op jit(solution)/shard_map/ppermute | solution.py:45
  41.8 5.3 %collective-permute-start.8 = (f32[2,24,64]{2,1,0:T(8,128)S(1)}, f32[2,24,64]{2,1,0:T(8,128)S(1)}, u32[]{:S(2)}, u32[]{:S(2)}) collective-permute-start(f32[2,24,64]{2,1,0:T(8,128)S(1)} %select_select_fusion.1), channel_id=1, source_target_pairs={{0,8},{1,9},{2,10},{3,11},{4,12},{5,13},{6,14},{7,15},{8,0},{9,1},... | collective-permute-start | bytes 36872 | tf_op jit(solution)/shard_map/ppermute | solution.py:45
  44.8 7.7 %collective-permute-start.7 = (f32[2,24,64]{2,1,0:T(8,128)S(1)}, f32[2,24,64]{2,1,0:T(8,128)S(1)}, u32[]{:S(2)}, u32[]{:S(2)}) collective-permute-start(f32[2,24,64]{2,1,0:T(8,128)S(1)} %select_select_fusion.1), channel_id=1, source_target_pairs={{0,12},{1,13},{2,14},{3,15},{4,0},{5,1},{6,2},{7,3},{8,4},{9,5},{1... | collective-permute-start | bytes 36872 | tf_op jit(solution)/shard_map/ppermute | solution.py:45
  55.8 2.9 %copy-start.2 = (f32[20,1024]{1,0:T(8,128)S(1)}, f32[20,1024]{1,0:T(8,128)}, u32[]{:S(2)}) copy-start(f32[20,1024]{1,0:T(8,128)} %get-tuple-element.54) | copy-start | bytes 245764
  55.8 2.9 %copy-start.3 = (f32[20,1024]{1,0:T(8,128)S(1)}, f32[20,1024]{1,0:T(8,128)}, u32[]{:S(2)}) copy-start(f32[20,1024]{1,0:T(8,128)} %get-tuple-element.47) | copy-start | bytes 245764
  55.8 2.9 %copy-start.4 = (f32[20,1024]{1,0:T(8,128)S(1)}, f32[20,1024]{1,0:T(8,128)}, u32[]{:S(2)}) copy-start(f32[20,1024]{1,0:T(8,128)} %get-tuple-element.48) | copy-start | bytes 245764
  67.1 1.8 %copy-start.5 = (f32[16,1024]{1,0:T(8,128)S(1)}, f32[16,1024]{1,0:T(8,128)}, u32[]{:S(2)}) copy-start(f32[16,1024]{1,0:T(8,128)} %slice.458) | copy-start | bytes 196612
  67.1 1.8 %copy-start.6 = (f32[16,1024]{1,0:T(8,128)S(1)}, f32[16,1024]{1,0:T(8,128)}, u32[]{:S(2)}) copy-start(f32[16,1024]{1,0:T(8,128)} %slice.460) | copy-start | bytes 196612
  68.9 1.9 %copy-start.7 = (f32[16,1024]{1,0:T(8,128)S(1)}, f32[16,1024]{1,0:T(8,128)}, u32[]{:S(2)}) copy-start(f32[16,1024]{1,0:T(8,128)} %get-tuple-element.57) | copy-start | bytes 196612
  68.9 1.9 %copy-start.8 = (f32[16,1024]{1,0:T(8,128)S(1)}, f32[16,1024]{1,0:T(8,128)}, u32[]{:S(2)}) copy-start(f32[16,1024]{1,0:T(8,128)} %get-tuple-element.58) | copy-start | bytes 196612
  68.9 1.9 %copy-start.9 = (f32[16,1024]{1,0:T(8,128)S(1)}, f32[16,1024]{1,0:T(8,128)}, u32[]{:S(2)}) copy-start(f32[16,1024]{1,0:T(8,128)} %get-tuple-element.49) | copy-start | bytes 196612
  68.9 1.9 %copy-start.10 = (f32[16,1024]{1,0:T(8,128)S(1)}, f32[16,1024]{1,0:T(8,128)}, u32[]{:S(2)}) copy-start(f32[16,1024]{1,0:T(8,128)} %get-tuple-element.50) | copy-start | bytes 196612

commit v3 on v2

--- a/solution.py
+++ b/solution.py
@@ -2,6 +2,8 @@
 import jax.numpy as jnp
 from jax import lax
 from jax.sharding import PartitionSpec as P
+from jax.experimental import pallas as pl
+from jax.experimental.pallas import tpu as pltpu
 
 ROWS = 32
 LEVELS = 32
@@ -151,6 +153,94 @@
     forcing = interior[:, 0, :, :ROWS] + objective_seeds
     surface = adjoint[..., :ROWS] + slopes[None] * forcing[:, None]
     return jnp.concatenate([surface, adjoint[..., ROWS:]], axis=-1)
+
+
+SPAN = 48
+ORIGIN = 16
+
+
+def halves(cells, axis, dim, width):
+    count = lax.axis_size(axis)
+    head = lax.slice_in_dim(cells, 0, width, axis=dim)
+    tail = lax.slice_in_dim(cells, cells.shape[dim] - width, cells.shape[dim], axis=dim)
+    west = lax.ppermute(tail, axis, [(i, (i + 1) % count) for i in range(count)])
+    east = lax.ppermute(head, axis, [((i + 1) % count, i) for i in range(count)])
+    return west, east
+
+
+def placed_rows(source, first, total=SPAN):
+    pad = [(0, 0)] * source.ndim
+    pad[-2] = (first, total - first - source.shape[-2])
+    return jnp.pad(source, pad)
+
+
+def lanes_to(source, width):
+    pad = [(0, 0)] * source.ndim
+    pad[-1] = (0, width - source.shape[-1])
+    return jnp.pad(source, pad)
+
+
+def retreat_kernel(center_ref, west_ref, east_ref, w_ref, s_ref, seed_ref, out_ref, e_ref, f_ref):
+    local = center_ref.shape[2]
+    width = center_ref.shape[3]
+    rim = west_ref.shape[2]
+    e_ref[:, ORIGIN : ORIGIN + local, :] = center_ref[0]
+    e_ref[:, ORIGIN - rim : ORIGIN, :] = west_ref[0]
+    e_ref[:, ORIGIN + local : ORIGIN + local + rim, :] = east_ref[0]
+
+    def block(src, r, t, stage):
+        x_m2 = src[t, r - 2 : r + 6, :]
+        x_m1 = src[t, r - 1 : r + 7, :]
+        x_0 = src[t, r : r + 8, :]
+        x_p1 = src[t, r + 1 : r + 9, :]
+        x_p2 = src[t, r + 2 : r + 10, :]
+        zonal = (
+            w_ref[0, r : r + 8, :] * (x_p2 - x_p1)
+            + w_ref[1, r : r + 8, :] * (x_p1 - x_0)
+            + w_ref[2, r : r + 8, :] * (x_0 - x_m1)
+            + w_ref[3, r : r + 8, :] * (x_m1 - x_m2)
+        )
+        row_flux = w_ref[4, r : r + 8, :] * (pltpu.roll(x_0, width - 1, 1) - x_0)
+        level_flux = w_ref[5, r : r + 8, :] * (pltpu.roll(x_0, width - ROWS, 1) - x_0)
+        mix = row_flux - pltpu.roll(row_flux, 1, 1) + level_flux - pltpu.roll(level_flux, ROWS, 1)
+        adjoint = x_0 + zonal + mix
+        forcing = src[0, r : r + 8, 0:128] + seed_ref[0, r : r + 8, :]
+        head = adjoint[:, 0:128] + s_ref[stage, t, r : r + 8, :] * forcing
+        return head, adjoint[:, 128:]
+
+    for r in range(ORIGIN - 8, ORIGIN + local + 8, 8):
+        for t in range(2):
+            head, rest = block(e_ref, r, t, 0)
+            f_ref[t, r : r + 8, 0:128] = head
+            f_ref[t, r : r + 8, 128:] = rest
+    for r in range(ORIGIN, ORIGIN + local, 8):
+        for t in range(2):
+            head, rest = block(f_ref, r, t, 1)
+            out_ref[0, t, r - ORIGIN : r - ORIGIN + 8, 0:128] = head
+            out_ref[0, t, r - ORIGIN : r - ORIGIN + 8, 128:] = rest
+
+
+def two_retreats(center, west, east, stencil, slopes, seeds):
+    groups, tracers, local, width = center.shape
+    rim = west.shape[2]
+    return pl.pallas_call(
+        retreat_kernel,
+        out_shape=jax.ShapeDtypeStruct(center.shape, center.dtype),
+        grid=(groups,),
+        in_specs=[
+            pl.BlockSpec((1, tracers, local, width), lambda g: (g, 0, 0, 0)),
+            pl.BlockSpec((1, tracers, rim, width), lambda g: (g, 0, 0, 0)),
+            pl.BlockSpec((1, tracers, rim, width), lambda g: (g, 0, 0, 0)),
+            pl.BlockSpec(stencil.shape, lambda g: (0, 0, 0)),
+            pl.BlockSpec(slopes.shape, lambda g: (0, 0, 0, 0)),
+            pl.BlockSpec((1,) + seeds.shape[1:], lambda g: (g, 0, 0)),
+        ],
+        out_specs=pl.BlockSpec((1, tracers, local, width), lambda g: (g, 0, 0, 0)),
+        scratch_shapes=[
+            pltpu.VMEM((tracers, SPAN, width), jnp.float32),
+            pltpu.VMEM((tracers, SPAN, width), jnp.float32),
+        ],
+    )(center, west, east, stencil, slopes, seeds)
 
 
 def body(
@@ -215,23 +305,29 @@
     _, slopes_second = surface_slopes(
         following[0, :, :ROWS], following[1, :, :ROWS], piston_inner, sea_inner
     )
-    extended = padded(adjoint_in, (("tile", 2),), rim_depth)
-    middle = retreat(
-        extended,
-        weights,
-        trim_rim(row_weight, inner_rim, rim_depth, 0),
-        trim_rim(level_weight, inner_rim, rim_depth, 0),
-        slopes_second,
-        trim_rim(objective_seeds, inner_rim, rim_depth, 1),
-    )
-    return retreat(
-        middle,
-        trim_rim(weights, inner_rim, rim_depth, 1),
-        trim_rim(row_weight, 0, rim_depth, 0),
-        trim_rim(level_weight, 0, rim_depth, 0),
-        trim_rim(slopes_first, 0, inner_rim, 1),
-        trim_rim(objective_seeds, 0, rim_depth, 1),
-    )
+    west, east = halves(adjoint_in, "tile", 2, rim_depth)
+    first = ORIGIN - rim_depth
+    stencil = jnp.stack(
+        [
+            placed_rows(weights[0], first - 1),
+            placed_rows(weights[1], first),
+            placed_rows(weights[2], first + 1),
+            placed_rows(weights[3], first + 2),
+            placed_rows(row_weight, first),
+            placed_rows(level_weight, first),
+        ]
+    )
+    slopes = lanes_to(
+        jnp.stack(
+            [
+                placed_rows(slopes_second, ORIGIN - inner_rim),
+                placed_rows(trim_rim(slopes_first, 0, inner_rim, 1), ORIGIN),
+            ]
+        ),
+        128,
+    )
+    seeds = lanes_to(placed_rows(objective_seeds, first), 128)
+    return two_retreats(adjoint_in, west, east, stencil, slopes, seeds)
 
 
 def solution(mesh):

time: 76.1 us -> 73 us (0.959)
  the two profiles are of different devices: /device:TPU:24 before, /device:TPU:18 now
where the time goes in v3:
time: 73 us; the launch traced here: 72.6 us
  starting transfers between devices  36.9 us (51%)
  Pallas kernels  18.7 us (26%)
  waiting for transfers between devices  8.42 us (12%)
  local copies, waits for them, and re-layouts  4.15 us (6%)
  other arithmetic  3.34 us (5%)
  between operations  1.07 us (1%)
    ppermute x6, starting transfers between devices, spread(): lax.ppermute(value, axis, [(i, (i + shift) % count) for i in range(count)])  29.4 us
    pallas_call x1, Pallas kernels, two_retreats(): pl.pallas_call(retreat_kernel, out_shape=jax.ShapeDtypeStruct(center.shap...  18.7 us
    ppermute x6, waiting for transfers between devices, spread(): lax.ppermute(value, axis, [(i, (i + shift) % count) for i in range(count)])  8.41 us
    ppermute x1, starting transfers between devices, halves(): lax.ppermute(head, axis, [((i + 1) % count, i) for i in range(count)])  5.46 us
    ppermute x1, starting transfers between devices, padded(): lax.ppermute(tail, axis, [(i, (i + 1) % count) for i in range(count)])  1.97 us
    slice x1, local copies, waits for them, and re-layouts, halves(): head = lax.slice_in_dim(cells, 0, width, axis=dim)  1.78 us
  transfers between devices with their start and end apart: 10, of which 3 were waited for; matrix products, arithmetic and copies ran while one was open for 7% of the time, Pallas kernels for 0%

profile of v3, /device:TPU:18, one launch (start us, length us, event | category | flops | bytes accessed | tf_op | source)
XLA Modules:
  0.0 72.6 jit_solution(14877338743455402278)
XLA Ops:
  0.7 0.7 convert_element_type.43
  1.4 0.8 %convert_element_type.42 = f32[16,1024]{1,0:T(8,128)S(1)} convert(s32[16,1024]{1,0:T(8,128)} %param.12) | non-fusion elementwise | flops 16384 | bytes 131072 | tf_op jit(solution)/shard_map/convert_element_type | solution.py:260
  2.3 1.0 %concatenate.30 = f32[16,3296]{1,0:T(8,128)S(1)} concatenate(f32[16,64]{1,0:T(8,128)S(1)} %get-tuple-element.38, f32[16,64]{1,0:T(8,128)S(1)} %get-tuple-element.37, f32[16,1024]{1,0:T(8,128)S(1)} %convert_element_type.42, f32[16,1024]{1,0:T(8,128)} %param.13, f32[16,1024]{1,0:T(8,128)} %param.14, f32[16,32]{1,0:T(8,128)} %param.15, f32[16,32]{1,0:T(8,128)} %param.16, ...), dimensions={1} | concatenate | bytes 421888 | tf_op jit(solution)/shard_map/concatenate | solution.py:256
  3.3 2.0 %collective-permute-start.2 = (f32[4,3296]{1,0:T(4,128)S(1)}, f32[4,3296]{1,0:T(4,128)S(1)}, u32[]{:S(2)}, u32[]{:S(2)}) collective-permute-start(f32[4,3296]{1,0:T(4,128)S(1)} %get-tuple-element.35), channel_id=1, source_target_pairs={{0,16},{16,32},{32,48},{48,64},{64,80},{80,96},{96,112},{112,128},... | collective-permute-start | bytes 158216 | tf_op jit(solution)/shard_map/ppermute | solution.py:29
  5.3 0.1 collective-permute-start.3
  5.4 1.8 %fusion.52 = (f32[16,2,4,1024]{3,2,1,0:T(4,128)S(1)}, f32[16,2,4,1024]{3,2,1,0:T(4,128)S(1)}) fusion(f32[16,2,16,1024]{3,2,1,0:T(8,128)} %center_ref.1), kind=kLoop, calls=%fused_computation.200 | loop fusion | bytes 2097152 | tf_op jit(solution)/shard_map/slice | solution.py:164
  7.2 5.5 %collective-permute-start.1 = (f32[16,2,4,1024]{3,2,1,0:T(4,128)S(1)}, f32[16,2,4,1024]{3,2,1,0:T(4,128)}, u32[]{:S(2)}, u32[]{:S(2)}) collective-permute-start(f32[16,2,4,1024]{3,2,1,0:T(4,128)S(1)} %get-tuple-element.24), channel_id=1, source_target_pairs={{16,0},{32,16},{48,32},{64,48},{80,64},{96,80},{112,96},{128,112},... | collective-permute-start | bytes 1572872 | tf_op jit(solution)/shard_map/ppermute | solution.py:167
  12.8 0.1 maximum_bitcast_fusion.1
  12.9 1.4 %collective-permute-start.5 = (f32[2,24,64]{2,1,0:T(8,128)S(1)}, f32[2,24,64]{2,1,0:T(8,128)S(1)}, u32[]{:S(2)}, u32[]{:S(2)}) collective-permute-start(f32[2,24,64]{2,1,0:T(8,128)S(1)} %pad_maximum_fusion.1), channel_id=1, source_target_pairs={{0,2},{1,3},{2,4},{3,5},{4,6},{5,7},{6,8},{7,9},{8,10},{9,11},{10,... | collective-permute-start | bytes 36872 | tf_op jit(solution)/shard_map/ppermute | solution.py:47
  14.3 2.7 %collective-permute-start.4 = (f32[2,24,64]{2,1,0:T(8,128)S(1)}, f32[2,24,64]{2,1,0:T(8,128)S(1)}, u32[]{:S(2)}, u32[]{:S(2)}) collective-permute-start(f32[2,24,64]{2,1,0:T(8,128)S(1)} %pad_maximum_fusion.1), channel_id=1, source_target_pairs={{0,3},{1,4},{2,5},{3,6},{4,7},{5,8},{6,9},{7,10},{8,11},{9,12},{10... | collective-permute-start | bytes 36872 | tf_op jit(solution)/shard_map/ppermute | solution.py:47
  17.1 0.1 slice.212
  17.1 0.1 slice.210
  17.6 0.1 compare_select_fusion
  17.7 1.6 %collective-permute-done.4 = f32[2,24,64]{2,1,0:T(8,128)S(1)} collective-permute-done((f32[2,24,64]{2,1,0:T(8,128)S(1)}, f32[2,24,64]{2,1,0:T(8,128)S(1)}, u32[]{:S(2)}, u32[]{:S(2)}) %collective-permute-start.4) | collective-permute-done | bytes 12320 | tf_op jit(solution)/shard_map/ppermute | solution.py:47
  19.3 23.1 %collective-permute-start.9 = (f32[2,24,64]{2,1,0:T(8,128)S(1)}, f32[2,24,64]{2,1,0:T(8,128)S(1)}, u32[]{:S(2)}, u32[]{:S(2)}) collective-permute-start(f32[2,24,64]{2,1,0:T(8,128)S(1)} %select_select_fusion.1), channel_id=1, source_target_pairs={{0,4},{1,5},{2,6},{3,7},{4,8},{5,9},{6,10},{7,11},{8,12},{9,13},{1... | collective-permute-start | bytes 36872 | tf_op jit(solution)/shard_map/ppermute | solution.py:47
  42.4 2.1 %collective-permute-start.8 = (f32[2,24,64]{2,1,0:T(8,128)S(1)}, f32[2,24,64]{2,1,0:T(8,128)S(1)}, u32[]{:S(2)}, u32[]{:S(2)}) collective-permute-start(f32[2,24,64]{2,1,0:T(8,128)S(1)} %select_select_fusion.1), channel_id=1, source_target_pairs={{0,8},{1,9},{2,10},{3,11},{4,12},{5,13},{6,14},{7,15},{8,0},{9,1},... | collective-permute-start | bytes 36872 | tf_op jit(solution)/shard_map/ppermute | solution.py:47
  44.6 0.9 %pad.99.seed_ref = f32[16,48,128]{2,1,0:T(8,128)} pad(f32[16,24,32]{2,1,0:T(8,128)S(1)} %compare_select_fusion, f32[]{:T(128)} %constant.130.clone.1), padding=0_0x12_12x0_96 | pad | bytes 442372 | tf_op jit(solution)/shard_map/jit(_pad)/pad | solution.py:180
  45.5 2.3 %collective-permute-done.8 = f32[2,24,64]{2,1,0:T(8,128)S(1)} collective-permute-done((f32[2,24,64]{2,1,0:T(8,128)S(1)}, f32[2,24,64]{2,1,0:T(8,128)S(1)}, u32[]{:S(2)}, u32[]{:S(2)}) %collective-permute-start.8) | collective-permute-done | bytes 12320 | tf_op jit(solution)/shard_map/ppermute | solution.py:47
  47.7 4.5 %collective-permute-done.7 = f32[2,24,64]{2,1,0:T(8,128)S(1)} collective-permute-done((f32[2,24,64]{2,1,0:T(8,128)S(1)}, f32[2,24,64]{2,1,0:T(8,128)S(1)}, u32[]{:S(2)}, u32[]{:S(2)}) %collective-permute-start.7) | collective-permute-done | bytes 12320 | tf_op jit(solution)/shard_map/ppermute | solution.py:47
  52.5 0.1 fusion.12
  52.6 0.1 fusion.18
  52.8 0.3 add_bitcast_fusion.3
  53.3 0.7 select_maximum_fusion.s_ref
  53.9 18.7 %shard_map.91 = f32[16,2,16,1024]{3,2,1,0:T(8,128)} custom-call(f32[16,2,16,1024]{3,2,1,0:T(8,128)} %center_ref.1, f32[16,2,4,1024]{3,2,1,0:T(4,128)} %collective-permute-done.west_ref, f32[16,2,4,1024]{3,2,1,0:T(4,128)} %collective-permute-done.1.east_ref, f32[6,48,1024]{2,1,0:T(8,128)} %copy-done.1, f32[2,2,48,128]{3,2,1,0:T(8,128)} %select_maximum_fusion.s_ref, ...), custom_call_target="tpu_custom_call" | custom-call | tf_op jit(solution)/shard_map/pallas_call | solution.py:226
  (48 shorter events, 1.0 us)
Async XLA Ops:
  0.0 2.3 %copy-start = (f32[4,2,16,1024]{3,2,1,0:T(8,128)S(1)}, f32[4,2,16,1024]{3,2,1,0:T(8,128)}, u32[]{:S(2)}) copy-start(f32[4,2,16,1024]{3,2,1,0:T(8,128)} %param.10) | copy-start | bytes 1572868
  3.3 9.4 %collective-permute-start.2 = (f32[4,3296]{1,0:T(4,128)S(1)}, f32[4,3296]{1,0:T(4,128)S(1)}, u32[]{:S(2)}, u32[]{:S(2)}) collective-permute-start(f32[4,3296]{1,0:T(4,128)S(1)} %get-tuple-element.35), channel_id=1, source_target_pairs={{0,16},{16,32},{32,48},{48,64},{64,80},{80,96},{96,112},{112,128},... | collective-permute-start | bytes 158216 | tf_op jit(solution)/shard_map/ppermute | solution.py:29
  5.3 7.5 %collective-permute-start.3 = (f32[4,3296]{1,0:T(4,128)S(1)}, f32[4,3296]{1,0:T(4,128)S(1)}, u32[]{:S(2)}, u32[]{:S(2)}) collective-permute-start(f32[4,3296]{1,0:T(4,128)S(1)} %get-tuple-element.36), channel_id=1, source_target_pairs={{16,0},{32,16},{48,32},{64,48},{80,64},{96,80},{112,96},{128,112},... | collective-permute-start | bytes 158216 | tf_op jit(solution)/shard_map/ppermute | solution.py:31
  7.2 46.7 %collective-permute-start.1 = (f32[16,2,4,1024]{3,2,1,0:T(4,128)S(1)}, f32[16,2,4,1024]{3,2,1,0:T(4,128)}, u32[]{:S(2)}, u32[]{:S(2)}) collective-permute-start(f32[16,2,4,1024]{3,2,1,0:T(4,128)S(1)} %get-tuple-element.24), channel_id=1, source_target_pairs={{16,0},{32,16},{48,32},{64,48},{80,64},{96,80},{112,96},{128,112},... | collective-permute-start | bytes 1572872 | tf_op jit(solution)/shard_map/ppermute | solution.py:167
  12.7 41.3 %collective-permute-start = (f32[16,2,4,1024]{3,2,1,0:T(4,128)S(1)}, f32[16,2,4,1024]{3,2,1,0:T(4,128)}, u32[]{:S(2)}, u32[]{:S(2)}) collective-permute-start(f32[16,2,4,1024]{3,2,1,0:T(4,128)S(1)} %get-tuple-element.25), channel_id=1, source_target_pairs={{0,16},{16,32},{32,48},{48,64},{64,80},{80,96},{96,112},{112,128},... | collective-permute-start | bytes 1572872 | tf_op jit(solution)/shard_map/ppermute | solution.py:166
  12.9 4.8 %collective-permute-start.6 = (f32[2,24,64]{2,1,0:T(8,128)S(1)}, f32[2,24,64]{2,1,0:T(8,128)S(1)}, u32[]{:S(2)}, u32[]{:S(2)}) collective-permute-start(f32[2,24,64]{2,1,0:T(8,128)S(1)} %pad_maximum_fusion.1), channel_id=1, source_target_pairs={{0,1},{1,2},{2,3},{3,4},{4,5},{5,6},{6,7},{7,8},{8,9},{9,10},{10,1... | collective-permute-start | bytes 36872 | tf_op jit(solution)/shard_map/ppermute | solution.py:47
  12.9 4.8 %collective-permute-start.5 = (f32[2,24,64]{2,1,0:T(8,128)S(1)}, f32[2,24,64]{2,1,0:T(8,128)S(1)}, u32[]{:S(2)}, u32[]{:S(2)}) collective-permute-start(f32[2,24,64]{2,1,0:T(8,128)S(1)} %pad_maximum_fusion.1), channel_id=1, source_target_pairs={{0,2},{1,3},{2,4},{3,5},{4,6},{5,7},{6,8},{7,9},{8,10},{9,11},{10,... | collective-permute-start | bytes 36872 | tf_op jit(solution)/shard_map/ppermute | solution.py:47
  14.3 5.0 %collective-permute-start.4 = (f32[2,24,64]{2,1,0:T(8,128)S(1)}, f32[2,24,64]{2,1,0:T(8,128)S(1)}, u32[]{:S(2)}, u32[]{:S(2)}) collective-permute-start(f32[2,24,64]{2,1,0:T(8,128)S(1)} %pad_maximum_fusion.1), channel_id=1, source_target_pairs={{0,3},{1,4},{2,5},{3,6},{4,7},{5,8},{6,9},{7,10},{8,11},{9,12},{10... | collective-permute-start | bytes 36872 | tf_op jit(solution)/shard_map/ppermute | solution.py:47
  19.3 26.1 %collective-permute-start.9 = (f32[2,24,64]{2,1,0:T(8,128)S(1)}, f32[2,24,64]{2,1,0:T(8,128)S(1)}, u32[]{:S(2)}, u32[]{:S(2)}) collective-permute-start(f32[2,24,64]{2,1,0:T(8,128)S(1)} %select_select_fusion.1), channel_id=1, source_target_pairs={{0,4},{1,5},{2,6},{3,7},{4,8},{5,9},{6,10},{7,11},{8,12},{9,13},{1... | collective-permute-start | bytes 36872 | tf_op jit(solution)/shard_map/ppermute | solution.py:47
  42.4 5.3 %collective-permute-start.8 = (f32[2,24,64]{2,1,0:T(8,128)S(1)}, f32[2,24,64]{2,1,0:T(8,128)S(1)}, u32[]{:S(2)}, u32[]{:S(2)}) collective-permute-start(f32[2,24,64]{2,1,0:T(8,128)S(1)} %select_select_fusion.1), channel_id=1, source_target_pairs={{0,8},{1,9},{2,10},{3,11},{4,12},{5,13},{6,14},{7,15},{8,0},{9,1},... | collective-permute-start | bytes 36872 | tf_op jit(solution)/shard_map/ppermute | solution.py:47
  44.5 7.7 %collective-permute-start.7 = (f32[2,24,64]{2,1,0:T(8,128)S(1)}, f32[2,24,64]{2,1,0:T(8,128)S(1)}, u32[]{:S(2)}, u32[]{:S(2)}) collective-permute-start(f32[2,24,64]{2,1,0:T(8,128)S(1)} %select_select_fusion.1), channel_id=1, source_target_pairs={{0,12},{1,13},{2,14},{3,15},{4,0},{5,1},{6,2},{7,3},{8,4},{9,5},{1... | collective-permute-start | bytes 36872 | tf_op jit(solution)/shard_map/ppermute | solution.py:47
  44.6 8.7 %copy-start.1 = (f32[6,48,1024]{2,1,0:T(8,128)}, f32[6,48,1024]{2,1,0:T(8,128)S(1)}, u32[]{:S(2)}) copy-start(f32[6,48,1024]{2,1,0:T(8,128)S(1)} %bitcast_dynamic-update-slice_fusion.w_ref) | copy-start | bytes 3538948

commit v4 on v3

--- a/solution.py
+++ b/solution.py
@@ -37,18 +37,19 @@
 
 def spread(value, axis, source):
     count = lax.axis_size(axis)
-    rank = (lax.axis_index(axis) - source) % count
-    reach = 1
-    while reach < count:
-        fan = min(4, -(-count // reach))
-        received = value
-        for k in range(1, fan):
-            shift = k * reach
-            moved = lax.ppermute(value, axis, [(i, (i + shift) % count) for i in range(count)])
-            received = jnp.where((rank >= shift) & (rank < shift + reach), moved, received)
-        value = received
-        reach *= fan
-    return value
+    top = count // 2
+    if count < 2 or count & (count - 1):
+        kept = jnp.where(lax.axis_index(axis) == source, value, 0).astype(value.dtype)
+        return lax.psum(kept, axis)
+    rank = jnp.bitwise_xor(lax.axis_index(axis), source)
+    moved = lax.ppermute(value, axis, [(i, i ^ top) for i in range(count)])
+    value = jnp.where(rank == top, moved, value)
+    low = rank & (top - 1)
+    received = value
+    for mask in range(1, top):
+        moved = lax.ppermute(value, axis, [(i, i ^ mask) for i in range(count)])
+        received = jnp.where(low == mask, moved, received)
+    return received
 
 
 def chemistry(carbon, alkalinity, piston, surface_sea):
@@ -155,8 +156,8 @@
     return jnp.concatenate([surface, adjoint[..., ROWS:]], axis=-1)
 
 
-SPAN = 48
-ORIGIN = 16
+SPAN = 40
+ORIGIN = 10
 
 
 def halves(cells, axis, dim, width):
@@ -208,7 +209,7 @@
         head = adjoint[:, 0:128] + s_ref[stage, t, r : r + 8, :] * forcing
         return head, adjoint[:, 128:]
 
-    for r in range(ORIGIN - 8, ORIGIN + local + 8, 8):
+    for r in range(ORIGIN - 2, ORIGIN + local + 2, 8):
         for t in range(2):
             head, rest = block(e_ref, r, t, 0)
             f_ref[t, r : r + 8, 0:128] = head

time: 73 us -> 72.9 us (level)
  the two profiles are of different devices: /device:TPU:18 before, /device:TPU:1 now
where the time goes in v4:
time: 72.9 us; the launch traced here: 72.3 us
  starting transfers between devices  23.5 us (32%)
  waiting for transfers between devices  21 us (29%)
  Pallas kernels  17 us (23%)
  local copies, waits for them, and re-layouts  6.5 us (9%)
  other arithmetic  3.35 us (5%)
  between operations  0.97 us (1%)
    ppermute x1, waiting for transfers between devices, halves(): lax.ppermute(head, axis, [((i + 1) % count, i) for i in range(count)])  19.6 us
    pallas_call x1, Pallas kernels, two_retreats(): pl.pallas_call(retreat_kernel, out_shape=jax.ShapeDtypeStruct(center.shap...  17 us
    ppermute x7, starting transfers between devices, spread(): moved = lax.ppermute(value, axis, [(i, i ^ mask) for i in range(count)])  10.1 us
    ppermute x1, starting transfers between devices, padded(): lax.ppermute(head, axis, [((i + 1) % count, i) for i in range(count)])  5.38 us
    ppermute x1, starting transfers between devices, halves(): lax.ppermute(head, axis, [((i + 1) % count, i) for i in range(count)])  3.37 us
    slice x1, local copies, waits for them, and re-layouts, halves(): head = lax.slice_in_dim(cells, 0, width, axis=dim)  2.57 us
    ppermute x1, starting transfers between devices, spread(): moved = lax.ppermute(value, axis, [(i, i ^ top) for i in range(count)])  2.53 us
    ppermute x1, starting transfers between devices, padded(): lax.ppermute(tail, axis, [(i, (i + 1) % count) for i in range(count)])  2.11 us
  transfers between devices with their start and end apart: 12, of which 2 were waited for; matrix products, arithmetic and copies ran while one was open for 7% of the time, Pallas kernels for 0%

profile of v4, /device:TPU:1, one launch (start us, length us, event | category | flops | bytes accessed | tf_op | source)
XLA Modules:
  0.0 72.3 jit_solution(8581829839205124377)
XLA Ops:
  0.7 0.7 convert_element_type.43
  1.4 0.8 %convert_element_type.42 = f32[16,1024]{1,0:T(8,128)S(1)} convert(s32[16,1024]{1,0:T(8,128)} %param.12) | non-fusion elementwise | flops 16384 | bytes 131072 | tf_op jit(solution)/shard_map/convert_element_type | solution.py:261
  2.3 1.0 %concatenate.30 = f32[16,3296]{1,0:T(8,128)S(1)} concatenate(f32[16,64]{1,0:T(8,128)S(1)} %get-tuple-element.38, f32[16,64]{1,0:T(8,128)S(1)} %get-tuple-element.37, f32[16,1024]{1,0:T(8,128)S(1)} %convert_element_type.42, f32[16,1024]{1,0:T(8,128)} %param.13, f32[16,1024]{1,0:T(8,128)} %param.14, f32[16,32]{1,0:T(8,128)} %param.15, f32[16,32]{1,0:T(8,128)} %param.16, ...), dimensions={1} | concatenate | bytes 421888 | tf_op jit(solution)/shard_map/concatenate | solution.py:257
  3.3 2.1 %collective-permute-start.2 = (f32[4,3296]{1,0:T(4,128)S(1)}, f32[4,3296]{1,0:T(4,128)S(1)}, u32[]{:S(2)}, u32[]{:S(2)}) collective-permute-start(f32[4,3296]{1,0:T(4,128)S(1)} %get-tuple-element.35), channel_id=1, source_target_pairs={{0,16},{16,32},{32,48},{48,64},{64,80},{80,96},{96,112},{112,128},... | collective-permute-start | bytes 158216 | tf_op jit(solution)/shard_map/ppermute | solution.py:29
  5.4 5.4 %collective-permute-start.3 = (f32[4,3296]{1,0:T(4,128)S(1)}, f32[4,3296]{1,0:T(4,128)S(1)}, u32[]{:S(2)}, u32[]{:S(2)}) collective-permute-start(f32[4,3296]{1,0:T(4,128)S(1)} %get-tuple-element.36), channel_id=1, source_target_pairs={{16,0},{32,16},{48,32},{64,48},{80,64},{96,80},{112,96},{128,112},... | collective-permute-start | bytes 158216 | tf_op jit(solution)/shard_map/ppermute | solution.py:31
  10.8 2.6 %fusion.52 = (f32[16,2,4,1024]{3,2,1,0:T(4,128)}, f32[16,2,4,1024]{3,2,1,0:T(4,128)S(1)}) fusion(f32[16,2,16,1024]{3,2,1,0:T(8,128)} %center_ref.1), kind=kLoop, calls=%fused_computation.200 | loop fusion | bytes 2097152 | tf_op jit(solution)/shard_map/slice | solution.py:165
  13.7 2.5 %collective-permute-start.4 = (f32[2,24,64]{2,1,0:T(8,128)S(1)}, f32[2,24,64]{2,1,0:T(8,128)S(1)}, u32[]{:S(2)}, u32[]{:S(2)}) collective-permute-start(f32[2,24,64]{2,1,0:T(8,128)S(1)} %pad_maximum_fusion.1), channel_id=1, source_target_pairs={{0,8},{1,9},{2,10},{3,11},{4,12},{5,13},{6,14},{7,15},{8,0},{9,1},... | collective-permute-start | bytes 36872 | tf_op jit(solution)/shard_map/ppermute | solution.py:45
  16.7 1.3 %collective-permute-done.4 = f32[2,24,64]{2,1,0:T(8,128)S(1)} collective-permute-done((f32[2,24,64]{2,1,0:T(8,128)S(1)}, f32[2,24,64]{2,1,0:T(8,128)S(1)}, u32[]{:S(2)}, u32[]{:S(2)}) %collective-permute-start.4) | collective-permute-done | bytes 12320 | tf_op jit(solution)/shard_map/ppermute | solution.py:45
  18.0 2.1 %collective-permute-start.11 = (f32[2,24,64]{2,1,0:T(8,128)S(1)}, f32[2,24,64]{2,1,0:T(8,128)S(1)}, u32[]{:S(2)}, u32[]{:S(2)}) collective-permute-start(f32[2,24,64]{2,1,0:T(8,128)S(1)} %broadcast_select_fusion), channel_id=1, source_target_pairs={{0,1},{1,0},{2,3},{3,2},{4,5},{5,4},{6,7},{7,6},{8,9},{9,8},{10,11... | collective-permute-start | bytes 36872 | tf_op jit(solution)/shard_map/ppermute | solution.py:50
  20.1 1.3 %collective-permute-start.10 = (f32[2,24,64]{2,1,0:T(8,128)S(1)}, f32[2,24,64]{2,1,0:T(8,128)S(1)}, u32[]{:S(2)}, u32[]{:S(2)}) collective-permute-start(f32[2,24,64]{2,1,0:T(8,128)S(1)} %broadcast_select_fusion), channel_id=1, source_target_pairs={{0,2},{1,3},{2,0},{3,1},{4,6},{5,7},{6,4},{7,5},{8,10},{9,11},{10,... | collective-permute-start | bytes 36872 | tf_op jit(solution)/shard_map/ppermute | solution.py:50
  21.4 0.5 collective-permute-start.9
  21.9 2.9 %collective-permute-start.8 = (f32[2,24,64]{2,1,0:T(8,128)S(1)}, f32[2,24,64]{2,1,0:T(8,128)S(1)}, u32[]{:S(2)}, u32[]{:S(2)}) collective-permute-start(f32[2,24,64]{2,1,0:T(8,128)S(1)} %broadcast_select_fusion), channel_id=1, source_target_pairs={{0,4},{1,5},{2,6},{3,7},{4,0},{5,1},{6,2},{7,3},{8,12},{9,13},{10,... | collective-permute-start | bytes 36872 | tf_op jit(solution)/shard_map/ppermute | solution.py:50
  24.9 0.4 collective-permute-start.7
  25.2 2.7 %collective-permute-start.6 = (f32[2,24,64]{2,1,0:T(8,128)S(1)}, f32[2,24,64]{2,1,0:T(8,128)S(1)}, u32[]{:S(2)}, u32[]{:S(2)}) collective-permute-start(f32[2,24,64]{2,1,0:T(8,128)S(1)} %broadcast_select_fusion), channel_id=1, source_target_pairs={{0,6},{1,7},{2,4},{3,5},{4,2},{5,3},{6,0},{7,1},{8,14},{9,15},{10,... | collective-permute-start | bytes 36872 | tf_op jit(solution)/shard_map/ppermute | solution.py:50
  27.9 0.2 collective-permute-start.5
  28.2 0.8 %pad.99.seed_ref = f32[16,40,128]{2,1,0:T(8,128)} pad(f32[16,24,32]{2,1,0:T(8,128)S(1)} %compare_select_fusion, f32[]{:T(128)} %constant.128.clone.1), padding=0_0x6_10x0_96 | pad | bytes 376836 | tf_op jit(solution)/shard_map/jit(_pad)/pad | solution.py:181
  29.0 3.4 %collective-permute-start.1 = (f32[16,2,4,1024]{3,2,1,0:T(4,128)}, f32[16,2,4,1024]{3,2,1,0:T(4,128)S(1)}, u32[]{:S(2)}, u32[]{:S(2)}) collective-permute-start(f32[16,2,4,1024]{3,2,1,0:T(4,128)} %get-tuple-element.24), channel_id=1, source_target_pairs={{16,0},{32,16},{48,32},{64,48},{80,64},{96,80},{112,96},{128,112},... | collective-permute-start | bytes 1572872 | tf_op jit(solution)/shard_map/ppermute | solution.py:168
  32.8 0.1 fusion.18
  33.0 0.3 add_bitcast_fusion.3
  33.4 0.6 select_maximum_fusion.s_ref
  34.1 19.6 %collective-permute-done.1.east_ref = f32[16,2,4,1024]{3,2,1,0:T(4,128)S(1)} collective-permute-done((f32[16,2,4,1024]{3,2,1,0:T(4,128)}, f32[16,2,4,1024]{3,2,1,0:T(4,128)S(1)}, u32[]{:S(2)}, u32[]{:S(2)}) %collective-permute-start.1) | collective-permute-done | bytes 524320 | tf_op jit(solution)/shard_map/ppermute | solution.py:168
  53.7 0.8 %copy-done.2 = f32[16,2,4,1024]{3,2,1,0:T(4,128)} copy-done((f32[16,2,4,1024]{3,2,1,0:T(4,128)}, f32[16,2,4,1024]{3,2,1,0:T(4,128)S(1)}, u32[]{:S(2)}) %copy-start.2) | copy-done | bytes 524312
  54.5 0.8 %copy-done.3 = f32[16,2,4,1024]{3,2,1,0:T(4,128)} copy-done((f32[16,2,4,1024]{3,2,1,0:T(4,128)}, f32[16,2,4,1024]{3,2,1,0:T(4,128)S(1)}, u32[]{:S(2)}) %copy-start.3) | copy-done | bytes 524312
  55.3 17.0 %shard_map.91 = f32[16,2,16,1024]{3,2,1,0:T(8,128)} custom-call(f32[16,2,16,1024]{3,2,1,0:T(8,128)} %center_ref.1, f32[16,2,4,1024]{3,2,1,0:T(4,128)} %copy-done.3, f32[16,2,4,1024]{3,2,1,0:T(4,128)} %copy-done.2, f32[6,40,1024]{2,1,0:T(8,128)} %copy-done.1, f32[2,2,40,128]{3,2,1,0:T(8,128)} %select_maximum_fusion.s_ref, f32[16,40,128]{2,1,0:T(8,128)} %pad.99.seed_ref), custom_call_target="tpu_custom_call" | custom-call | tf_op jit(solution)/shard_map/pallas_call | solution.py:227
  (56 shorter events, 1.4 us)
Async XLA Ops:
  0.0 2.3 %copy-start = (f32[4,2,16,1024]{3,2,1,0:T(8,128)S(1)}, f32[4,2,16,1024]{3,2,1,0:T(8,128)}, u32[]{:S(2)}) copy-start(f32[4,2,16,1024]{3,2,1,0:T(8,128)} %param.10) | copy-start | bytes 1572868
  3.3 10.1 %collective-permute-start.2 = (f32[4,3296]{1,0:T(4,128)S(1)}, f32[4,3296]{1,0:T(4,128)S(1)}, u32[]{:S(2)}, u32[]{:S(2)}) collective-permute-start(f32[4,3296]{1,0:T(4,128)S(1)} %get-tuple-element.35), channel_id=1, source_target_pairs={{0,16},{16,32},{32,48},{48,64},{64,80},{80,96},{96,112},{112,128},... | collective-permute-start | bytes 158216 | tf_op jit(solution)/shard_map/ppermute | solution.py:29
  5.4 8.0 %collective-permute-start.3 = (f32[4,3296]{1,0:T(4,128)S(1)}, f32[4,3296]{1,0:T(4,128)S(1)}, u32[]{:S(2)}, u32[]{:S(2)}) collective-permute-start(f32[4,3296]{1,0:T(4,128)S(1)} %get-tuple-element.36), channel_id=1, source_target_pairs={{16,0},{32,16},{48,32},{64,48},{80,64},{96,80},{112,96},{128,112},... | collective-permute-start | bytes 158216 | tf_op jit(solution)/shard_map/ppermute | solution.py:31
  13.7 4.3 %collective-permute-start.4 = (f32[2,24,64]{2,1,0:T(8,128)S(1)}, f32[2,24,64]{2,1,0:T(8,128)S(1)}, u32[]{:S(2)}, u32[]{:S(2)}) collective-permute-start(f32[2,24,64]{2,1,0:T(8,128)S(1)} %pad_maximum_fusion.1), channel_id=1, source_target_pairs={{0,8},{1,9},{2,10},{3,11},{4,12},{5,13},{6,14},{7,15},{8,0},{9,1},... | collective-permute-start | bytes 36872 | tf_op jit(solution)/shard_map/ppermute | solution.py:45
  18.0 7.2 %collective-permute-start.11 = (f32[2,24,64]{2,1,0:T(8,128)S(1)}, f32[2,24,64]{2,1,0:T(8,128)S(1)}, u32[]{:S(2)}, u32[]{:S(2)}) collective-permute-start(f32[2,24,64]{2,1,0:T(8,128)S(1)} %broadcast_select_fusion), channel_id=1, source_target_pairs={{0,1},{1,0},{2,3},{3,2},{4,5},{5,4},{6,7},{7,6},{8,9},{9,8},{10,11... | collective-permute-start | bytes 36872 | tf_op jit(solution)/shard_map/ppermute | solution.py:50
  20.1 7.8 %collective-permute-start.10 = (f32[2,24,64]{2,1,0:T(8,128)S(1)}, f32[2,24,64]{2,1,0:T(8,128)S(1)}, u32[]{:S(2)}, u32[]{:S(2)}) collective-permute-start(f32[2,24,64]{2,1,0:T(8,128)S(1)} %broadcast_select_fusion), channel_id=1, source_target_pairs={{0,2},{1,3},{2,0},{3,1},{4,6},{5,7},{6,4},{7,5},{8,10},{9,11},{10,... | collective-permute-start | bytes 36872 | tf_op jit(solution)/shard_map/ppermute | solution.py:50
  21.4 7.6 %collective-permute-start.9 = (f32[2,24,64]{2,1,0:T(8,128)S(1)}, f32[2,24,64]{2,1,0:T(8,128)S(1)}, u32[]{:S(2)}, u32[]{:S(2)}) collective-permute-start(f32[2,24,64]{2,1,0:T(8,128)S(1)} %broadcast_select_fusion), channel_id=1, source_target_pairs={{0,3},{1,2},{2,1},{3,0},{4,7},{5,6},{6,5},{7,4},{8,11},{9,10},{10,... | collective-permute-start | bytes 36872 | tf_op jit(solution)/shard_map/ppermute | solution.py:50
  21.9 10.5 %collective-permute-start.8 = (f32[2,24,64]{2,1,0:T(8,128)S(1)}, f32[2,24,64]{2,1,0:T(8,128)S(1)}, u32[]{:S(2)}, u32[]{:S(2)}) collective-permute-start(f32[2,24,64]{2,1,0:T(8,128)S(1)} %broadcast_select_fusion), channel_id=1, source_target_pairs={{0,4},{1,5},{2,6},{3,7},{4,0},{5,1},{6,2},{7,3},{8,12},{9,13},{10,... | collective-permute-start | bytes 36872 | tf_op jit(solution)/shard_map/ppermute | solution.py:50
  24.9 7.6 %collective-permute-start.7 = (f32[2,24,64]{2,1,0:T(8,128)S(1)}, f32[2,24,64]{2,1,0:T(8,128)S(1)}, u32[]{:S(2)}, u32[]{:S(2)}) collective-permute-start(f32[2,24,64]{2,1,0:T(8,128)S(1)} %broadcast_select_fusion), channel_id=1, source_target_pairs={{0,5},{1,4},{2,7},{3,6},{4,1},{5,0},{6,3},{7,2},{8,13},{9,12},{10,... | collective-permute-start | bytes 36872 | tf_op jit(solution)/shard_map/ppermute | solution.py:50
  25.2 7.2 %collective-permute-start.6 = (f32[2,24,64]{2,1,0:T(8,128)S(1)}, f32[2,24,64]{2,1,0:T(8,128)S(1)}, u32[]{:S(2)}, u32[]{:S(2)}) collective-permute-start(f32[2,24,64]{2,1,0:T(8,128)S(1)} %broadcast_select_fusion), channel_id=1, source_target_pairs={{0,6},{1,7},{2,4},{3,5},{4,2},{5,3},{6,0},{7,1},{8,14},{9,15},{10,... | collective-permute-start | bytes 36872 | tf_op jit(solution)/shard_map/ppermute | solution.py:50
  27.9 4.5 %collective-permute-start.5 = (f32[2,24,64]{2,1,0:T(8,128)S(1)}, f32[2,24,64]{2,1,0:T(8,128)S(1)}, u32[]{:S(2)}, u32[]{:S(2)}) collective-permute-start(f32[2,24,64]{2,1,0:T(8,128)S(1)} %broadcast_select_fusion), channel_id=1, source_target_pairs={{0,7},{1,6},{2,5},{3,4},{4,3},{5,2},{6,1},{7,0},{8,15},{9,14},{10,... | collective-permute-start | bytes 36872 | tf_op jit(solution)/shard_map/ppermute | solution.py:50
  28.2 25.5 %copy-start.1 = (f32[6,40,1024]{2,1,0:T(8,128)}, f32[6,40,1024]{2,1,0:T(8,128)S(1)}, u32[]{:S(2)}) copy-start(f32[6,40,1024]{2,1,0:T(8,128)S(1)} %bitcast_dynamic-update-slice_fusion.w_ref) | copy-start | bytes 2949124
  29.0 24.6 %collective-permute-start.1 = (f32[16,2,4,1024]{3,2,1,0:T(4,128)}, f32[16,2,4,1024]{3,2,1,0:T(4,128)S(1)}, u32[]{:S(2)}, u32[]{:S(2)}) collective-permute-start(f32[16,2,4,1024]{3,2,1,0:T(4,128)} %get-tuple-element.24), channel_id=1, source_target_pairs={{16,0},{32,16},{48,32},{64,48},{80,64},{96,80},{112,96},{128,112},... | collective-permute-start | bytes 1572872 | tf_op jit(solution)/shard_map/ppermute | solution.py:168
  32.4 21.3 %collective-permute-start = (f32[16,2,4,1024]{3,2,1,0:T(4,128)S(1)}, f32[16,2,4,1024]{3,2,1,0:T(4,128)S(1)}, u32[]{:S(2)}, u32[]{:S(2)}) collective-permute-start(f32[16,2,4,1024]{3,2,1,0:T(4,128)S(1)} %get-tuple-element.25), channel_id=1, source_target_pairs={{0,16},{16,32},{32,48},{48,64},{64,80},{80,96},{96,112},{112,128},... | collective-permute-start | bytes 1572872 | tf_op jit(solution)/shard_map/ppermute | solution.py:167
  53.7 0.8 %copy-start.2 = (f32[16,2,4,1024]{3,2,1,0:T(4,128)}, f32[16,2,4,1024]{3,2,1,0:T(4,128)S(1)}, u32[]{:S(2)}) copy-start(f32[16,2,4,1024]{3,2,1,0:T(4,128)S(1)} %collective-permute-done.1.east_ref) | copy-start | bytes 1572868
  54.5 0.8 %copy-start.3 = (f32[16,2,4,1024]{3,2,1,0:T(4,128)}, f32[16,2,4,1024]{3,2,1,0:T(4,128)S(1)}, u32[]{:S(2)}) copy-start(f32[16,2,4,1024]{3,2,1,0:T(4,128)S(1)} %collective-permute-done.west_ref) | copy-start | bytes 1572868

commit v5 on v4

--- a/solution.py
+++ b/solution.py
@@ -54,7 +54,7 @@
 
 def chemistry(carbon, alkalinity, piston, surface_sea):
     hydrogen = jnp.full_like(carbon, START_HYDROGEN)
-    for iteration in range(NEWTON):
+    for _ in range(NEWTON):
         square = hydrogen * hydrogen
         denominator = square + DISSOCIATION_ONE * hydrogen + DISSOCIATION_ONE * DISSOCIATION_TWO
         carbonate = carbon * DISSOCIATION_ONE * (hydrogen + 2.0 * DISSOCIATION_TWO) / denominator
@@ -138,22 +138,6 @@
     surface_row = transported[0, :, :ROWS] + uptake
     carbon = jnp.concatenate([surface_row, transported[0, :, ROWS:]], axis=-1)
     return jnp.stack([carbon, transported[1]])
-
-
-def retreat(extended, weights, row_weight, level_weight, slopes, objective_seeds):
-    length = extended.shape[2]
-    difference = extended[:, :, 1:] - extended[:, :, :-1]
-    zonal_term = (
-        weights[0, 3 : length - 1] * difference[:, :, 3 : length - 1]
-        + weights[1, 2 : length - 2] * difference[:, :, 2 : length - 2]
-        + weights[2, 1 : length - 3] * difference[:, :, 1 : length - 3]
-        + weights[3, 0 : length - 4] * difference[:, :, 0 : length - 4]
-    )
-    interior = extended[:, :, 2 : length - 2]
-    adjoint = interior + zonal_term + column_mix(interior, row_weight, level_weight)
-    forcing = interior[:, 0, :, :ROWS] + objective_seeds
-    surface = adjoint[..., :ROWS] + slopes[None] * forcing[:, None]
-    return jnp.concatenate([surface, adjoint[..., ROWS:]], axis=-1)
 
 
 SPAN = 40
@@ -244,7 +228,7 @@
     )(center, west, east, stencil, slopes, seeds)
 
 
-def body(
+def staged(
     adjoint_in, checkpoint_store, interval, sea_mask, zonal_speed, mixing, piston, cell_area, region
 ):
     groups = adjoint_in.shape[0]
@@ -344,5 +328,5 @@
         P("tile", None),
     )
     return jax.shard_map(
-        body, mesh=mesh, in_specs=placed, out_specs=P("obj", None, "tile", None), check_vma=False
-    )
+        staged, mesh=mesh, in_specs=placed, out_specs=P("obj", None, "tile", None), check_vma=False
+    )

time: 72.9 us -> 72.9 us (level)
  no operation moved by 1% of the time
where the time goes in v5:
time: 72.9 us; the launch traced here: 72.3 us
  starting transfers between devices  23.5 us (32%)
  waiting for transfers between devices  21 us (29%)
  Pallas kernels  17 us (23%)
  local copies, waits for them, and re-layouts  6.5 us (9%)
  other arithmetic  3.35 us (5%)
  between operations  0.97 us (1%)
    ppermute x1, waiting for transfers between devices, halves(): lax.ppermute(head, axis, [((i + 1) % count, i) for i in range(count)])  19.6 us
    pallas_call x1, Pallas kernels, two_retreats(): pl.pallas_call(retreat_kernel, out_shape=jax.ShapeDtypeStruct(center.shap...  17 us
    ppermute x7, starting transfers between devices, spread(): moved = lax.ppermute(value, axis, [(i, i ^ mask) for i in range(count)])  10.1 us
    ppermute x1, starting transfers between devices, padded(): lax.ppermute(head, axis, [((i + 1) % count, i) for i in range(count)])  5.38 us
    ppermute x1, starting transfers between devices, halves(): lax.ppermute(head, axis, [((i + 1) % count, i) for i in range(count)])  3.37 us
    slice x1, local copies, waits for them, and re-layouts, halves(): head = lax.slice_in_dim(cells, 0, width, axis=dim)  2.57 us
    ppermute x1, starting transfers between devices, spread(): moved = lax.ppermute(value, axis, [(i, i ^ top) for i in range(count)])  2.53 us
    ppermute x1, starting transfers between devices, padded(): lax.ppermute(tail, axis, [(i, (i + 1) % count) for i in range(count)])  2.11 us
  transfers between devices with their start and end apart: 12, of which 2 were waited for; matrix products, arithmetic and copies ran while one was open for 7% of the time, Pallas kernels for 0%

profile of v5, /device:TPU:1, one launch (start us, length us, event | category | flops | bytes accessed | tf_op | source)
XLA Modules:
  0.0 72.3 jit_solution(8581829839205124377)
XLA Ops:
  0.7 0.7 convert_element_type.43
  1.4 0.8 %convert_element_type.42 = f32[16,1024]{1,0:T(8,128)S(1)} convert(s32[16,1024]{1,0:T(8,128)} %param.12) | non-fusion elementwise | flops 16384 | bytes 131072 | tf_op jit(solution)/shard_map/convert_element_type | solution.py:245
  2.3 1.0 %concatenate.30 = f32[16,3296]{1,0:T(8,128)S(1)} concatenate(f32[16,64]{1,0:T(8,128)S(1)} %get-tuple-element.38, f32[16,64]{1,0:T(8,128)S(1)} %get-tuple-element.37, f32[16,1024]{1,0:T(8,128)S(1)} %convert_element_type.42, f32[16,1024]{1,0:T(8,128)} %param.13, f32[16,1024]{1,0:T(8,128)} %param.14, f32[16,32]{1,0:T(8,128)} %param.15, f32[16,32]{1,0:T(8,128)} %param.16, ...), dimensions={1} | concatenate | bytes 421888 | tf_op jit(solution)/shard_map/concatenate | solution.py:241
  3.3 2.1 %collective-permute-start.2 = (f32[4,3296]{1,0:T(4,128)S(1)}, f32[4,3296]{1,0:T(4,128)S(1)}, u32[]{:S(2)}, u32[]{:S(2)}) collective-permute-start(f32[4,3296]{1,0:T(4,128)S(1)} %get-tuple-element.35), channel_id=1, source_target_pairs={{0,16},{16,32},{32,48},{48,64},{64,80},{80,96},{96,112},{112,128},... | collective-permute-start | bytes 158216 | tf_op jit(solution)/shard_map/ppermute | solution.py:29
  5.4 5.4 %collective-permute-start.3 = (f32[4,3296]{1,0:T(4,128)S(1)}, f32[4,3296]{1,0:T(4,128)S(1)}, u32[]{:S(2)}, u32[]{:S(2)}) collective-permute-start(f32[4,3296]{1,0:T(4,128)S(1)} %get-tuple-element.36), channel_id=1, source_target_pairs={{16,0},{32,16},{48,32},{64,48},{80,64},{96,80},{112,96},{128,112},... | collective-permute-start | bytes 158216 | tf_op jit(solution)/shard_map/ppermute | solution.py:31
  10.8 2.6 %fusion.52 = (f32[16,2,4,1024]{3,2,1,0:T(4,128)}, f32[16,2,4,1024]{3,2,1,0:T(4,128)S(1)}) fusion(f32[16,2,16,1024]{3,2,1,0:T(8,128)} %center_ref.1), kind=kLoop, calls=%fused_computation.200 | loop fusion | bytes 2097152 | tf_op jit(solution)/shard_map/slice | solution.py:149
  13.7 2.5 %collective-permute-start.4 = (f32[2,24,64]{2,1,0:T(8,128)S(1)}, f32[2,24,64]{2,1,0:T(8,128)S(1)}, u32[]{:S(2)}, u32[]{:S(2)}) collective-permute-start(f32[2,24,64]{2,1,0:T(8,128)S(1)} %pad_maximum_fusion.1), channel_id=1, source_target_pairs={{0,8},{1,9},{2,10},{3,11},{4,12},{5,13},{6,14},{7,15},{8,0},{9,1},... | collective-permute-start | bytes 36872 | tf_op jit(solution)/shard_map/ppermute | solution.py:45
  16.7 1.3 %collective-permute-done.4 = f32[2,24,64]{2,1,0:T(8,128)S(1)} collective-permute-done((f32[2,24,64]{2,1,0:T(8,128)S(1)}, f32[2,24,64]{2,1,0:T(8,128)S(1)}, u32[]{:S(2)}, u32[]{:S(2)}) %collective-permute-start.4) | collective-permute-done | bytes 12320 | tf_op jit(solution)/shard_map/ppermute | solution.py:45
  18.0 2.1 %collective-permute-start.11 = (f32[2,24,64]{2,1,0:T(8,128)S(1)}, f32[2,24,64]{2,1,0:T(8,128)S(1)}, u32[]{:S(2)}, u32[]{:S(2)}) collective-permute-start(f32[2,24,64]{2,1,0:T(8,128)S(1)} %broadcast_select_fusion), channel_id=1, source_target_pairs={{0,1},{1,0},{2,3},{3,2},{4,5},{5,4},{6,7},{7,6},{8,9},{9,8},{10,11... | collective-permute-start | bytes 36872 | tf_op jit(solution)/shard_map/ppermute | solution.py:50
  20.1 1.3 %collective-permute-start.10 = (f32[2,24,64]{2,1,0:T(8,128)S(1)}, f32[2,24,64]{2,1,0:T(8,128)S(1)}, u32[]{:S(2)}, u32[]{:S(2)}) collective-permute-start(f32[2,24,64]{2,1,0:T(8,128)S(1)} %broadcast_select_fusion), channel_id=1, source_target_pairs={{0,2},{1,3},{2,0},{3,1},{4,6},{5,7},{6,4},{7,5},{8,10},{9,11},{10,... | collective-permute-start | bytes 36872 | tf_op jit(solution)/shard_map/ppermute | solution.py:50
  21.4 0.5 collective-permute-start.9
  21.9 2.9 %collective-permute-start.8 = (f32[2,24,64]{2,1,0:T(8,128)S(1)}, f32[2,24,64]{2,1,0:T(8,128)S(1)}, u32[]{:S(2)}, u32[]{:S(2)}) collective-permute-start(f32[2,24,64]{2,1,0:T(8,128)S(1)} %broadcast_select_fusion), channel_id=1, source_target_pairs={{0,4},{1,5},{2,6},{3,7},{4,0},{5,1},{6,2},{7,3},{8,12},{9,13},{10,... | collective-permute-start | bytes 36872 | tf_op jit(solution)/shard_map/ppermute | solution.py:50
  24.9 0.4 collective-permute-start.7
  25.2 2.7 %collective-permute-start.6 = (f32[2,24,64]{2,1,0:T(8,128)S(1)}, f32[2,24,64]{2,1,0:T(8,128)S(1)}, u32[]{:S(2)}, u32[]{:S(2)}) collective-permute-start(f32[2,24,64]{2,1,0:T(8,128)S(1)} %broadcast_select_fusion), channel_id=1, source_target_pairs={{0,6},{1,7},{2,4},{3,5},{4,2},{5,3},{6,0},{7,1},{8,14},{9,15},{10,... | collective-permute-start | bytes 36872 | tf_op jit(solution)/shard_map/ppermute | solution.py:50
  27.9 0.2 collective-permute-start.5
  28.2 0.8 %pad.99.seed_ref = f32[16,40,128]{2,1,0:T(8,128)} pad(f32[16,24,32]{2,1,0:T(8,128)S(1)} %compare_select_fusion, f32[]{:T(128)} %constant.128.clone.1), padding=0_0x6_10x0_96 | pad | bytes 376836 | tf_op jit(solution)/shard_map/jit(_pad)/pad | solution.py:165
  29.0 3.4 %collective-permute-start.1 = (f32[16,2,4,1024]{3,2,1,0:T(4,128)}, f32[16,2,4,1024]{3,2,1,0:T(4,128)S(1)}, u32[]{:S(2)}, u32[]{:S(2)}) collective-permute-start(f32[16,2,4,1024]{3,2,1,0:T(4,128)} %get-tuple-element.24), channel_id=1, source_target_pairs={{16,0},{32,16},{48,32},{64,48},{80,64},{96,80},{112,96},{128,112},... | collective-permute-start | bytes 1572872 | tf_op jit(solution)/shard_map/ppermute | solution.py:152
  32.8 0.1 fusion.18
  33.0 0.3 add_bitcast_fusion.3
  33.4 0.6 select_maximum_fusion.s_ref
  34.1 19.6 %collective-permute-done.1.east_ref = f32[16,2,4,1024]{3,2,1,0:T(4,128)S(1)} collective-permute-done((f32[16,2,4,1024]{3,2,1,0:T(4,128)}, f32[16,2,4,1024]{3,2,1,0:T(4,128)S(1)}, u32[]{:S(2)}, u32[]{:S(2)}) %collective-permute-start.1) | collective-permute-done | bytes 524320 | tf_op jit(solution)/shard_map/ppermute | solution.py:152
  53.7 0.8 %copy-done.2 = f32[16,2,4,1024]{3,2,1,0:T(4,128)} copy-done((f32[16,2,4,1024]{3,2,1,0:T(4,128)}, f32[16,2,4,1024]{3,2,1,0:T(4,128)S(1)}, u32[]{:S(2)}) %copy-start.2) | copy-done | bytes 524312
  54.5 0.8 %copy-done.3 = f32[16,2,4,1024]{3,2,1,0:T(4,128)} copy-done((f32[16,2,4,1024]{3,2,1,0:T(4,128)}, f32[16,2,4,1024]{3,2,1,0:T(4,128)S(1)}, u32[]{:S(2)}) %copy-start.3) | copy-done | bytes 524312
  55.3 17.0 %shard_map.91 = f32[16,2,16,1024]{3,2,1,0:T(8,128)} custom-call(f32[16,2,16,1024]{3,2,1,0:T(8,128)} %center_ref.1, f32[16,2,4,1024]{3,2,1,0:T(4,128)} %copy-done.3, f32[16,2,4,1024]{3,2,1,0:T(4,128)} %copy-done.2, f32[6,40,1024]{2,1,0:T(8,128)} %copy-done.1, f32[2,2,40,128]{3,2,1,0:T(8,128)} %select_maximum_fusion.s_ref, f32[16,40,128]{2,1,0:T(8,128)} %pad.99.seed_ref), custom_call_target="tpu_custom_call" | custom-call | tf_op jit(solution)/shard_map/pallas_call | solution.py:211
  (56 shorter events, 1.4 us)
Async XLA Ops:
  0.0 2.3 %copy-start = (f32[4,2,16,1024]{3,2,1,0:T(8,128)S(1)}, f32[4,2,16,1024]{3,2,1,0:T(8,128)}, u32[]{:S(2)}) copy-start(f32[4,2,16,1024]{3,2,1,0:T(8,128)} %param.10) | copy-start | bytes 1572868
  3.3 10.1 %collective-permute-start.2 = (f32[4,3296]{1,0:T(4,128)S(1)}, f32[4,3296]{1,0:T(4,128)S(1)}, u32[]{:S(2)}, u32[]{:S(2)}) collective-permute-start(f32[4,3296]{1,0:T(4,128)S(1)} %get-tuple-element.35), channel_id=1, source_target_pairs={{0,16},{16,32},{32,48},{48,64},{64,80},{80,96},{96,112},{112,128},... | collective-permute-start | bytes 158216 | tf_op jit(solution)/shard_map/ppermute | solution.py:29
  5.4 8.0 %collective-permute-start.3 = (f32[4,3296]{1,0:T(4,128)S(1)}, f32[4,3296]{1,0:T(4,128)S(1)}, u32[]{:S(2)}, u32[]{:S(2)}) collective-permute-start(f32[4,3296]{1,0:T(4,128)S(1)} %get-tuple-element.36), channel_id=1, source_target_pairs={{16,0},{32,16},{48,32},{64,48},{80,64},{96,80},{112,96},{128,112},... | collective-permute-start | bytes 158216 | tf_op jit(solution)/shard_map/ppermute | solution.py:31
  13.7 4.3 %collective-permute-start.4 = (f32[2,24,64]{2,1,0:T(8,128)S(1)}, f32[2,24,64]{2,1,0:T(8,128)S(1)}, u32[]{:S(2)}, u32[]{:S(2)}) collective-permute-start(f32[2,24,64]{2,1,0:T(8,128)S(1)} %pad_maximum_fusion.1), channel_id=1, source_target_pairs={{0,8},{1,9},{2,10},{3,11},{4,12},{5,13},{6,14},{7,15},{8,0},{9,1},... | collective-permute-start | bytes 36872 | tf_op jit(solution)/shard_map/ppermute | solution.py:45
  18.0 7.2 %collective-permute-start.11 = (f32[2,24,64]{2,1,0:T(8,128)S(1)}, f32[2,24,64]{2,1,0:T(8,128)S(1)}, u32[]{:S(2)}, u32[]{:S(2)}) collective-permute-start(f32[2,24,64]{2,1,0:T(8,128)S(1)} %broadcast_select_fusion), channel_id=1, source_target_pairs={{0,1},{1,0},{2,3},{3,2},{4,5},{5,4},{6,7},{7,6},{8,9},{9,8},{10,11... | collective-permute-start | bytes 36872 | tf_op jit(solution)/shard_map/ppermute | solution.py:50
  20.1 7.8 %collective-permute-start.10 = (f32[2,24,64]{2,1,0:T(8,128)S(1)}, f32[2,24,64]{2,1,0:T(8,128)S(1)}, u32[]{:S(2)}, u32[]{:S(2)}) collective-permute-start(f32[2,24,64]{2,1,0:T(8,128)S(1)} %broadcast_select_fusion), channel_id=1, source_target_pairs={{0,2},{1,3},{2,0},{3,1},{4,6},{5,7},{6,4},{7,5},{8,10},{9,11},{10,... | collective-permute-start | bytes 36872 | tf_op jit(solution)/shard_map/ppermute | solution.py:50
  21.4 7.6 %collective-permute-start.9 = (f32[2,24,64]{2,1,0:T(8,128)S(1)}, f32[2,24,64]{2,1,0:T(8,128)S(1)}, u32[]{:S(2)}, u32[]{:S(2)}) collective-permute-start(f32[2,24,64]{2,1,0:T(8,128)S(1)} %broadcast_select_fusion), channel_id=1, source_target_pairs={{0,3},{1,2},{2,1},{3,0},{4,7},{5,6},{6,5},{7,4},{8,11},{9,10},{10,... | collective-permute-start | bytes 36872 | tf_op jit(solution)/shard_map/ppermute | solution.py:50
  21.9 10.5 %collective-permute-start.8 = (f32[2,24,64]{2,1,0:T(8,128)S(1)}, f32[2,24,64]{2,1,0:T(8,128)S(1)}, u32[]{:S(2)}, u32[]{:S(2)}) collective-permute-start(f32[2,24,64]{2,1,0:T(8,128)S(1)} %broadcast_select_fusion), channel_id=1, source_target_pairs={{0,4},{1,5},{2,6},{3,7},{4,0},{5,1},{6,2},{7,3},{8,12},{9,13},{10,... | collective-permute-start | bytes 36872 | tf_op jit(solution)/shard_map/ppermute | solution.py:50
  24.9 7.6 %collective-permute-start.7 = (f32[2,24,64]{2,1,0:T(8,128)S(1)}, f32[2,24,64]{2,1,0:T(8,128)S(1)}, u32[]{:S(2)}, u32[]{:S(2)}) collective-permute-start(f32[2,24,64]{2,1,0:T(8,128)S(1)} %broadcast_select_fusion), channel_id=1, source_target_pairs={{0,5},{1,4},{2,7},{3,6},{4,1},{5,0},{6,3},{7,2},{8,13},{9,12},{10,... | collective-permute-start | bytes 36872 | tf_op jit(solution)/shard_map/ppermute | solution.py:50
  25.2 7.2 %collective-permute-start.6 = (f32[2,24,64]{2,1,0:T(8,128)S(1)}, f32[2,24,64]{2,1,0:T(8,128)S(1)}, u32[]{:S(2)}, u32[]{:S(2)}) collective-permute-start(f32[2,24,64]{2,1,0:T(8,128)S(1)} %broadcast_select_fusion), channel_id=1, source_target_pairs={{0,6},{1,7},{2,4},{3,5},{4,2},{5,3},{6,0},{7,1},{8,14},{9,15},{10,... | collective-permute-start | bytes 36872 | tf_op jit(solution)/shard_map/ppermute | solution.py:50
  27.9 4.5 %collective-permute-start.5 = (f32[2,24,64]{2,1,0:T(8,128)S(1)}, f32[2,24,64]{2,1,0:T(8,128)S(1)}, u32[]{:S(2)}, u32[]{:S(2)}) collective-permute-start(f32[2,24,64]{2,1,0:T(8,128)S(1)} %broadcast_select_fusion), channel_id=1, source_target_pairs={{0,7},{1,6},{2,5},{3,4},{4,3},{5,2},{6,1},{7,0},{8,15},{9,14},{10,... | collective-permute-start | bytes 36872 | tf_op jit(solution)/shard_map/ppermute | solution.py:50
  28.2 25.5 %copy-start.1 = (f32[6,40,1024]{2,1,0:T(8,128)}, f32[6,40,1024]{2,1,0:T(8,128)S(1)}, u32[]{:S(2)}) copy-start(f32[6,40,1024]{2,1,0:T(8,128)S(1)} %bitcast_dynamic-update-slice_fusion.w_ref) | copy-start | bytes 2949124
  29.0 24.6 %collective-permute-start.1 = (f32[16,2,4,1024]{3,2,1,0:T(4,128)}, f32[16,2,4,1024]{3,2,1,0:T(4,128)S(1)}, u32[]{:S(2)}, u32[]{:S(2)}) collective-permute-start(f32[16,2,4,1024]{3,2,1,0:T(4,128)} %get-tuple-element.24), channel_id=1, source_target_pairs={{16,0},{32,16},{48,32},{64,48},{80,64},{96,80},{112,96},{128,112},... | collective-permute-start | bytes 1572872 | tf_op jit(solution)/shard_map/ppermute | solution.py:152
  32.4 21.3 %collective-permute-start = (f32[16,2,4,1024]{3,2,1,0:T(4,128)S(1)}, f32[16,2,4,1024]{3,2,1,0:T(4,128)S(1)}, u32[]{:S(2)}, u32[]{:S(2)}) collective-permute-start(f32[16,2,4,1024]{3,2,1,0:T(4,128)S(1)} %get-tuple-element.25), channel_id=1, source_target_pairs={{0,16},{16,32},{32,48},{48,64},{64,80},{80,96},{96,112},{112,128},... | collective-permute-start | bytes 1572872 | tf_op jit(solution)/shard_map/ppermute | solution.py:151
  53.7 0.8 %copy-start.2 = (f32[16,2,4,1024]{3,2,1,0:T(4,128)}, f32[16,2,4,1024]{3,2,1,0:T(4,128)S(1)}, u32[]{:S(2)}) copy-start(f32[16,2,4,1024]{3,2,1,0:T(4,128)S(1)} %collective-permute-done.1.east_ref) | copy-start | bytes 1572868
  54.5 0.8 %copy-start.3 = (f32[16,2,4,1024]{3,2,1,0:T(4,128)}, f32[16,2,4,1024]{3,2,1,0:T(4,128)S(1)}, u32[]{:S(2)}) copy-start(f32[16,2,4,1024]{3,2,1,0:T(4,128)S(1)} %collective-permute-done.west_ref) | copy-start | bytes 1572868

commit v6 on v5

--- a/solution.py
+++ b/solution.py
@@ -140,10 +140,6 @@
     return jnp.stack([carbon, transported[1]])
 
 
-SPAN = 40
-ORIGIN = 10
-
-
 def halves(cells, axis, dim, width):
     count = lax.axis_size(axis)
     head = lax.slice_in_dim(cells, 0, width, axis=dim)
@@ -153,79 +149,86 @@
     return west, east
 
 
-def placed_rows(source, first, total=SPAN):
-    pad = [(0, 0)] * source.ndim
-    pad[-2] = (first, total - first - source.shape[-2])
-    return jnp.pad(source, pad)
-
-
-def lanes_to(source, width):
-    pad = [(0, 0)] * source.ndim
-    pad[-1] = (0, width - source.shape[-1])
-    return jnp.pad(source, pad)
+def cell_shift(x, step, lane, forward):
+    if forward:
+        turned = pltpu.roll(x, 128 - step, 1)
+        carried = pltpu.roll(turned, 7, 0)
+        return jnp.where(lane >= 128 - step, carried, turned)
+    turned = pltpu.roll(x, step, 1)
+    carried = pltpu.roll(turned, 1, 0)
+    return jnp.where(lane < step, carried, turned)
 
 
 def retreat_kernel(center_ref, west_ref, east_ref, w_ref, s_ref, seed_ref, out_ref, e_ref, f_ref):
+    tracers = center_ref.shape[1]
     local = center_ref.shape[2]
-    width = center_ref.shape[3]
     rim = west_ref.shape[2]
-    e_ref[:, ORIGIN : ORIGIN + local, :] = center_ref[0]
-    e_ref[:, ORIGIN - rim : ORIGIN, :] = west_ref[0]
-    e_ref[:, ORIGIN + local : ORIGIN + local + rim, :] = east_ref[0]
-
-    def block(src, r, t, stage):
-        x_m2 = src[t, r - 2 : r + 6, :]
-        x_m1 = src[t, r - 1 : r + 7, :]
-        x_0 = src[t, r : r + 8, :]
-        x_p1 = src[t, r + 1 : r + 9, :]
-        x_p2 = src[t, r + 2 : r + 10, :]
-        zonal = (
-            w_ref[0, r : r + 8, :] * (x_p2 - x_p1)
-            + w_ref[1, r : r + 8, :] * (x_p1 - x_0)
-            + w_ref[2, r : r + 8, :] * (x_0 - x_m1)
-            + w_ref[3, r : r + 8, :] * (x_m1 - x_m2)
-        )
-        row_flux = w_ref[4, r : r + 8, :] * (pltpu.roll(x_0, width - 1, 1) - x_0)
-        level_flux = w_ref[5, r : r + 8, :] * (pltpu.roll(x_0, width - ROWS, 1) - x_0)
-        mix = row_flux - pltpu.roll(row_flux, 1, 1) + level_flux - pltpu.roll(level_flux, ROWS, 1)
-        adjoint = x_0 + zonal + mix
-        forcing = src[0, r : r + 8, 0:128] + seed_ref[0, r : r + 8, :]
-        head = adjoint[:, 0:128] + s_ref[stage, t, r : r + 8, :] * forcing
-        return head, adjoint[:, 128:]
-
-    for r in range(ORIGIN - 2, ORIGIN + local + 2, 8):
-        for t in range(2):
-            head, rest = block(e_ref, r, t, 0)
-            f_ref[t, r : r + 8, 0:128] = head
-            f_ref[t, r : r + 8, 128:] = rest
-    for r in range(ORIGIN, ORIGIN + local, 8):
-        for t in range(2):
-            head, rest = block(f_ref, r, t, 1)
-            out_ref[0, t, r - ORIGIN : r - ORIGIN + 8, 0:128] = head
-            out_ref[0, t, r - ORIGIN : r - ORIGIN + 8, 128:] = rest
+    lane = lax.broadcasted_iota(jnp.int32, (8, 128), 1)
+    e_ref[:, rim : rim + local] = center_ref[0]
+    e_ref[:, 0:rim] = west_ref[0]
+    e_ref[:, rim + local : 2 * rim + local] = east_ref[0]
+
+    def step(src, k, stage):
+        w = [w_ref[m, k] for m in range(8)]
+        results = []
+        for t in range(tracers):
+            x_0 = src[t, k]
+            zonal = (
+                w[0] * (src[t, k + 2] - src[t, k + 1])
+                + w[1] * (src[t, k + 1] - x_0)
+                + w[2] * (x_0 - src[t, k - 1])
+                + w[3] * (src[t, k - 1] - src[t, k - 2])
+            )
+            mix = (
+                w[4] * (cell_shift(x_0, 1, lane, True) - x_0)
+                - w[5] * (x_0 - cell_shift(x_0, 1, lane, False))
+                + w[6] * (cell_shift(x_0, ROWS, lane, True) - x_0)
+                - w[7] * (x_0 - cell_shift(x_0, ROWS, lane, False))
+            )
+            forcing = src[0, k] + seed_ref[0, k]
+            results.append(x_0 + zonal + mix + s_ref[stage, t, k] * forcing)
+        return results
+
+    def first(k, carry):
+        for t, value in enumerate(step(e_ref, k, 0)):
+            f_ref[t, k] = value
+        return carry
+
+    def second(k, carry):
+        for t, value in enumerate(step(f_ref, k, 1)):
+            out_ref[0, t, k - rim] = value
+        return carry
+
+    lax.fori_loop(2, 2 * rim + local - 2, first, 0, unroll=True)
+    lax.fori_loop(rim, rim + local, second, 0, unroll=True)
 
 
 def two_retreats(center, west, east, stencil, slopes, seeds):
-    groups, tracers, local, width = center.shape
+    groups, tracers, local, sub, lanes = center.shape
     rim = west.shape[2]
+    span = local + 2 * rim
     return pl.pallas_call(
         retreat_kernel,
         out_shape=jax.ShapeDtypeStruct(center.shape, center.dtype),
         grid=(groups,),
         in_specs=[
-            pl.BlockSpec((1, tracers, local, width), lambda g: (g, 0, 0, 0)),
-            pl.BlockSpec((1, tracers, rim, width), lambda g: (g, 0, 0, 0)),
-            pl.BlockSpec((1, tracers, rim, width), lambda g: (g, 0, 0, 0)),
-            pl.BlockSpec(stencil.shape, lambda g: (0, 0, 0)),
-            pl.BlockSpec(slopes.shape, lambda g: (0, 0, 0, 0)),
-            pl.BlockSpec((1,) + seeds.shape[1:], lambda g: (g, 0, 0)),
+            pl.BlockSpec((1, tracers, local, sub, lanes), lambda g: (g, 0, 0, 0, 0)),
+            pl.BlockSpec((1, tracers, rim, sub, lanes), lambda g: (g, 0, 0, 0, 0)),
+            pl.BlockSpec((1, tracers, rim, sub, lanes), lambda g: (g, 0, 0, 0, 0)),
+            pl.BlockSpec(stencil.shape, lambda g: (0, 0, 0, 0)),
+            pl.BlockSpec(slopes.shape, lambda g: (0, 0, 0, 0, 0)),
+            pl.BlockSpec((1,) + seeds.shape[1:], lambda g: (g, 0, 0, 0)),
         ],
-        out_specs=pl.BlockSpec((1, tracers, local, width), lambda g: (g, 0, 0, 0)),
+        out_specs=pl.BlockSpec((1, tracers, local, sub, lanes), lambda g: (g, 0, 0, 0, 0)),
         scratch_shapes=[
-            pltpu.VMEM((tracers, SPAN, width), jnp.float32),
-            pltpu.VMEM((tracers, SPAN, width), jnp.float32),
+            pltpu.VMEM((tracers, span, sub, lanes), jnp.float32),
+            pltpu.VMEM((tracers, span, sub, lanes), jnp.float32),
         ],
     )(center, west, east, stencil, slopes, seeds)
+
+
+def as_tiles(source):
+    return source.reshape(source.shape[:-1] + (source.shape[-1] // 128, 128))
 
 
 def staged(
@@ -290,29 +293,49 @@
     _, slopes_second = surface_slopes(
         following[0, :, :ROWS], following[1, :, :ROWS], piston_inner, sea_inner
     )
-    west, east = halves(adjoint_in, "tile", 2, rim_depth)
-    first = ORIGIN - rim_depth
-    stencil = jnp.stack(
-        [
-            placed_rows(weights[0], first - 1),
-            placed_rows(weights[1], first),
-            placed_rows(weights[2], first + 1),
-            placed_rows(weights[3], first + 2),
-            placed_rows(row_weight, first),
-            placed_rows(level_weight, first),
-        ]
-    )
-    slopes = lanes_to(
+    west, east = halves(as_tiles(adjoint_in), "tile", 2, rim_depth)
+    span = adjoint_in.shape[2] + 2 * rim_depth
+
+    def along(source, lead):
+        pad = [(0, 0)] * source.ndim
+        pad[0] = (lead, span - lead - source.shape[0])
+        return jnp.pad(source, pad)
+
+    def cells_of(source):
+        pad = [(0, 0)] * source.ndim
+        pad[-1] = (0, cell_count - source.shape[-1])
+        return jnp.pad(source, pad)
+
+    wide = weights.shape[1]
+    stencil = as_tiles(
         jnp.stack(
             [
-                placed_rows(slopes_second, ORIGIN - inner_rim),
-                placed_rows(trim_rim(slopes_first, 0, inner_rim, 1), ORIGIN),
+                along(weights[0][1:], 0),
+                weights[1],
+                along(weights[2][: wide - 1], 1),
+                along(weights[3][: wide - 2], 2),
+                row_weight,
+                backward_shift(row_weight, 1),
+                level_weight,
+                backward_shift(level_weight, ROWS),
             ]
-        ),
-        128,
-    )
-    seeds = lanes_to(placed_rows(objective_seeds, first), 128)
-    return two_retreats(adjoint_in, west, east, stencil, slopes, seeds)
+        )
+    )
+    second = jnp.moveaxis(slopes_second, 1, 0)
+    first_slopes = jnp.moveaxis(trim_rim(slopes_first, 0, inner_rim, 1), 1, 0)
+    slopes = as_tiles(
+        cells_of(
+            jnp.stack(
+                [
+                    jnp.moveaxis(along(second, inner_rim), 0, 1),
+                    jnp.moveaxis(along(first_slopes, rim_depth), 0, 1),
+                ]
+            )
+        )
+    )
+    seeds = as_tiles(cells_of(objective_seeds))
+    out = two_retreats(as_tiles(adjoint_in), west, east, stencil, slopes, seeds)
+    return out.reshape(adjoint_in.shape)
 
 
 def solution(mesh):

time: 72.9 us -> 72.9 us (level)
  local copies, waits for them, and re-layouts: 6.5 us -> 11.7 us
  Pallas kernels: 17 us -> 13.3 us
    unnamed x13 -> x35, local copies, waits for them, and re-layouts: 1.67 us -> 5.78 us
    pallas_call x1, Pallas kernels: 17 us -> 13.3 us  [two_retreats(): pl.pallas_call(retreat_kernel, out_shape=jax.ShapeDtypeStruct(center.shap...]
    reshape x0 -> x1, local copies, waits for them, and re-layouts: none -> 2.7 us  [staged(): return out.reshape(adjoint_in.shape)]
    slice x1, local copies, waits for them, and re-layouts: 2.57 us -> 0.95 us  [halves(): head = lax.slice_in_dim(cells, 0, width, axis=dim)]
  transfers between devices with their start and end apart: 12 -> 12, of which waited for: 2 -> 2; matrix products, arithmetic and copies ran while one was open for 7% -> 10% of each run, Pallas kernels for 0% -> 0%
where the time goes in v6:
time: 72.9 us; the launch traced here: 72.3 us
  starting transfers between devices  23 us (32%)
  waiting for transfers between devices  20.5 us (28%)
  Pallas kernels  13.3 us (18%)
  local copies, waits for them, and re-layouts  11.7 us (16%)
  other arithmetic  2.73 us (4%)
  between operations  1.14 us (2%)
    ppermute x1, waiting for transfers between devices, halves(): lax.ppermute(head, axis, [((i + 1) % count, i) for i in range(count)])  19.6 us
    pallas_call x1, Pallas kernels, two_retreats(): pl.pallas_call(retreat_kernel, out_shape=jax.ShapeDtypeStruct(center.shap...  13.3 us
    ppermute x7, starting transfers between devices, spread(): moved = lax.ppermute(value, axis, [(i, i ^ mask) for i in range(count)])  10.1 us
    unnamed x35, local copies, waits for them, and re-layouts  5.78 us
    ppermute x1, starting transfers between devices, padded(): lax.ppermute(head, axis, [((i + 1) % count, i) for i in range(count)])  5.3 us
    ppermute x1, starting transfers between devices, halves(): lax.ppermute(head, axis, [((i + 1) % count, i) for i in range(count)])  2.99 us
    reshape x1, local copies, waits for them, and re-layouts, staged(): return out.reshape(adjoint_in.shape)  2.7 us
    ppermute x1, starting transfers between devices, spread(): moved = lax.ppermute(value, axis, [(i, i ^ top) for i in range(count)])  2.53 us
  transfers between devices with their start and end apart: 12, of which 2 were waited for; matrix products, arithmetic and copies ran while one was open for 10% of the time, Pallas kernels for 0%

profile of v6, /device:TPU:1, one launch (start us, length us, event | category | flops | bytes accessed | tf_op | source)
XLA Modules:
  0.0 72.3 jit_solution(150454935806482359)
XLA Ops:
  0.7 0.7 convert_element_type.37
  1.4 0.8 %convert_element_type.36 = f32[16,1024]{1,0:T(8,128)S(1)} convert(s32[16,1024]{1,0:T(8,128)} %param.12) | non-fusion elementwise | flops 16384 | bytes 131072 | tf_op jit(solution)/shard_map/convert_element_type | solution.py:248
  2.3 1.0 %concatenate.37 = f32[16,3296]{1,0:T(8,128)S(1)} concatenate(f32[16,64]{1,0:T(8,128)S(1)} %get-tuple-element.39, f32[16,64]{1,0:T(8,128)S(1)} %get-tuple-element.38, f32[16,1024]{1,0:T(8,128)S(1)} %convert_element_type.36, f32[16,1024]{1,0:T(8,128)} %param.13, f32[16,1024]{1,0:T(8,128)} %param.14, f32[16,32]{1,0:T(8,128)} %param.15, f32[16,32]{1,0:T(8,128)} %param.16, ...), dimensions={1} | concatenate | bytes 421888 | tf_op jit(solution)/shard_map/concatenate | solution.py:244
  3.3 0.6 fusion.52
  3.9 2.0 %collective-permute-start.2 = (f32[4,3296]{1,0:T(4,128)}, f32[4,3296]{1,0:T(4,128)S(1)}, u32[]{:S(2)}, u32[]{:S(2)}) collective-permute-start(f32[4,3296]{1,0:T(4,128)} %get-tuple-element.36), channel_id=1, source_target_pairs={{0,16},{16,32},{32,48},{48,64},{64,80},{80,96},{96,112},{112,128},... | collective-permute-start | bytes 158216 | tf_op jit(solution)/shard_map/ppermute | solution.py:29
  5.9 5.3 %collective-permute-start.3 = (f32[4,3296]{1,0:T(4,128)S(1)}, f32[4,3296]{1,0:T(4,128)S(1)}, u32[]{:S(2)}, u32[]{:S(2)}) collective-permute-start(f32[4,3296]{1,0:T(4,128)S(1)} %get-tuple-element.37), channel_id=1, source_target_pairs={{16,0},{32,16},{48,32},{64,48},{80,64},{96,80},{112,96},{128,112},... | collective-permute-start | bytes 158216 | tf_op jit(solution)/shard_map/ppermute | solution.py:31
  11.2 2.1 %copy.10 = f32[64,8,8,128]{3,2,1,0:T(8,128)S(1)} copy(f32[64,8,8,128]{3,1,2,0:T(8,128)} %bitcast.414) | data formatting | bytes 4194304
  13.3 0.9 %fusion.51 = (f32[16,2,4,8,128]{4,3,2,1,0:T(8,128)}, f32[16,2,4,8,128]{4,3,2,1,0:T(8,128)S(1)}) fusion(f32[16,2,16,8,128]{4,3,2,1,0:T(8,128)S(1)} %bitcast.410), kind=kLoop, calls=%fused_computation.204 | loop fusion | bytes 2097152 | tf_op jit(solution)/shard_map/slice | solution.py:145
  14.6 2.5 %collective-permute-start.4 = (f32[2,24,64]{2,1,0:T(8,128)S(1)}, f32[2,24,64]{2,1,0:T(8,128)S(1)}, u32[]{:S(2)}, u32[]{:S(2)}) collective-permute-start(f32[2,24,64]{2,1,0:T(8,128)S(1)} %pad_maximum_fusion.1), channel_id=1, source_target_pairs={{0,8},{1,9},{2,10},{3,11},{4,12},{5,13},{6,14},{7,15},{8,0},{9,1},... | collective-permute-start | bytes 36872 | tf_op jit(solution)/shard_map/ppermute | solution.py:45
  18.0 0.8 %collective-permute-done.4 = f32[2,24,64]{2,1,0:T(8,128)S(1)} collective-permute-done((f32[2,24,64]{2,1,0:T(8,128)S(1)}, f32[2,24,64]{2,1,0:T(8,128)S(1)}, u32[]{:S(2)}, u32[]{:S(2)}) %collective-permute-start.4) | collective-permute-done | bytes 12320 | tf_op jit(solution)/shard_map/ppermute | solution.py:45
  18.9 2.1 %collective-permute-start.11 = (f32[2,24,64]{2,1,0:T(8,128)S(1)}, f32[2,24,64]{2,1,0:T(8,128)S(1)}, u32[]{:S(2)}, u32[]{:S(2)}) collective-permute-start(f32[2,24,64]{2,1,0:T(8,128)S(1)} %broadcast_select_fusion), channel_id=1, source_target_pairs={{0,1},{1,0},{2,3},{3,2},{4,5},{5,4},{6,7},{7,6},{8,9},{9,8},{10,11... | collective-permute-start | bytes 36872 | tf_op jit(solution)/shard_map/ppermute | solution.py:50
  21.0 1.3 %collective-permute-start.10 = (f32[2,24,64]{2,1,0:T(8,128)S(1)}, f32[2,24,64]{2,1,0:T(8,128)S(1)}, u32[]{:S(2)}, u32[]{:S(2)}) collective-permute-start(f32[2,24,64]{2,1,0:T(8,128)S(1)} %broadcast_select_fusion), channel_id=1, source_target_pairs={{0,2},{1,3},{2,0},{3,1},{4,6},{5,7},{6,4},{7,5},{8,10},{9,11},{10,... | collective-permute-start | bytes 36872 | tf_op jit(solution)/shard_map/ppermute | solution.py:50
  22.3 0.5 collective-permute-start.9
  22.8 2.9 %collective-permute-start.8 = (f32[2,24,64]{2,1,0:T(8,128)S(1)}, f32[2,24,64]{2,1,0:T(8,128)S(1)}, u32[]{:S(2)}, u32[]{:S(2)}) collective-permute-start(f32[2,24,64]{2,1,0:T(8,128)S(1)} %broadcast_select_fusion), channel_id=1, source_target_pairs={{0,4},{1,5},{2,6},{3,7},{4,0},{5,1},{6,2},{7,3},{8,12},{9,13},{10,... | collective-permute-start | bytes 36872 | tf_op jit(solution)/shard_map/ppermute | solution.py:50
  25.8 0.4 collective-permute-start.7
  26.1 2.7 %collective-permute-start.6 = (f32[2,24,64]{2,1,0:T(8,128)S(1)}, f32[2,24,64]{2,1,0:T(8,128)S(1)}, u32[]{:S(2)}, u32[]{:S(2)}) collective-permute-start(f32[2,24,64]{2,1,0:T(8,128)S(1)} %broadcast_select_fusion), channel_id=1, source_target_pairs={{0,6},{1,7},{2,4},{3,5},{4,2},{5,3},{6,0},{7,1},{8,14},{9,15},{10,... | collective-permute-start | bytes 36872 | tf_op jit(solution)/shard_map/ppermute | solution.py:50
  29.3 1.5 %copy.20 = f32[48,8,8,128]{3,2,1,0:T(8,128)} copy(f32[48,8,8,128]{3,1,2,0:T(8,128)S(1)} %bitcast.412) | data formatting | bytes 3145728
  30.8 3.0 %collective-permute-start.1 = (f32[16,2,4,8,128]{4,3,2,1,0:T(8,128)S(1)}, f32[16,2,4,8,128]{4,3,2,1,0:T(8,128)S(1)}, u32[]{:S(2)}, u32[]{:S(2)}) collective-permute-start(f32[16,2,4,8,128]{4,3,2,1,0:T(8,128)S(1)} %copy-done.3), channel_id=1, source_target_pairs={{16,0},{32,16},{48,32},{64,48},{80,64},{96,80},{112,96},{128,112},... | collective-permute-start | bytes 1572872 | tf_op jit(solution)/shard_map/ppermute | solution.py:148
  34.4 0.3 add_bitcast_fusion.3
  34.9 0.8 %copy.19 = f32[12,8,8,128]{3,2,1,0:T(8,128)} copy(f32[12,8,8,128]{3,1,2,0:T(8,128)S(1)} %bitcast.416) | data formatting | bytes 786432
  35.7 19.6 %collective-permute-done.1.east_ref = f32[16,2,4,8,128]{4,3,2,1,0:T(8,128)S(1)} collective-permute-done((f32[16,2,4,8,128]{4,3,2,1,0:T(8,128)S(1)}, f32[16,2,4,8,128]{4,3,2,1,0:T(8,128)S(1)}, u32[]{:S(2)}, u32[]{:S(2)}) %collective-permute-start.1) | collective-permute-done | bytes 524320 | tf_op jit(solution)/shard_map/ppermute | solution.py:148
  55.3 0.8 %copy-done.4 = f32[16,2,4,8,128]{4,3,2,1,0:T(8,128)} copy-done((f32[16,2,4,8,128]{4,3,2,1,0:T(8,128)}, f32[16,2,4,8,128]{4,3,2,1,0:T(8,128)S(1)}, u32[]{:S(2)}) %copy-start.4) | copy-done | bytes 524312
  56.3 13.3 %shard_map.91 = f32[16,2,16,8,128]{4,3,2,1,0:T(8,128)} custom-call(f32[16,2,16,8,128]{4,3,2,1,0:T(8,128)} %bitcast.411, f32[16,2,4,8,128]{4,3,2,1,0:T(8,128)} %copy-done.5, f32[16,2,4,8,128]{4,3,2,1,0:T(8,128)} %copy-done.4, f32[8,24,8,128]{3,2,1,0:T(8,128)} %copy-done.2, f32[2,2,24,8,128]{4,3,2,1,0:T(8,128)} %bitcast.415, f32[16,24,8,128]{3,2,1,0:T(8,128)} %bitcast.413), custom_call_target="tpu_custom_call" | custom-call | tf_op jit(solution)/shard_map/pallas_call | solution.py:210
  69.6 2.7 %reshape.68 = f32[16,2,16,1024]{3,2,1,0:T(8,128)} reshape(f32[16,2,16,8,128]{4,3,2,1,0:T(8,128)} %shard_map.91) | data formatting | bytes 4194304 | tf_op jit(solution)/shard_map/reshape | solution.py:338
  (82 shorter events, 2.4 us)
Async XLA Ops:
  0.0 2.3 %copy-start = (f32[4,2,16,1024]{3,2,1,0:T(8,128)S(1)}, f32[4,2,16,1024]{3,2,1,0:T(8,128)}, u32[]{:S(2)}) copy-start(f32[4,2,16,1024]{3,2,1,0:T(8,128)} %param.10) | copy-start | bytes 1572868
  3.9 10.4 %collective-permute-start.2 = (f32[4,3296]{1,0:T(4,128)}, f32[4,3296]{1,0:T(4,128)S(1)}, u32[]{:S(2)}, u32[]{:S(2)}) collective-permute-start(f32[4,3296]{1,0:T(4,128)} %get-tuple-element.36), channel_id=1, source_target_pairs={{0,16},{16,32},{32,48},{48,64},{64,80},{80,96},{96,112},{112,128},... | collective-permute-start | bytes 158216 | tf_op jit(solution)/shard_map/ppermute | solution.py:29
  5.9 8.3 %collective-permute-start.3 = (f32[4,3296]{1,0:T(4,128)S(1)}, f32[4,3296]{1,0:T(4,128)S(1)}, u32[]{:S(2)}, u32[]{:S(2)}) collective-permute-start(f32[4,3296]{1,0:T(4,128)S(1)} %get-tuple-element.37), channel_id=1, source_target_pairs={{16,0},{32,16},{48,32},{64,48},{80,64},{96,80},{112,96},{128,112},... | collective-permute-start | bytes 158216 | tf_op jit(solution)/shard_map/ppermute | solution.py:31
  13.3 3.9 %copy-start.1 = (f32[64,8,8,128]{3,2,1,0:T(8,128)}, f32[64,8,8,128]{3,2,1,0:T(8,128)S(1)}, u32[]{:S(2)}) copy-start(f32[64,8,8,128]{3,2,1,0:T(8,128)S(1)} %copy.10) | copy-start | bytes 6291460
  14.6 4.3 %collective-permute-start.4 = (f32[2,24,64]{2,1,0:T(8,128)S(1)}, f32[2,24,64]{2,1,0:T(8,128)S(1)}, u32[]{:S(2)}, u32[]{:S(2)}) collective-permute-start(f32[2,24,64]{2,1,0:T(8,128)S(1)} %pad_maximum_fusion.1), channel_id=1, source_target_pairs={{0,8},{1,9},{2,10},{3,11},{4,12},{5,13},{6,14},{7,15},{8,0},{9,1},... | collective-permute-start | bytes 36872 | tf_op jit(solution)/shard_map/ppermute | solution.py:45
  18.9 7.2 %collective-permute-start.11 = (f32[2,24,64]{2,1,0:T(8,128)S(1)}, f32[2,24,64]{2,1,0:T(8,128)S(1)}, u32[]{:S(2)}, u32[]{:S(2)}) collective-permute-start(f32[2,24,64]{2,1,0:T(8,128)S(1)} %broadcast_select_fusion), channel_id=1, source_target_pairs={{0,1},{1,0},{2,3},{3,2},{4,5},{5,4},{6,7},{7,6},{8,9},{9,8},{10,11... | collective-permute-start | bytes 36872 | tf_op jit(solution)/shard_map/ppermute | solution.py:50
  21.0 7.9 %collective-permute-start.10 = (f32[2,24,64]{2,1,0:T(8,128)S(1)}, f32[2,24,64]{2,1,0:T(8,128)S(1)}, u32[]{:S(2)}, u32[]{:S(2)}) collective-permute-start(f32[2,24,64]{2,1,0:T(8,128)S(1)} %broadcast_select_fusion), channel_id=1, source_target_pairs={{0,2},{1,3},{2,0},{3,1},{4,6},{5,7},{6,4},{7,5},{8,10},{9,11},{10,... | collective-permute-start | bytes 36872 | tf_op jit(solution)/shard_map/ppermute | solution.py:50
  22.3 8.5 %collective-permute-start.9 = (f32[2,24,64]{2,1,0:T(8,128)S(1)}, f32[2,24,64]{2,1,0:T(8,128)S(1)}, u32[]{:S(2)}, u32[]{:S(2)}) collective-permute-start(f32[2,24,64]{2,1,0:T(8,128)S(1)} %broadcast_select_fusion), channel_id=1, source_target_pairs={{0,3},{1,2},{2,1},{3,0},{4,7},{5,6},{6,5},{7,4},{8,11},{9,10},{10,... | collective-permute-start | bytes 36872 | tf_op jit(solution)/shard_map/ppermute | solution.py:50
  22.8 10.9 %collective-permute-start.8 = (f32[2,24,64]{2,1,0:T(8,128)S(1)}, f32[2,24,64]{2,1,0:T(8,128)S(1)}, u32[]{:S(2)}, u32[]{:S(2)}) collective-permute-start(f32[2,24,64]{2,1,0:T(8,128)S(1)} %broadcast_select_fusion), channel_id=1, source_target_pairs={{0,4},{1,5},{2,6},{3,7},{4,0},{5,1},{6,2},{7,3},{8,12},{9,13},{10,... | collective-permute-start | bytes 36872 | tf_op jit(solution)/shard_map/ppermute | solution.py:50
  25.8 8.0 %collective-permute-start.7 = (f32[2,24,64]{2,1,0:T(8,128)S(1)}, f32[2,24,64]{2,1,0:T(8,128)S(1)}, u32[]{:S(2)}, u32[]{:S(2)}) collective-permute-start(f32[2,24,64]{2,1,0:T(8,128)S(1)} %broadcast_select_fusion), channel_id=1, source_target_pairs={{0,5},{1,4},{2,7},{3,6},{4,1},{5,0},{6,3},{7,2},{8,13},{9,12},{10,... | collective-permute-start | bytes 36872 | tf_op jit(solution)/shard_map/ppermute | solution.py:50
  26.1 7.7 %collective-permute-start.6 = (f32[2,24,64]{2,1,0:T(8,128)S(1)}, f32[2,24,64]{2,1,0:T(8,128)S(1)}, u32[]{:S(2)}, u32[]{:S(2)}) collective-permute-start(f32[2,24,64]{2,1,0:T(8,128)S(1)} %broadcast_select_fusion), channel_id=1, source_target_pairs={{0,6},{1,7},{2,4},{3,5},{4,2},{5,3},{6,0},{7,1},{8,14},{9,15},{10,... | collective-permute-start | bytes 36872 | tf_op jit(solution)/shard_map/ppermute | solution.py:50
  28.9 5.0 %collective-permute-start.5 = (f32[2,24,64]{2,1,0:T(8,128)S(1)}, f32[2,24,64]{2,1,0:T(8,128)S(1)}, u32[]{:S(2)}, u32[]{:S(2)}) collective-permute-start(f32[2,24,64]{2,1,0:T(8,128)S(1)} %broadcast_select_fusion), channel_id=1, source_target_pairs={{0,7},{1,6},{2,5},{3,4},{4,3},{5,2},{6,1},{7,0},{8,15},{9,14},{10,... | collective-permute-start | bytes 36872 | tf_op jit(solution)/shard_map/ppermute | solution.py:50
  29.1 1.7 %copy-start.2 = (f32[8,24,8,128]{3,2,1,0:T(8,128)}, f32[8,24,8,128]{3,2,1,0:T(8,128)S(1)}, u32[]{:S(2)}) copy-start(f32[8,24,8,128]{3,2,1,0:T(8,128)S(1)} %bitcast_dynamic-update-slice_fusion.w_ref) | copy-start | bytes 2359300
  29.1 1.7 %copy-start.3 = (f32[16,2,4,8,128]{4,3,2,1,0:T(8,128)S(1)}, f32[16,2,4,8,128]{4,3,2,1,0:T(8,128)}, u32[]{:S(2)}) copy-start(f32[16,2,4,8,128]{4,3,2,1,0:T(8,128)} %get-tuple-element.24) | copy-start | bytes 1572868
  30.8 24.5 %collective-permute-start.1 = (f32[16,2,4,8,128]{4,3,2,1,0:T(8,128)S(1)}, f32[16,2,4,8,128]{4,3,2,1,0:T(8,128)S(1)}, u32[]{:S(2)}, u32[]{:S(2)}) collective-permute-start(f32[16,2,4,8,128]{4,3,2,1,0:T(8,128)S(1)} %copy-done.3), channel_id=1, source_target_pairs={{16,0},{32,16},{48,32},{64,48},{80,64},{96,80},{112,96},{128,112},... | collective-permute-start | bytes 1572872 | tf_op jit(solution)/shard_map/ppermute | solution.py:148
  33.8 21.5 %collective-permute-start = (f32[16,2,4,8,128]{4,3,2,1,0:T(8,128)S(1)}, f32[16,2,4,8,128]{4,3,2,1,0:T(8,128)S(1)}, u32[]{:S(2)}, u32[]{:S(2)}) collective-permute-start(f32[16,2,4,8,128]{4,3,2,1,0:T(8,128)S(1)} %get-tuple-element.25), channel_id=1, source_target_pairs={{0,16},{16,32},{32,48},{48,64},{64,80},{80,96},{96,112},{112,128},... | collective-permute-start | bytes 1572872 | tf_op jit(solution)/shard_map/ppermute | solution.py:147
  55.3 0.8 %copy-start.4 = (f32[16,2,4,8,128]{4,3,2,1,0:T(8,128)}, f32[16,2,4,8,128]{4,3,2,1,0:T(8,128)S(1)}, u32[]{:S(2)}) copy-start(f32[16,2,4,8,128]{4,3,2,1,0:T(8,128)S(1)} %collective-permute-done.1.east_ref) | copy-start | bytes 1572868
  55.3 1.0 %copy-start.5 = (f32[16,2,4,8,128]{4,3,2,1,0:T(8,128)}, f32[16,2,4,8,128]{4,3,2,1,0:T(8,128)S(1)}, u32[]{:S(2)}) copy-start(f32[16,2,4,8,128]{4,3,2,1,0:T(8,128)S(1)} %collective-permute-done.west_ref) | copy-start | bytes 1572868

commit v7 on v6

--- a/solution.py
+++ b/solution.py
@@ -159,72 +159,115 @@
     return jnp.where(lane < step, carried, turned)
 
 
-def retreat_kernel(center_ref, west_ref, east_ref, w_ref, s_ref, seed_ref, out_ref, e_ref, f_ref):
-    tracers = center_ref.shape[1]
+def stencil_step(src, k, stage, shift, w_ref, s_ref, seed_ref, lane):
+    w = [w_ref[m, k + shift] for m in range(8)]
+    results = []
+    for t in range(src.shape[0]):
+        x_0 = src[t, k]
+        zonal = (
+            w[0] * (src[t, k + 2] - src[t, k + 1])
+            + w[1] * (src[t, k + 1] - x_0)
+            + w[2] * (x_0 - src[t, k - 1])
+            + w[3] * (src[t, k - 1] - src[t, k - 2])
+        )
+        mix = (
+            w[4] * (cell_shift(x_0, 1, lane, True) - x_0)
+            - w[5] * (x_0 - cell_shift(x_0, 1, lane, False))
+            + w[6] * (cell_shift(x_0, ROWS, lane, True) - x_0)
+            - w[7] * (x_0 - cell_shift(x_0, ROWS, lane, False))
+        )
+        forcing = src[0, k] + seed_ref[0, k + shift]
+        results.append(x_0 + zonal + mix + s_ref[stage, t, k + shift] * forcing)
+    return results
+
+
+def run_steps(e_ref, f_ref, out_ref, first_rows, second_rows, shift, out_start, refs):
+    w_ref, s_ref, seed_ref = refs
+    lane = lax.broadcasted_iota(jnp.int32, (8, 128), 1)
+    for k in first_rows:
+        for t, value in enumerate(stencil_step(e_ref, k, 0, shift, w_ref, s_ref, seed_ref, lane)):
+            f_ref[t, k] = value
+    for k in second_rows:
+        for t, value in enumerate(stencil_step(f_ref, k, 1, shift, w_ref, s_ref, seed_ref, lane)):
+            out_ref[0, t, k - out_start] = value
+
+
+def interior_kernel(center_ref, w_ref, s_ref, seed_ref, out_ref, e_ref, f_ref):
+    local = center_ref.shape[2]
+    rim = (w_ref.shape[1] - local) // 2
+    e_ref[...] = center_ref[0]
+    run_steps(
+        e_ref, f_ref, out_ref, range(2, local - 2), range(rim, local - rim), rim, 0,
+        (w_ref, s_ref, seed_ref),
+    )
+
+
+def edge_kernel(center_ref, west_ref, east_ref, w_ref, s_ref, seed_ref, done_ref, out_ref, e_ref, f_ref):
+    del done_ref
     local = center_ref.shape[2]
     rim = west_ref.shape[2]
-    lane = lax.broadcasted_iota(jnp.int32, (8, 128), 1)
-    e_ref[:, rim : rim + local] = center_ref[0]
-    e_ref[:, 0:rim] = west_ref[0]
-    e_ref[:, rim + local : 2 * rim + local] = east_ref[0]
-
-    def step(src, k, stage):
-        w = [w_ref[m, k] for m in range(8)]
-        results = []
-        for t in range(tracers):
-            x_0 = src[t, k]
-            zonal = (
-                w[0] * (src[t, k + 2] - src[t, k + 1])
-                + w[1] * (src[t, k + 1] - x_0)
-                + w[2] * (x_0 - src[t, k - 1])
-                + w[3] * (src[t, k - 1] - src[t, k - 2])
-            )
-            mix = (
-                w[4] * (cell_shift(x_0, 1, lane, True) - x_0)
-                - w[5] * (x_0 - cell_shift(x_0, 1, lane, False))
-                + w[6] * (cell_shift(x_0, ROWS, lane, True) - x_0)
-                - w[7] * (x_0 - cell_shift(x_0, ROWS, lane, False))
-            )
-            forcing = src[0, k] + seed_ref[0, k]
-            results.append(x_0 + zonal + mix + s_ref[stage, t, k] * forcing)
-        return results
-
-    def first(k, carry):
-        for t, value in enumerate(step(e_ref, k, 0)):
-            f_ref[t, k] = value
-        return carry
-
-    def second(k, carry):
-        for t, value in enumerate(step(f_ref, k, 1)):
-            out_ref[0, t, k - rim] = value
-        return carry
-
-    lax.fori_loop(2, 2 * rim + local - 2, first, 0, unroll=True)
-    lax.fori_loop(rim, rim + local, second, 0, unroll=True)
+    side = pl.program_id(1)
+
+    @pl.when(side == 0)
+    def _():
+        e_ref[:, 0:rim] = west_ref[0]
+        e_ref[:, rim : 3 * rim] = center_ref[0, :, 0 : 2 * rim]
+        run_steps(
+            e_ref, f_ref, out_ref, range(2, 3 * rim - 2), range(rim, 2 * rim), 0, rim,
+            (w_ref, s_ref, seed_ref),
+        )
+
+    @pl.when(side == 1)
+    def _():
+        e_ref[:, 0 : 2 * rim] = center_ref[0, :, local - 2 * rim : local]
+        e_ref[:, 2 * rim : 3 * rim] = east_ref[0]
+        run_steps(
+            e_ref, f_ref, out_ref, range(2, 3 * rim - 2), range(rim, 2 * rim), local - rim, rim,
+            (w_ref, s_ref, seed_ref),
+        )
 
 
 def two_retreats(center, west, east, stencil, slopes, seeds):
     groups, tracers, local, sub, lanes = center.shape
     rim = west.shape[2]
-    span = local + 2 * rim
-    return pl.pallas_call(
-        retreat_kernel,
+    tile = (sub, lanes)
+    whole = (1, tracers, local) + tile
+    shared = [
+        pl.BlockSpec(stencil.shape, lambda *g: (0, 0, 0, 0)),
+        pl.BlockSpec(slopes.shape, lambda *g: (0, 0, 0, 0, 0)),
+        pl.BlockSpec((1,) + seeds.shape[1:], lambda g, *e: (g, 0, 0, 0)),
+    ]
+    inner = pl.pallas_call(
+        interior_kernel,
         out_shape=jax.ShapeDtypeStruct(center.shape, center.dtype),
         grid=(groups,),
+        in_specs=[pl.BlockSpec(whole, lambda g: (g, 0, 0, 0, 0))] + shared,
+        out_specs=pl.BlockSpec(whole, lambda g: (g, 0, 0, 0, 0)),
+        scratch_shapes=[
+            pltpu.VMEM((tracers, local) + tile, jnp.float32),
+            pltpu.VMEM((tracers, local) + tile, jnp.float32),
+        ],
+    )(center, stencil, slopes, seeds)
+    edge = (1, tracers, rim) + tile
+    last = local // rim - 1
+    return pl.pallas_call(
+        edge_kernel,
+        out_shape=jax.ShapeDtypeStruct(center.shape, center.dtype),
+        grid=(groups, 2),
         in_specs=[
-            pl.BlockSpec((1, tracers, local, sub, lanes), lambda g: (g, 0, 0, 0, 0)),
-            pl.BlockSpec((1, tracers, rim, sub, lanes), lambda g: (g, 0, 0, 0, 0)),
-            pl.BlockSpec((1, tracers, rim, sub, lanes), lambda g: (g, 0, 0, 0, 0)),
-            pl.BlockSpec(stencil.shape, lambda g: (0, 0, 0, 0)),
-            pl.BlockSpec(slopes.shape, lambda g: (0, 0, 0, 0, 0)),
-            pl.BlockSpec((1,) + seeds.shape[1:], lambda g: (g, 0, 0, 0)),
+            pl.BlockSpec(whole, lambda g, e: (g, 0, 0, 0, 0)),
+            pl.BlockSpec(edge, lambda g, e: (g, 0, 0, 0, 0)),
+            pl.BlockSpec(edge, lambda g, e: (g, 0, 0, 0, 0)),
+        ]
+        + shared
+        + [pl.BlockSpec(memory_space=pl.ANY)],
+        out_specs=pl.BlockSpec(edge, lambda g, e: (g, 0, e * last, 0, 0)),
+        scratch_shapes=[
+            pltpu.VMEM((tracers, 3 * rim) + tile, jnp.float32),
+            pltpu.VMEM((tracers, 3 * rim) + tile, jnp.float32),
         ],
-        out_specs=pl.BlockSpec((1, tracers, local, sub, lanes), lambda g: (g, 0, 0, 0, 0)),
-        scratch_shapes=[
-            pltpu.VMEM((tracers, span, sub, lanes), jnp.float32),
-            pltpu.VMEM((tracers, span, sub, lanes), jnp.float32),
-        ],
-    )(center, west, east, stencil, slopes, seeds)
+        input_output_aliases={6: 0},
+    )(center, west, east, stencil, slopes, seeds, inner)
 
 
 def as_tiles(source):

time: 72.9 us -> 81.8 us (1.12)
  Pallas kernels: 13.3 us -> 33.2 us
  waiting for transfers between devices: 20.5 us -> 8.46 us
    pallas_call x1 -> x2, Pallas kernels: 13.3 us -> 33.2 us  [the longest x1 21.2 us: two_retreats(): pl.pallas_call(edge_kernel, out_shape=jax.ShapeDtypeStruct(center.shape,...]
    ppermute x1, waiting for transfers between devices: 19.6 us -> 7.6 us  [halves(): lax.ppermute(head, axis, [((i + 1) % count, i) for i in range(count)])]
  transfers between devices with their start and end apart: 12 -> 12, of which waited for: 2 -> 2; matrix products, arithmetic and copies ran while one was open for 10% -> 9% of each run, Pallas kernels for 0% -> 15%
where the time goes in v7:
time: 81.8 us; the launch traced here: 80.8 us
  Pallas kernels  33.2 us (41%)
  starting transfers between devices  23 us (28%)
  local copies, waits for them, and re-layouts  12.3 us (15%)
  waiting for transfers between devices  8.46 us (10%)
  other arithmetic  2.73 us (3%)
  between operations  1.15 us (1%)
    pallas_call x1, Pallas kernels, two_retreats(): pl.pallas_call(edge_kernel, out_shape=jax.ShapeDtypeStruct(center.shape,...  21.2 us
    pallas_call x1, Pallas kernels, two_retreats(): pl.pallas_call(interior_kernel, out_shape=jax.ShapeDtypeStruct(center.sha...  12 us
    ppermute x7, starting transfers between devices, spread(): moved = lax.ppermute(value, axis, [(i, i ^ mask) for i in range(count)])  10.1 us
    ppermute x1, waiting for transfers between devices, halves(): lax.ppermute(head, axis, [((i + 1) % count, i) for i in range(count)])  7.6 us
    unnamed x35, local copies, waits for them, and re-layouts  6.42 us
    ppermute x1, starting transfers between devices, padded(): lax.ppermute(head, axis, [((i + 1) % count, i) for i in range(count)])  5.3 us
    ppermute x1, starting transfers between devices, halves(): lax.ppermute(head, axis, [((i + 1) % count, i) for i in range(count)])  2.99 us
    reshape x1, local copies, waits for them, and re-layouts, staged(): return out.reshape(adjoint_in.shape)  2.7 us
  transfers between devices with their start and end apart: 12, of which 2 were waited for; matrix products, arithmetic and copies ran while one was open for 9% of the time, Pallas kernels for 15%

profile of v7, /device:TPU:1, one launch (start us, length us, event | category | flops | bytes accessed | tf_op | source)
XLA Modules:
  0.0 80.8 jit_solution(14886400690908705712)
XLA Ops:
  0.7 0.7 convert_element_type.37
  1.4 0.8 %convert_element_type.36 = f32[16,1024]{1,0:T(8,128)S(1)} convert(s32[16,1024]{1,0:T(8,128)} %param.12) | non-fusion elementwise | flops 16384 | bytes 131072 | tf_op jit(solution)/shard_map/convert_element_type | solution.py:291
  2.3 1.0 %concatenate.37 = f32[16,3296]{1,0:T(8,128)S(1)} concatenate(f32[16,64]{1,0:T(8,128)S(1)} %get-tuple-element.39, f32[16,64]{1,0:T(8,128)S(1)} %get-tuple-element.38, f32[16,1024]{1,0:T(8,128)S(1)} %convert_element_type.36, f32[16,1024]{1,0:T(8,128)} %param.13, f32[16,1024]{1,0:T(8,128)} %param.14, f32[16,32]{1,0:T(8,128)} %param.15, f32[16,32]{1,0:T(8,128)} %param.16, ...), dimensions={1} | concatenate | bytes 421888 | tf_op jit(solution)/shard_map/concatenate | solution.py:287
  3.3 0.6 fusion.52
  3.9 2.0 %collective-permute-start.2 = (f32[4,3296]{1,0:T(4,128)}, f32[4,3296]{1,0:T(4,128)S(1)}, u32[]{:S(2)}, u32[]{:S(2)}) collective-permute-start(f32[4,3296]{1,0:T(4,128)} %get-tuple-element.36), channel_id=1, source_target_pairs={{0,16},{16,32},{32,48},{48,64},{64,80},{80,96},{96,112},{112,128},... | collective-permute-start | bytes 158216 | tf_op jit(solution)/shard_map/ppermute | solution.py:29
  5.9 5.3 %collective-permute-start.3 = (f32[4,3296]{1,0:T(4,128)S(1)}, f32[4,3296]{1,0:T(4,128)S(1)}, u32[]{:S(2)}, u32[]{:S(2)}) collective-permute-start(f32[4,3296]{1,0:T(4,128)S(1)} %get-tuple-element.37), channel_id=1, source_target_pairs={{16,0},{32,16},{48,32},{64,48},{80,64},{96,80},{112,96},{128,112},... | collective-permute-start | bytes 158216 | tf_op jit(solution)/shard_map/ppermute | solution.py:31
  11.2 2.1 %copy.11 = f32[64,8,8,128]{3,2,1,0:T(8,128)S(1)} copy(f32[64,8,8,128]{3,1,2,0:T(8,128)} %bitcast.418) | data formatting | bytes 4194304
  13.3 0.9 %fusion.51 = (f32[16,2,4,8,128]{4,3,2,1,0:T(8,128)}, f32[16,2,4,8,128]{4,3,2,1,0:T(8,128)S(1)}) fusion(f32[16,2,16,8,128]{4,3,2,1,0:T(8,128)S(1)} %bitcast.410), kind=kLoop, calls=%fused_computation.204 | loop fusion | bytes 2097152 | tf_op jit(solution)/shard_map/slice | solution.py:145
  14.6 2.5 %collective-permute-start.4 = (f32[2,24,64]{2,1,0:T(8,128)S(1)}, f32[2,24,64]{2,1,0:T(8,128)S(1)}, u32[]{:S(2)}, u32[]{:S(2)}) collective-permute-start(f32[2,24,64]{2,1,0:T(8,128)S(1)} %pad_maximum_fusion.1), channel_id=1, source_target_pairs={{0,8},{1,9},{2,10},{3,11},{4,12},{5,13},{6,14},{7,15},{8,0},{9,1},... | collective-permute-start | bytes 36872 | tf_op jit(solution)/shard_map/ppermute | solution.py:45
  18.0 0.8 %collective-permute-done.4 = f32[2,24,64]{2,1,0:T(8,128)S(1)} collective-permute-done((f32[2,24,64]{2,1,0:T(8,128)S(1)}, f32[2,24,64]{2,1,0:T(8,128)S(1)}, u32[]{:S(2)}, u32[]{:S(2)}) %collective-permute-start.4) | collective-permute-done | bytes 12320 | tf_op jit(solution)/shard_map/ppermute | solution.py:45
  18.9 2.1 %collective-permute-start.11 = (f32[2,24,64]{2,1,0:T(8,128)S(1)}, f32[2,24,64]{2,1,0:T(8,128)S(1)}, u32[]{:S(2)}, u32[]{:S(2)}) collective-permute-start(f32[2,24,64]{2,1,0:T(8,128)S(1)} %broadcast_select_fusion), channel_id=1, source_target_pairs={{0,1},{1,0},{2,3},{3,2},{4,5},{5,4},{6,7},{7,6},{8,9},{9,8},{10,11... | collective-permute-start | bytes 36872 | tf_op jit(solution)/shard_map/ppermute | solution.py:50
  21.0 1.3 %collective-permute-start.10 = (f32[2,24,64]{2,1,0:T(8,128)S(1)}, f32[2,24,64]{2,1,0:T(8,128)S(1)}, u32[]{:S(2)}, u32[]{:S(2)}) collective-permute-start(f32[2,24,64]{2,1,0:T(8,128)S(1)} %broadcast_select_fusion), channel_id=1, source_target_pairs={{0,2},{1,3},{2,0},{3,1},{4,6},{5,7},{6,4},{7,5},{8,10},{9,11},{10,... | collective-permute-start | bytes 36872 | tf_op jit(solution)/shard_map/ppermute | solution.py:50
  22.3 0.5 collective-permute-start.9
  22.8 2.9 %collective-permute-start.8 = (f32[2,24,64]{2,1,0:T(8,128)S(1)}, f32[2,24,64]{2,1,0:T(8,128)S(1)}, u32[]{:S(2)}, u32[]{:S(2)}) collective-permute-start(f32[2,24,64]{2,1,0:T(8,128)S(1)} %broadcast_select_fusion), channel_id=1, source_target_pairs={{0,4},{1,5},{2,6},{3,7},{4,0},{5,1},{6,2},{7,3},{8,12},{9,13},{10,... | collective-permute-start | bytes 36872 | tf_op jit(solution)/shard_map/ppermute | solution.py:50
  26.1 2.7 %collective-permute-start.6 = (f32[2,24,64]{2,1,0:T(8,128)S(1)}, f32[2,24,64]{2,1,0:T(8,128)S(1)}, u32[]{:S(2)}, u32[]{:S(2)}) collective-permute-start(f32[2,24,64]{2,1,0:T(8,128)S(1)} %broadcast_select_fusion), channel_id=1, source_target_pairs={{0,6},{1,7},{2,4},{3,5},{4,2},{5,3},{6,0},{7,1},{8,14},{9,15},{10,... | collective-permute-start | bytes 36872 | tf_op jit(solution)/shard_map/ppermute | solution.py:50
  29.3 1.5 %copy.21 = f32[48,8,8,128]{3,2,1,0:T(8,128)} copy(f32[48,8,8,128]{3,1,2,0:T(8,128)S(1)} %bitcast.415) | data formatting | bytes 3145728
  30.8 3.0 %collective-permute-start.1 = (f32[16,2,4,8,128]{4,3,2,1,0:T(8,128)S(1)}, f32[16,2,4,8,128]{4,3,2,1,0:T(8,128)S(1)}, u32[]{:S(2)}, u32[]{:S(2)}) collective-permute-start(f32[16,2,4,8,128]{4,3,2,1,0:T(8,128)S(1)} %copy-done.5), channel_id=1, source_target_pairs={{16,0},{32,16},{48,32},{64,48},{80,64},{96,80},{112,96},{128,112},... | collective-permute-start | bytes 1572872 | tf_op jit(solution)/shard_map/ppermute | solution.py:148
  34.9 0.8 %copy.20 = f32[12,8,8,128]{3,2,1,0:T(8,128)} copy(f32[12,8,8,128]{3,1,2,0:T(8,128)S(1)} %bitcast.419) | data formatting | bytes 786432
  35.7 12.0 %shard_map.91.done_ref = f32[16,2,16,8,128]{4,3,2,1,0:T(8,128)} custom-call(f32[16,2,16,8,128]{4,3,2,1,0:T(8,128)} %bitcast.411, f32[8,24,8,128]{3,2,1,0:T(8,128)} %copy-done.2, f32[2,2,24,8,128]{4,3,2,1,0:T(8,128)} %bitcast.416, f32[16,24,8,128]{3,2,1,0:T(8,128)} %bitcast.413), custom_call_target="tpu_custom_call" | custom-call | tf_op jit(solution)/shard_map/pallas_call | solution.py:240
  47.7 7.6 %collective-permute-done.1.east_ref = f32[16,2,4,8,128]{4,3,2,1,0:T(8,128)S(1)} collective-permute-done((f32[16,2,4,8,128]{4,3,2,1,0:T(8,128)S(1)}, f32[16,2,4,8,128]{4,3,2,1,0:T(8,128)S(1)}, u32[]{:S(2)}, u32[]{:S(2)}) %collective-permute-start.1) | collective-permute-done | bytes 524320 | tf_op jit(solution)/shard_map/ppermute | solution.py:148
  55.3 0.8 %copy-done.3 = f32[16,2,4,8,128]{4,3,2,1,0:T(8,128)} copy-done((f32[16,2,4,8,128]{4,3,2,1,0:T(8,128)}, f32[16,2,4,8,128]{4,3,2,1,0:T(8,128)S(1)}, u32[]{:S(2)}) %copy-start.3) | copy-done | bytes 524312
  56.1 0.8 copy-done.4
  56.9 21.2 %shard_map.92 = f32[16,2,16,8,128]{4,3,2,1,0:T(8,128)} custom-call(f32[16,2,16,8,128]{4,3,2,1,0:T(8,128)} %bitcast.412, f32[16,2,4,8,128]{4,3,2,1,0:T(8,128)} %copy-done.4, f32[16,2,4,8,128]{4,3,2,1,0:T(8,128)} %copy-done.3, f32[8,24,8,128]{3,2,1,0:T(8,128)} %copy-done.2, f32[2,2,24,8,128]{4,3,2,1,0:T(8,128)} %bitcast.417, ...), custom_call_target="tpu_custom_call", output_to_operand_aliasing={{}: (6, {})} | custom-call | tf_op jit(solution)/shard_map/pallas_call | solution.py:253
  78.1 2.7 %reshape.68 = f32[16,2,16,1024]{3,2,1,0:T(8,128)} reshape(f32[16,2,16,8,128]{4,3,2,1,0:T(8,128)} %shard_map.92) | data formatting | bytes 4194304 | tf_op jit(solution)/shard_map/reshape | solution.py:381
  (83 shorter events, 2.9 us)
Async XLA Ops:
  0.0 2.3 %copy-start = (f32[4,2,16,1024]{3,2,1,0:T(8,128)S(1)}, f32[4,2,16,1024]{3,2,1,0:T(8,128)}, u32[]{:S(2)}) copy-start(f32[4,2,16,1024]{3,2,1,0:T(8,128)} %param.10) | copy-start | bytes 1572868
  3.9 10.4 %collective-permute-start.2 = (f32[4,3296]{1,0:T(4,128)}, f32[4,3296]{1,0:T(4,128)S(1)}, u32[]{:S(2)}, u32[]{:S(2)}) collective-permute-start(f32[4,3296]{1,0:T(4,128)} %get-tuple-element.36), channel_id=1, source_target_pairs={{0,16},{16,32},{32,48},{48,64},{64,80},{80,96},{96,112},{112,128},... | collective-permute-start | bytes 158216 | tf_op jit(solution)/shard_map/ppermute | solution.py:29
  5.9 8.3 %collective-permute-start.3 = (f32[4,3296]{1,0:T(4,128)S(1)}, f32[4,3296]{1,0:T(4,128)S(1)}, u32[]{:S(2)}, u32[]{:S(2)}) collective-permute-start(f32[4,3296]{1,0:T(4,128)S(1)} %get-tuple-element.37), channel_id=1, source_target_pairs={{16,0},{32,16},{48,32},{64,48},{80,64},{96,80},{112,96},{128,112},... | collective-permute-start | bytes 158216 | tf_op jit(solution)/shard_map/ppermute | solution.py:31
  13.3 3.9 %copy-start.1 = (f32[64,8,8,128]{3,2,1,0:T(8,128)}, f32[64,8,8,128]{3,2,1,0:T(8,128)S(1)}, u32[]{:S(2)}) copy-start(f32[64,8,8,128]{3,2,1,0:T(8,128)S(1)} %copy.11) | copy-start | bytes 6291460
  14.6 4.3 %collective-permute-start.4 = (f32[2,24,64]{2,1,0:T(8,128)S(1)}, f32[2,24,64]{2,1,0:T(8,128)S(1)}, u32[]{:S(2)}, u32[]{:S(2)}) collective-permute-start(f32[2,24,64]{2,1,0:T(8,128)S(1)} %pad_maximum_fusion.1), channel_id=1, source_target_pairs={{0,8},{1,9},{2,10},{3,11},{4,12},{5,13},{6,14},{7,15},{8,0},{9,1},... | collective-permute-start | bytes 36872 | tf_op jit(solution)/shard_map/ppermute | solution.py:45
  18.9 7.2 %collective-permute-start.11 = (f32[2,24,64]{2,1,0:T(8,128)S(1)}, f32[2,24,64]{2,1,0:T(8,128)S(1)}, u32[]{:S(2)}, u32[]{:S(2)}) collective-permute-start(f32[2,24,64]{2,1,0:T(8,128)S(1)} %broadcast_select_fusion), channel_id=1, source_target_pairs={{0,1},{1,0},{2,3},{3,2},{4,5},{5,4},{6,7},{7,6},{8,9},{9,8},{10,11... | collective-permute-start | bytes 36872 | tf_op jit(solution)/shard_map/ppermute | solution.py:50
  21.0 7.9 %collective-permute-start.10 = (f32[2,24,64]{2,1,0:T(8,128)S(1)}, f32[2,24,64]{2,1,0:T(8,128)S(1)}, u32[]{:S(2)}, u32[]{:S(2)}) collective-permute-start(f32[2,24,64]{2,1,0:T(8,128)S(1)} %broadcast_select_fusion), channel_id=1, source_target_pairs={{0,2},{1,3},{2,0},{3,1},{4,6},{5,7},{6,4},{7,5},{8,10},{9,11},{10,... | collective-permute-start | bytes 36872 | tf_op jit(solution)/shard_map/ppermute | solution.py:50
  22.3 8.5 %collective-permute-start.9 = (f32[2,24,64]{2,1,0:T(8,128)S(1)}, f32[2,24,64]{2,1,0:T(8,128)S(1)}, u32[]{:S(2)}, u32[]{:S(2)}) collective-permute-start(f32[2,24,64]{2,1,0:T(8,128)S(1)} %broadcast_select_fusion), channel_id=1, source_target_pairs={{0,3},{1,2},{2,1},{3,0},{4,7},{5,6},{6,5},{7,4},{8,11},{9,10},{10,... | collective-permute-start | bytes 36872 | tf_op jit(solution)/shard_map/ppermute | solution.py:50
  22.8 10.9 %collective-permute-start.8 = (f32[2,24,64]{2,1,0:T(8,128)S(1)}, f32[2,24,64]{2,1,0:T(8,128)S(1)}, u32[]{:S(2)}, u32[]{:S(2)}) collective-permute-start(f32[2,24,64]{2,1,0:T(8,128)S(1)} %broadcast_select_fusion), channel_id=1, source_target_pairs={{0,4},{1,5},{2,6},{3,7},{4,0},{5,1},{6,2},{7,3},{8,12},{9,13},{10,... | collective-permute-start | bytes 36872 | tf_op jit(solution)/shard_map/ppermute | solution.py:50
  25.8 8.0 %collective-permute-start.7 = (f32[2,24,64]{2,1,0:T(8,128)S(1)}, f32[2,24,64]{2,1,0:T(8,128)S(1)}, u32[]{:S(2)}, u32[]{:S(2)}) collective-permute-start(f32[2,24,64]{2,1,0:T(8,128)S(1)} %broadcast_select_fusion), channel_id=1, source_target_pairs={{0,5},{1,4},{2,7},{3,6},{4,1},{5,0},{6,3},{7,2},{8,13},{9,12},{10,... | collective-permute-start | bytes 36872 | tf_op jit(solution)/shard_map/ppermute | solution.py:50
  26.1 7.7 %collective-permute-start.6 = (f32[2,24,64]{2,1,0:T(8,128)S(1)}, f32[2,24,64]{2,1,0:T(8,128)S(1)}, u32[]{:S(2)}, u32[]{:S(2)}) collective-permute-start(f32[2,24,64]{2,1,0:T(8,128)S(1)} %broadcast_select_fusion), channel_id=1, source_target_pairs={{0,6},{1,7},{2,4},{3,5},{4,2},{5,3},{6,0},{7,1},{8,14},{9,15},{10,... | collective-permute-start | bytes 36872 | tf_op jit(solution)/shard_map/ppermute | solution.py:50
  28.9 5.0 %collective-permute-start.5 = (f32[2,24,64]{2,1,0:T(8,128)S(1)}, f32[2,24,64]{2,1,0:T(8,128)S(1)}, u32[]{:S(2)}, u32[]{:S(2)}) collective-permute-start(f32[2,24,64]{2,1,0:T(8,128)S(1)} %broadcast_select_fusion), channel_id=1, source_target_pairs={{0,7},{1,6},{2,5},{3,4},{4,3},{5,2},{6,1},{7,0},{8,15},{9,14},{10,... | collective-permute-start | bytes 36872 | tf_op jit(solution)/shard_map/ppermute | solution.py:50
  29.1 1.7 %copy-start.2 = (f32[8,24,8,128]{3,2,1,0:T(8,128)}, f32[8,24,8,128]{3,2,1,0:T(8,128)S(1)}, u32[]{:S(2)}) copy-start(f32[8,24,8,128]{3,2,1,0:T(8,128)S(1)} %bitcast_dynamic-update-slice_fusion.w_ref) | copy-start | bytes 2359300
  29.1 1.7 %copy-start.5 = (f32[16,2,4,8,128]{4,3,2,1,0:T(8,128)S(1)}, f32[16,2,4,8,128]{4,3,2,1,0:T(8,128)}, u32[]{:S(2)}) copy-start(f32[16,2,4,8,128]{4,3,2,1,0:T(8,128)} %get-tuple-element.24) | copy-start | bytes 1572868
  30.8 24.5 %collective-permute-start.1 = (f32[16,2,4,8,128]{4,3,2,1,0:T(8,128)S(1)}, f32[16,2,4,8,128]{4,3,2,1,0:T(8,128)S(1)}, u32[]{:S(2)}, u32[]{:S(2)}) collective-permute-start(f32[16,2,4,8,128]{4,3,2,1,0:T(8,128)S(1)} %copy-done.5), channel_id=1, source_target_pairs={{16,0},{32,16},{48,32},{64,48},{80,64},{96,80},{112,96},{128,112},... | collective-permute-start | bytes 1572872 | tf_op jit(solution)/shard_map/ppermute | solution.py:148
  33.8 21.5 %collective-permute-start = (f32[16,2,4,8,128]{4,3,2,1,0:T(8,128)S(1)}, f32[16,2,4,8,128]{4,3,2,1,0:T(8,128)S(1)}, u32[]{:S(2)}, u32[]{:S(2)}) collective-permute-start(f32[16,2,4,8,128]{4,3,2,1,0:T(8,128)S(1)} %get-tuple-element.25), channel_id=1, source_target_pairs={{0,16},{16,32},{32,48},{48,64},{64,80},{80,96},{96,112},{112,128},... | collective-permute-start | bytes 1572872 | tf_op jit(solution)/shard_map/ppermute | solution.py:147
  55.3 0.8 %copy-start.3 = (f32[16,2,4,8,128]{4,3,2,1,0:T(8,128)}, f32[16,2,4,8,128]{4,3,2,1,0:T(8,128)S(1)}, u32[]{:S(2)}) copy-start(f32[16,2,4,8,128]{4,3,2,1,0:T(8,128)S(1)} %collective-permute-done.1.east_ref) | copy-start | bytes 1572868
  56.1 0.8 copy-start.4

commit v8 on v6

--- a/solution.py
+++ b/solution.py
@@ -147,6 +147,12 @@
     west = lax.ppermute(tail, axis, [(i, (i + 1) % count) for i in range(count)])
     east = lax.ppermute(head, axis, [((i + 1) % count, i) for i in range(count)])
     return west, east
+
+
+def lanes_to(source, width):
+    pad = [(0, 0)] * source.ndim
+    pad[-1] = (0, width - source.shape[-1])
+    return jnp.pad(source, pad)
 
 
 def cell_shift(x, step, lane, forward):
@@ -333,7 +339,7 @@
             )
         )
     )
-    seeds = as_tiles(cells_of(objective_seeds))
+    seeds = lanes_to(objective_seeds, 128)[:, :, None, :]
     out = two_retreats(as_tiles(adjoint_in), west, east, stencil, slopes, seeds)
     return out.reshape(adjoint_in.shape)
 

time: 72.9 us -> 71.3 us (0.978)
  local copies, waits for them, and re-layouts: 11.7 us -> 10.8 us
    unnamed x35 -> x34, local copies, waits for them, and re-layouts: 5.78 us -> 4.34 us
  transfers between devices with their start and end apart: 12 -> 12, of which waited for: 2 -> 3; matrix products, arithmetic and copies ran while one was open for 10% -> 9% of each run, Pallas kernels for 0% -> 0%
where the time goes in v8:
time: 71.3 us; the launch traced here: 70.8 us
  starting transfers between devices  22.9 us (32%)
  waiting for transfers between devices  20.5 us (29%)
  Pallas kernels  12.7 us (18%)
  local copies, waits for them, and re-layouts  10.8 us (15%)
  other arithmetic  2.72 us (4%)
  between operations  1.13 us (2%)
    ppermute x1, waiting for transfers between devices, halves(): lax.ppermute(head, axis, [((i + 1) % count, i) for i in range(count)])  19.1 us
    pallas_call x1, Pallas kernels, two_retreats(): pl.pallas_call(retreat_kernel, out_shape=jax.ShapeDtypeStruct(center.shap...  12.7 us
    ppermute x7, starting transfers between devices, spread(): moved = lax.ppermute(value, axis, [(i, i ^ mask) for i in range(count)])  10.1 us
    ppermute x1, starting transfers between devices, padded(): lax.ppermute(head, axis, [((i + 1) % count, i) for i in range(count)])  5.3 us
    unnamed x34, local copies, waits for them, and re-layouts  4.34 us
    ppermute x1, starting transfers between devices, halves(): lax.ppermute(head, axis, [((i + 1) % count, i) for i in range(count)])  2.91 us
    reshape x1, local copies, waits for them, and re-layouts, staged(): return out.reshape(adjoint_in.shape)  2.7 us
    ppermute x1, starting transfers between devices, spread(): moved = lax.ppermute(value, axis, [(i, i ^ top) for i in range(count)])  2.53 us
  transfers between devices with their start and end apart: 12, of which 3 were waited for; matrix products, arithmetic and copies ran while one was open for 9% of the time, Pallas kernels for 0%

profile of v8, /device:TPU:1, one launch (start us, length us, event | category | flops | bytes accessed | tf_op | source)
XLA Modules:
  0.0 70.8 jit_solution(8511504904468112796)
XLA Ops:
  0.7 0.7 convert_element_type.37
  1.4 0.8 %convert_element_type.36 = f32[16,1024]{1,0:T(8,128)S(1)} convert(s32[16,1024]{1,0:T(8,128)} %param.12) | non-fusion elementwise | flops 16384 | bytes 131072 | tf_op jit(solution)/shard_map/convert_element_type | solution.py:254
  2.3 1.0 %concatenate.37 = f32[16,3296]{1,0:T(8,128)S(1)} concatenate(f32[16,64]{1,0:T(8,128)S(1)} %get-tuple-element.39, f32[16,64]{1,0:T(8,128)S(1)} %get-tuple-element.38, f32[16,1024]{1,0:T(8,128)S(1)} %convert_element_type.36, f32[16,1024]{1,0:T(8,128)} %param.13, f32[16,1024]{1,0:T(8,128)} %param.14, f32[16,32]{1,0:T(8,128)} %param.15, f32[16,32]{1,0:T(8,128)} %param.16, ...), dimensions={1} | concatenate | bytes 421888 | tf_op jit(solution)/shard_map/concatenate | solution.py:250
  3.3 0.6 fusion.52
  3.9 2.0 %collective-permute-start.2 = (f32[4,3296]{1,0:T(4,128)}, f32[4,3296]{1,0:T(4,128)S(1)}, u32[]{:S(2)}, u32[]{:S(2)}) collective-permute-start(f32[4,3296]{1,0:T(4,128)} %get-tuple-element.36), channel_id=1, source_target_pairs={{0,16},{16,32},{32,48},{48,64},{64,80},{80,96},{96,112},{112,128},... | collective-permute-start | bytes 158216 | tf_op jit(solution)/shard_map/ppermute | solution.py:29
  5.9 5.3 %collective-permute-start.3 = (f32[4,3296]{1,0:T(4,128)S(1)}, f32[4,3296]{1,0:T(4,128)S(1)}, u32[]{:S(2)}, u32[]{:S(2)}) collective-permute-start(f32[4,3296]{1,0:T(4,128)S(1)} %get-tuple-element.37), channel_id=1, source_target_pairs={{16,0},{32,16},{48,32},{64,48},{80,64},{96,80},{112,96},{128,112},... | collective-permute-start | bytes 158216 | tf_op jit(solution)/shard_map/ppermute | solution.py:31
  11.2 2.1 %copy.10 = f32[64,8,8,128]{3,2,1,0:T(8,128)S(1)} copy(f32[64,8,8,128]{3,1,2,0:T(8,128)} %bitcast.409) | data formatting | bytes 4194304
  13.3 1.0 %fusion.51 = (f32[16,2,4,8,128]{4,3,2,1,0:T(8,128)}, f32[16,2,4,8,128]{4,3,2,1,0:T(8,128)S(1)}) fusion(f32[16,2,16,8,128]{4,3,2,1,0:T(8,128)S(1)} %bitcast.407), kind=kLoop, calls=%fused_computation.204 | loop fusion | bytes 2097152 | tf_op jit(solution)/shard_map/slice | solution.py:145
  14.6 2.5 %collective-permute-start.4 = (f32[2,24,64]{2,1,0:T(8,128)S(1)}, f32[2,24,64]{2,1,0:T(8,128)S(1)}, u32[]{:S(2)}, u32[]{:S(2)}) collective-permute-start(f32[2,24,64]{2,1,0:T(8,128)S(1)} %pad_maximum_fusion.1), channel_id=1, source_target_pairs={{0,8},{1,9},{2,10},{3,11},{4,12},{5,13},{6,14},{7,15},{8,0},{9,1},... | collective-permute-start | bytes 36872 | tf_op jit(solution)/shard_map/ppermute | solution.py:45
  18.1 0.8 %collective-permute-done.4 = f32[2,24,64]{2,1,0:T(8,128)S(1)} collective-permute-done((f32[2,24,64]{2,1,0:T(8,128)S(1)}, f32[2,24,64]{2,1,0:T(8,128)S(1)}, u32[]{:S(2)}, u32[]{:S(2)}) %collective-permute-start.4) | collective-permute-done | bytes 12320 | tf_op jit(solution)/shard_map/ppermute | solution.py:45
  18.9 2.1 %collective-permute-start.11 = (f32[2,24,64]{2,1,0:T(8,128)S(1)}, f32[2,24,64]{2,1,0:T(8,128)S(1)}, u32[]{:S(2)}, u32[]{:S(2)}) collective-permute-start(f32[2,24,64]{2,1,0:T(8,128)S(1)} %broadcast_select_fusion), channel_id=1, source_target_pairs={{0,1},{1,0},{2,3},{3,2},{4,5},{5,4},{6,7},{7,6},{8,9},{9,8},{10,11... | collective-permute-start | bytes 36872 | tf_op jit(solution)/shard_map/ppermute | solution.py:50
  21.0 1.3 %collective-permute-start.10 = (f32[2,24,64]{2,1,0:T(8,128)S(1)}, f32[2,24,64]{2,1,0:T(8,128)S(1)}, u32[]{:S(2)}, u32[]{:S(2)}) collective-permute-start(f32[2,24,64]{2,1,0:T(8,128)S(1)} %broadcast_select_fusion), channel_id=1, source_target_pairs={{0,2},{1,3},{2,0},{3,1},{4,6},{5,7},{6,4},{7,5},{8,10},{9,11},{10,... | collective-permute-start | bytes 36872 | tf_op jit(solution)/shard_map/ppermute | solution.py:50
  22.3 0.5 collective-permute-start.9
  22.9 2.9 %collective-permute-start.8 = (f32[2,24,64]{2,1,0:T(8,128)S(1)}, f32[2,24,64]{2,1,0:T(8,128)S(1)}, u32[]{:S(2)}, u32[]{:S(2)}) collective-permute-start(f32[2,24,64]{2,1,0:T(8,128)S(1)} %broadcast_select_fusion), channel_id=1, source_target_pairs={{0,4},{1,5},{2,6},{3,7},{4,0},{5,1},{6,2},{7,3},{8,12},{9,13},{10,... | collective-permute-start | bytes 36872 | tf_op jit(solution)/shard_map/ppermute | solution.py:50
  25.8 0.4 collective-permute-start.7
  26.1 2.7 %collective-permute-start.6 = (f32[2,24,64]{2,1,0:T(8,128)S(1)}, f32[2,24,64]{2,1,0:T(8,128)S(1)}, u32[]{:S(2)}, u32[]{:S(2)}) collective-permute-start(f32[2,24,64]{2,1,0:T(8,128)S(1)} %broadcast_select_fusion), channel_id=1, source_target_pairs={{0,6},{1,7},{2,4},{3,5},{4,2},{5,3},{6,0},{7,1},{8,14},{9,15},{10,... | collective-permute-start | bytes 36872 | tf_op jit(solution)/shard_map/ppermute | solution.py:50
  29.1 0.7 %pad.43 = f32[16,24,128]{2,1,0:T(8,128)} pad(f32[16,24,32]{2,1,0:T(8,128)S(1)} %compare_select_fusion, f32[]{:T(128)} %constant.128.clone.1), padding=0_0x0_0x0_96 | pad | bytes 245764 | tf_op jit(solution)/shard_map/jit(_pad)/pad | solution.py:155
  29.9 2.9 %collective-permute-start.1 = (f32[16,2,4,8,128]{4,3,2,1,0:T(8,128)S(1)}, f32[16,2,4,8,128]{4,3,2,1,0:T(8,128)S(1)}, u32[]{:S(2)}, u32[]{:S(2)}) collective-permute-start(f32[16,2,4,8,128]{4,3,2,1,0:T(8,128)S(1)} %copy-done.5), channel_id=1, source_target_pairs={{16,0},{32,16},{48,32},{64,48},{80,64},{96,80},{112,96},{128,112},... | collective-permute-start | bytes 1572872 | tf_op jit(solution)/shard_map/ppermute | solution.py:148
  32.8 0.5 collective-permute-done.5
  34.4 0.8 %copy.19 = f32[12,8,8,128]{3,2,1,0:T(8,128)} copy(f32[12,8,8,128]{3,1,2,0:T(8,128)S(1)} %bitcast.411) | data formatting | bytes 786432
  35.2 19.1 %collective-permute-done.1.east_ref = f32[16,2,4,8,128]{4,3,2,1,0:T(8,128)S(1)} collective-permute-done((f32[16,2,4,8,128]{4,3,2,1,0:T(8,128)S(1)}, f32[16,2,4,8,128]{4,3,2,1,0:T(8,128)S(1)}, u32[]{:S(2)}, u32[]{:S(2)}) %collective-permute-start.1) | collective-permute-done | bytes 524320 | tf_op jit(solution)/shard_map/ppermute | solution.py:148
  54.3 0.8 %copy-done.3 = f32[16,2,4,8,128]{4,3,2,1,0:T(8,128)} copy-done((f32[16,2,4,8,128]{4,3,2,1,0:T(8,128)}, f32[16,2,4,8,128]{4,3,2,1,0:T(8,128)S(1)}, u32[]{:S(2)}) %copy-start.3) | copy-done | bytes 524312
  55.3 12.7 %shard_map.91 = f32[16,2,16,8,128]{4,3,2,1,0:T(8,128)} custom-call(f32[16,2,16,8,128]{4,3,2,1,0:T(8,128)} %bitcast.408, f32[16,2,4,8,128]{4,3,2,1,0:T(8,128)} %copy-done.4, f32[16,2,4,8,128]{4,3,2,1,0:T(8,128)} %copy-done.3, f32[8,24,8,128]{3,2,1,0:T(8,128)} %copy-done.2, f32[2,2,24,8,128]{4,3,2,1,0:T(8,128)} %bitcast.410, f32[16,24,1,128]{3,2,1,0:T(1,128)} %bitcast.416), custom_call_target="tpu_custom_call" | custom-call | tf_op jit(solution)/shard_map/pallas_call | solution.py:216
  68.1 2.7 %reshape.64 = f32[16,2,16,1024]{3,2,1,0:T(8,128)} reshape(f32[16,2,16,8,128]{4,3,2,1,0:T(8,128)} %shard_map.91) | data formatting | bytes 4194304 | tf_op jit(solution)/shard_map/reshape | solution.py:344
  (81 shorter events, 2.6 us)
Async XLA Ops:
  0.0 2.3 %copy-start = (f32[4,2,16,1024]{3,2,1,0:T(8,128)S(1)}, f32[4,2,16,1024]{3,2,1,0:T(8,128)}, u32[]{:S(2)}) copy-start(f32[4,2,16,1024]{3,2,1,0:T(8,128)} %param.10) | copy-start | bytes 1572868
  3.9 10.4 %collective-permute-start.2 = (f32[4,3296]{1,0:T(4,128)}, f32[4,3296]{1,0:T(4,128)S(1)}, u32[]{:S(2)}, u32[]{:S(2)}) collective-permute-start(f32[4,3296]{1,0:T(4,128)} %get-tuple-element.36), channel_id=1, source_target_pairs={{0,16},{16,32},{32,48},{48,64},{64,80},{80,96},{96,112},{112,128},... | collective-permute-start | bytes 158216 | tf_op jit(solution)/shard_map/ppermute | solution.py:29
  5.9 8.3 %collective-permute-start.3 = (f32[4,3296]{1,0:T(4,128)S(1)}, f32[4,3296]{1,0:T(4,128)S(1)}, u32[]{:S(2)}, u32[]{:S(2)}) collective-permute-start(f32[4,3296]{1,0:T(4,128)S(1)} %get-tuple-element.37), channel_id=1, source_target_pairs={{16,0},{32,16},{48,32},{64,48},{80,64},{96,80},{112,96},{128,112},... | collective-permute-start | bytes 158216 | tf_op jit(solution)/shard_map/ppermute | solution.py:31
  13.3 3.9 %copy-start.1 = (f32[64,8,8,128]{3,2,1,0:T(8,128)}, f32[64,8,8,128]{3,2,1,0:T(8,128)S(1)}, u32[]{:S(2)}) copy-start(f32[64,8,8,128]{3,2,1,0:T(8,128)S(1)} %copy.10) | copy-start | bytes 6291460
  14.6 4.3 %collective-permute-start.4 = (f32[2,24,64]{2,1,0:T(8,128)S(1)}, f32[2,24,64]{2,1,0:T(8,128)S(1)}, u32[]{:S(2)}, u32[]{:S(2)}) collective-permute-start(f32[2,24,64]{2,1,0:T(8,128)S(1)} %pad_maximum_fusion.1), channel_id=1, source_target_pairs={{0,8},{1,9},{2,10},{3,11},{4,12},{5,13},{6,14},{7,15},{8,0},{9,1},... | collective-permute-start | bytes 36872 | tf_op jit(solution)/shard_map/ppermute | solution.py:45
  17.6 12.3 %copy-start.5 = (f32[16,2,4,8,128]{4,3,2,1,0:T(8,128)S(1)}, f32[16,2,4,8,128]{4,3,2,1,0:T(8,128)}, u32[]{:S(2)}) copy-start(f32[16,2,4,8,128]{4,3,2,1,0:T(8,128)} %get-tuple-element.24) | copy-start | bytes 1572868
  18.9 7.2 %collective-permute-start.11 = (f32[2,24,64]{2,1,0:T(8,128)S(1)}, f32[2,24,64]{2,1,0:T(8,128)S(1)}, u32[]{:S(2)}, u32[]{:S(2)}) collective-permute-start(f32[2,24,64]{2,1,0:T(8,128)S(1)} %broadcast_select_fusion), channel_id=1, source_target_pairs={{0,1},{1,0},{2,3},{3,2},{4,5},{5,4},{6,7},{7,6},{8,9},{9,8},{10,11... | collective-permute-start | bytes 36872 | tf_op jit(solution)/shard_map/ppermute | solution.py:50
  21.0 7.9 %collective-permute-start.10 = (f32[2,24,64]{2,1,0:T(8,128)S(1)}, f32[2,24,64]{2,1,0:T(8,128)S(1)}, u32[]{:S(2)}, u32[]{:S(2)}) collective-permute-start(f32[2,24,64]{2,1,0:T(8,128)S(1)} %broadcast_select_fusion), channel_id=1, source_target_pairs={{0,2},{1,3},{2,0},{3,1},{4,6},{5,7},{6,4},{7,5},{8,10},{9,11},{10,... | collective-permute-start | bytes 36872 | tf_op jit(solution)/shard_map/ppermute | solution.py:50
  22.3 7.5 %collective-permute-start.9 = (f32[2,24,64]{2,1,0:T(8,128)S(1)}, f32[2,24,64]{2,1,0:T(8,128)S(1)}, u32[]{:S(2)}, u32[]{:S(2)}) collective-permute-start(f32[2,24,64]{2,1,0:T(8,128)S(1)} %broadcast_select_fusion), channel_id=1, source_target_pairs={{0,3},{1,2},{2,1},{3,0},{4,7},{5,6},{6,5},{7,4},{8,11},{9,10},{10,... | collective-permute-start | bytes 36872 | tf_op jit(solution)/shard_map/ppermute | solution.py:50
  22.9 9.9 %collective-permute-start.8 = (f32[2,24,64]{2,1,0:T(8,128)S(1)}, f32[2,24,64]{2,1,0:T(8,128)S(1)}, u32[]{:S(2)}, u32[]{:S(2)}) collective-permute-start(f32[2,24,64]{2,1,0:T(8,128)S(1)} %broadcast_select_fusion), channel_id=1, source_target_pairs={{0,4},{1,5},{2,6},{3,7},{4,0},{5,1},{6,2},{7,3},{8,12},{9,13},{10,... | collective-permute-start | bytes 36872 | tf_op jit(solution)/shard_map/ppermute | solution.py:50
  25.8 7.0 %collective-permute-start.7 = (f32[2,24,64]{2,1,0:T(8,128)S(1)}, f32[2,24,64]{2,1,0:T(8,128)S(1)}, u32[]{:S(2)}, u32[]{:S(2)}) collective-permute-start(f32[2,24,64]{2,1,0:T(8,128)S(1)} %broadcast_select_fusion), channel_id=1, source_target_pairs={{0,5},{1,4},{2,7},{3,6},{4,1},{5,0},{6,3},{7,2},{8,13},{9,12},{10,... | collective-permute-start | bytes 36872 | tf_op jit(solution)/shard_map/ppermute | solution.py:50
  26.1 6.7 %collective-permute-start.6 = (f32[2,24,64]{2,1,0:T(8,128)S(1)}, f32[2,24,64]{2,1,0:T(8,128)S(1)}, u32[]{:S(2)}, u32[]{:S(2)}) collective-permute-start(f32[2,24,64]{2,1,0:T(8,128)S(1)} %broadcast_select_fusion), channel_id=1, source_target_pairs={{0,6},{1,7},{2,4},{3,5},{4,2},{5,3},{6,0},{7,1},{8,14},{9,15},{10,... | collective-permute-start | bytes 36872 | tf_op jit(solution)/shard_map/ppermute | solution.py:50
  28.9 4.5 %collective-permute-start.5 = (f32[2,24,64]{2,1,0:T(8,128)S(1)}, f32[2,24,64]{2,1,0:T(8,128)S(1)}, u32[]{:S(2)}, u32[]{:S(2)}) collective-permute-start(f32[2,24,64]{2,1,0:T(8,128)S(1)} %broadcast_select_fusion), channel_id=1, source_target_pairs={{0,7},{1,6},{2,5},{3,4},{4,3},{5,2},{6,1},{7,0},{8,15},{9,14},{10,... | collective-permute-start | bytes 36872 | tf_op jit(solution)/shard_map/ppermute | solution.py:50
  29.1 25.2 %copy-start.2 = (f32[8,24,8,128]{3,2,1,0:T(8,128)}, f32[8,24,8,128]{3,2,1,0:T(8,128)S(1)}, u32[]{:S(2)}) copy-start(f32[8,24,8,128]{3,2,1,0:T(8,128)S(1)} %bitcast_dynamic-update-slice_fusion.w_ref) | copy-start | bytes 2359300
  29.9 24.4 %collective-permute-start.1 = (f32[16,2,4,8,128]{4,3,2,1,0:T(8,128)S(1)}, f32[16,2,4,8,128]{4,3,2,1,0:T(8,128)S(1)}, u32[]{:S(2)}, u32[]{:S(2)}) collective-permute-start(f32[16,2,4,8,128]{4,3,2,1,0:T(8,128)S(1)} %copy-done.5), channel_id=1, source_target_pairs={{16,0},{32,16},{48,32},{64,48},{80,64},{96,80},{112,96},{128,112},... | collective-permute-start | bytes 1572872 | tf_op jit(solution)/shard_map/ppermute | solution.py:148
  32.8 21.5 %collective-permute-start = (f32[16,2,4,8,128]{4,3,2,1,0:T(8,128)S(1)}, f32[16,2,4,8,128]{4,3,2,1,0:T(8,128)S(1)}, u32[]{:S(2)}, u32[]{:S(2)}) collective-permute-start(f32[16,2,4,8,128]{4,3,2,1,0:T(8,128)S(1)} %get-tuple-element.25), channel_id=1, source_target_pairs={{0,16},{16,32},{32,48},{48,64},{64,80},{80,96},{96,112},{112,128},... | collective-permute-start | bytes 1572872 | tf_op jit(solution)/shard_map/ppermute | solution.py:147
  54.3 0.8 %copy-start.3 = (f32[16,2,4,8,128]{4,3,2,1,0:T(8,128)}, f32[16,2,4,8,128]{4,3,2,1,0:T(8,128)S(1)}, u32[]{:S(2)}) copy-start(f32[16,2,4,8,128]{4,3,2,1,0:T(8,128)S(1)} %collective-permute-done.1.east_ref) | copy-start | bytes 1572868
  54.3 1.0 %copy-start.4 = (f32[16,2,4,8,128]{4,3,2,1,0:T(8,128)}, f32[16,2,4,8,128]{4,3,2,1,0:T(8,128)S(1)}, u32[]{:S(2)}) copy-start(f32[16,2,4,8,128]{4,3,2,1,0:T(8,128)S(1)} %collective-permute-done.west_ref) | copy-start | bytes 1572868

commit v9 on v8

--- a/solution.py
+++ b/solution.py
@@ -170,11 +170,8 @@
     local = center_ref.shape[2]
     rim = west_ref.shape[2]
     lane = lax.broadcasted_iota(jnp.int32, (8, 128), 1)
-    e_ref[:, rim : rim + local] = center_ref[0]
-    e_ref[:, 0:rim] = west_ref[0]
-    e_ref[:, rim + local : 2 * rim + local] = east_ref[0]
-
-    def step(src, k, stage):
+
+    def step(src, k, stage, o):
         w = [w_ref[m, k] for m in range(8)]
         results = []
         for t in range(tracers):
@@ -191,41 +188,40 @@
                 + w[6] * (cell_shift(x_0, ROWS, lane, True) - x_0)
                 - w[7] * (x_0 - cell_shift(x_0, ROWS, lane, False))
             )
-            forcing = src[0, k] + seed_ref[0, k]
+            forcing = src[0, k] + seed_ref[o, k]
             results.append(x_0 + zonal + mix + s_ref[stage, t, k] * forcing)
         return results
 
-    def first(k, carry):
-        for t, value in enumerate(step(e_ref, k, 0)):
-            f_ref[t, k] = value
-        return carry
-
-    def second(k, carry):
-        for t, value in enumerate(step(f_ref, k, 1)):
-            out_ref[0, t, k - rim] = value
-        return carry
-
-    lax.fori_loop(2, 2 * rim + local - 2, first, 0, unroll=True)
-    lax.fori_loop(rim, rim + local, second, 0, unroll=True)
+    for o in range(center_ref.shape[0]):
+        e_ref[:, rim : rim + local] = center_ref[o]
+        e_ref[:, 0:rim] = west_ref[o]
+        e_ref[:, rim + local : 2 * rim + local] = east_ref[o]
+        for k in range(2, 2 * rim + local - 2):
+            for t, value in enumerate(step(e_ref, k, 0, o)):
+                f_ref[t, k] = value
+        for k in range(rim, rim + local):
+            for t, value in enumerate(step(f_ref, k, 1, o)):
+                out_ref[o, t, k - rim] = value
 
 
 def two_retreats(center, west, east, stencil, slopes, seeds):
     groups, tracers, local, sub, lanes = center.shape
     rim = west.shape[2]
     span = local + 2 * rim
+    pack = 4 if groups % 4 == 0 else 1
     return pl.pallas_call(
         retreat_kernel,
         out_shape=jax.ShapeDtypeStruct(center.shape, center.dtype),
-        grid=(groups,),
+        grid=(groups // pack,),
         in_specs=[
-            pl.BlockSpec((1, tracers, local, sub, lanes), lambda g: (g, 0, 0, 0, 0)),
-            pl.BlockSpec((1, tracers, rim, sub, lanes), lambda g: (g, 0, 0, 0, 0)),
-            pl.BlockSpec((1, tracers, rim, sub, lanes), lambda g: (g, 0, 0, 0, 0)),
+            pl.BlockSpec((pack, tracers, local, sub, lanes), lambda g: (g, 0, 0, 0, 0)),
+            pl.BlockSpec((pack, tracers, rim, sub, lanes), lambda g: (g, 0, 0, 0, 0)),
+            pl.BlockSpec((pack, tracers, rim, sub, lanes), lambda g: (g, 0, 0, 0, 0)),
             pl.BlockSpec(stencil.shape, lambda g: (0, 0, 0, 0)),
             pl.BlockSpec(slopes.shape, lambda g: (0, 0, 0, 0, 0)),
-            pl.BlockSpec((1,) + seeds.shape[1:], lambda g: (g, 0, 0, 0)),
+            pl.BlockSpec((pack,) + seeds.shape[1:], lambda g: (g, 0, 0, 0)),
         ],
-        out_specs=pl.BlockSpec((1, tracers, local, sub, lanes), lambda g: (g, 0, 0, 0, 0)),
+        out_specs=pl.BlockSpec((pack, tracers, local, sub, lanes), lambda g: (g, 0, 0, 0, 0)),
         scratch_shapes=[
             pltpu.VMEM((tracers, span, sub, lanes), jnp.float32),
             pltpu.VMEM((tracers, span, sub, lanes), jnp.float32),

time: 71.3 us -> 66 us (0.926)
  Pallas kernels: 12.7 us -> 7.63 us
    pallas_call x1, Pallas kernels: 12.7 us -> 7.63 us  [two_retreats(): pl.pallas_call(retreat_kernel, out_shape=jax.ShapeDtypeStruct(center.shap...]
  transfers between devices with their start and end apart: 12 -> 12, of which waited for: 3 -> 3; matrix products, arithmetic and copies ran while one was open for 9% -> 10% of each run, Pallas kernels for 0% -> 0%
where the time goes in v9:
time: 66 us; the launch traced here: 65.6 us
  starting transfers between devices  22.9 us (35%)
  waiting for transfers between devices  20.5 us (31%)
  local copies, waits for them, and re-layouts  10.8 us (16%)
  Pallas kernels  7.63 us (12%)
  other arithmetic  2.72 us (4%)
  between operations  1.13 us (2%)
    ppermute x1, waiting for transfers between devices, halves(): lax.ppermute(head, axis, [((i + 1) % count, i) for i in range(count)])  19.1 us
    ppermute x7, starting transfers between devices, spread(): moved = lax.ppermute(value, axis, [(i, i ^ mask) for i in range(count)])  10.1 us
    pallas_call x1, Pallas kernels, two_retreats(): pl.pallas_call(retreat_kernel, out_shape=jax.ShapeDtypeStruct(center.shap...  7.63 us
    ppermute x1, starting transfers between devices, padded(): lax.ppermute(head, axis, [((i + 1) % count, i) for i in range(count)])  5.3 us
    unnamed x34, local copies, waits for them, and re-layouts  4.34 us
    ppermute x1, starting transfers between devices, halves(): lax.ppermute(head, axis, [((i + 1) % count, i) for i in range(count)])  2.92 us
    reshape x1, local copies, waits for them, and re-layouts, staged(): return out.reshape(adjoint_in.shape)  2.7 us
    ppermute x1, starting transfers between devices, spread(): moved = lax.ppermute(value, axis, [(i, i ^ top) for i in range(count)])  2.53 us
  transfers between devices with their start and end apart: 12, of which 3 were waited for; matrix products, arithmetic and copies ran while one was open for 10% of the time, Pallas kernels for 0%

profile of v9, /device:TPU:1, one launch (start us, length us, event | category | flops | bytes accessed | tf_op | source)
XLA Modules:
  0.0 65.6 jit_solution(10602059705462629550)
XLA Ops:
  0.7 0.7 %convert_element_type.37 = f32[16,32]{1,0:T(8,128)S(1)} convert(s32[16,32]{1,0:T(8,128)} %param.17) | non-fusion elementwise | flops 512 | bytes 4096 | tf_op jit(solution)/shard_map/convert_element_type | solution.py:255
  1.4 0.8 %convert_element_type.36 = f32[16,1024]{1,0:T(8,128)S(1)} convert(s32[16,1024]{1,0:T(8,128)} %param.12) | non-fusion elementwise | flops 16384 | bytes 131072 | tf_op jit(solution)/shard_map/convert_element_type | solution.py:250
  2.3 1.0 %concatenate.37 = f32[16,3296]{1,0:T(8,128)S(1)} concatenate(f32[16,64]{1,0:T(8,128)S(1)} %get-tuple-element.39, f32[16,64]{1,0:T(8,128)S(1)} %get-tuple-element.38, f32[16,1024]{1,0:T(8,128)S(1)} %convert_element_type.36, f32[16,1024]{1,0:T(8,128)} %param.13, f32[16,1024]{1,0:T(8,128)} %param.14, f32[16,32]{1,0:T(8,128)} %param.15, f32[16,32]{1,0:T(8,128)} %param.16, ...), dimensions={1} | concatenate | bytes 421888 | tf_op jit(solution)/shard_map/concatenate | solution.py:246
  3.3 0.6 fusion.52
  3.9 2.0 %collective-permute-start.2 = (f32[4,3296]{1,0:T(4,128)}, f32[4,3296]{1,0:T(4,128)S(1)}, u32[]{:S(2)}, u32[]{:S(2)}) collective-permute-start(f32[4,3296]{1,0:T(4,128)} %get-tuple-element.36), channel_id=1, source_target_pairs={{0,16},{16,32},{32,48},{48,64},{64,80},{80,96},{96,112},{112,128},... | collective-permute-start | bytes 158216 | tf_op jit(solution)/shard_map/ppermute | solution.py:29
  5.9 5.3 %collective-permute-start.3 = (f32[4,3296]{1,0:T(4,128)S(1)}, f32[4,3296]{1,0:T(4,128)S(1)}, u32[]{:S(2)}, u32[]{:S(2)}) collective-permute-start(f32[4,3296]{1,0:T(4,128)S(1)} %get-tuple-element.37), channel_id=1, source_target_pairs={{16,0},{32,16},{48,32},{64,48},{80,64},{96,80},{112,96},{128,112},... | collective-permute-start | bytes 158216 | tf_op jit(solution)/shard_map/ppermute | solution.py:31
  11.2 2.1 %copy.10 = f32[64,8,8,128]{3,2,1,0:T(8,128)S(1)} copy(f32[64,8,8,128]{3,1,2,0:T(8,128)} %bitcast.409) | data formatting | bytes 4194304
  13.3 0.9 %fusion.51 = (f32[16,2,4,8,128]{4,3,2,1,0:T(8,128)}, f32[16,2,4,8,128]{4,3,2,1,0:T(8,128)S(1)}) fusion(f32[16,2,16,8,128]{4,3,2,1,0:T(8,128)S(1)} %bitcast.407), kind=kLoop, calls=%fused_computation.204 | loop fusion | bytes 2097152 | tf_op jit(solution)/shard_map/slice | solution.py:145
  14.6 2.5 %collective-permute-start.4 = (f32[2,24,64]{2,1,0:T(8,128)S(1)}, f32[2,24,64]{2,1,0:T(8,128)S(1)}, u32[]{:S(2)}, u32[]{:S(2)}) collective-permute-start(f32[2,24,64]{2,1,0:T(8,128)S(1)} %pad_maximum_fusion.1), channel_id=1, source_target_pairs={{0,8},{1,9},{2,10},{3,11},{4,12},{5,13},{6,14},{7,15},{8,0},{9,1},... | collective-permute-start | bytes 36872 | tf_op jit(solution)/shard_map/ppermute | solution.py:45
  18.1 0.8 %collective-permute-done.4 = f32[2,24,64]{2,1,0:T(8,128)S(1)} collective-permute-done((f32[2,24,64]{2,1,0:T(8,128)S(1)}, f32[2,24,64]{2,1,0:T(8,128)S(1)}, u32[]{:S(2)}, u32[]{:S(2)}) %collective-permute-start.4) | collective-permute-done | bytes 12320 | tf_op jit(solution)/shard_map/ppermute | solution.py:45
  18.9 2.1 %collective-permute-start.11 = (f32[2,24,64]{2,1,0:T(8,128)S(1)}, f32[2,24,64]{2,1,0:T(8,128)S(1)}, u32[]{:S(2)}, u32[]{:S(2)}) collective-permute-start(f32[2,24,64]{2,1,0:T(8,128)S(1)} %broadcast_select_fusion), channel_id=1, source_target_pairs={{0,1},{1,0},{2,3},{3,2},{4,5},{5,4},{6,7},{7,6},{8,9},{9,8},{10,11... | collective-permute-start | bytes 36872 | tf_op jit(solution)/shard_map/ppermute | solution.py:50
  21.0 1.3 %collective-permute-start.10 = (f32[2,24,64]{2,1,0:T(8,128)S(1)}, f32[2,24,64]{2,1,0:T(8,128)S(1)}, u32[]{:S(2)}, u32[]{:S(2)}) collective-permute-start(f32[2,24,64]{2,1,0:T(8,128)S(1)} %broadcast_select_fusion), channel_id=1, source_target_pairs={{0,2},{1,3},{2,0},{3,1},{4,6},{5,7},{6,4},{7,5},{8,10},{9,11},{10,... | collective-permute-start | bytes 36872 | tf_op jit(solution)/shard_map/ppermute | solution.py:50
  22.3 0.5 collective-permute-start.9
  22.8 2.9 %collective-permute-start.8 = (f32[2,24,64]{2,1,0:T(8,128)S(1)}, f32[2,24,64]{2,1,0:T(8,128)S(1)}, u32[]{:S(2)}, u32[]{:S(2)}) collective-permute-start(f32[2,24,64]{2,1,0:T(8,128)S(1)} %broadcast_select_fusion), channel_id=1, source_target_pairs={{0,4},{1,5},{2,6},{3,7},{4,0},{5,1},{6,2},{7,3},{8,12},{9,13},{10,... | collective-permute-start | bytes 36872 | tf_op jit(solution)/shard_map/ppermute | solution.py:50
  25.8 0.4 collective-permute-start.7
  26.1 2.7 %collective-permute-start.6 = (f32[2,24,64]{2,1,0:T(8,128)S(1)}, f32[2,24,64]{2,1,0:T(8,128)S(1)}, u32[]{:S(2)}, u32[]{:S(2)}) collective-permute-start(f32[2,24,64]{2,1,0:T(8,128)S(1)} %broadcast_select_fusion), channel_id=1, source_target_pairs={{0,6},{1,7},{2,4},{3,5},{4,2},{5,3},{6,0},{7,1},{8,14},{9,15},{10,... | collective-permute-start | bytes 36872 | tf_op jit(solution)/shard_map/ppermute | solution.py:50
  29.1 0.7 %pad.43 = f32[16,24,128]{2,1,0:T(8,128)} pad(f32[16,24,32]{2,1,0:T(8,128)S(1)} %compare_select_fusion, f32[]{:T(128)} %constant.128.clone.1), padding=0_0x0_0x0_96 | pad | bytes 245764 | tf_op jit(solution)/shard_map/jit(_pad)/pad | solution.py:155
  29.9 2.9 %collective-permute-start.1 = (f32[16,2,4,8,128]{4,3,2,1,0:T(8,128)S(1)}, f32[16,2,4,8,128]{4,3,2,1,0:T(8,128)S(1)}, u32[]{:S(2)}, u32[]{:S(2)}) collective-permute-start(f32[16,2,4,8,128]{4,3,2,1,0:T(8,128)S(1)} %copy-done.5), channel_id=1, source_target_pairs={{16,0},{32,16},{48,32},{64,48},{80,64},{96,80},{112,96},{128,112},... | collective-permute-start | bytes 1572872 | tf_op jit(solution)/shard_map/ppermute | solution.py:148
  32.8 0.5 collective-permute-done.5
  34.4 0.8 %copy.19 = f32[12,8,8,128]{3,2,1,0:T(8,128)} copy(f32[12,8,8,128]{3,1,2,0:T(8,128)S(1)} %bitcast.411) | data formatting | bytes 786432
  35.2 19.1 %collective-permute-done.1.east_ref = f32[16,2,4,8,128]{4,3,2,1,0:T(8,128)S(1)} collective-permute-done((f32[16,2,4,8,128]{4,3,2,1,0:T(8,128)S(1)}, f32[16,2,4,8,128]{4,3,2,1,0:T(8,128)S(1)}, u32[]{:S(2)}, u32[]{:S(2)}) %collective-permute-start.1) | collective-permute-done | bytes 524320 | tf_op jit(solution)/shard_map/ppermute | solution.py:148
  54.3 0.8 %copy-done.3 = f32[16,2,4,8,128]{4,3,2,1,0:T(8,128)} copy-done((f32[16,2,4,8,128]{4,3,2,1,0:T(8,128)}, f32[16,2,4,8,128]{4,3,2,1,0:T(8,128)S(1)}, u32[]{:S(2)}) %copy-start.3) | copy-done | bytes 524312
  55.3 7.6 %shard_map.91 = f32[16,2,16,8,128]{4,3,2,1,0:T(8,128)} custom-call(f32[16,2,16,8,128]{4,3,2,1,0:T(8,128)} %bitcast.408, f32[16,2,4,8,128]{4,3,2,1,0:T(8,128)} %copy-done.4, f32[16,2,4,8,128]{4,3,2,1,0:T(8,128)} %copy-done.3, f32[8,24,8,128]{3,2,1,0:T(8,128)} %copy-done.2, f32[2,2,24,8,128]{4,3,2,1,0:T(8,128)} %bitcast.410, f32[16,24,1,128]{3,2,1,0:T(1,128)} %bitcast.416), custom_call_target="tpu_custom_call" | custom-call | tf_op jit(solution)/shard_map/pallas_call | solution.py:212
  62.9 2.7 %reshape.64 = f32[16,2,16,1024]{3,2,1,0:T(8,128)} reshape(f32[16,2,16,8,128]{4,3,2,1,0:T(8,128)} %shard_map.91) | data formatting | bytes 4194304 | tf_op jit(solution)/shard_map/reshape | solution.py:340
  (81 shorter events, 2.6 us)
Async XLA Ops:
  0.0 2.3 %copy-start = (f32[4,2,16,1024]{3,2,1,0:T(8,128)S(1)}, f32[4,2,16,1024]{3,2,1,0:T(8,128)}, u32[]{:S(2)}) copy-start(f32[4,2,16,1024]{3,2,1,0:T(8,128)} %param.10) | copy-start | bytes 1572868
  3.9 10.4 %collective-permute-start.2 = (f32[4,3296]{1,0:T(4,128)}, f32[4,3296]{1,0:T(4,128)S(1)}, u32[]{:S(2)}, u32[]{:S(2)}) collective-permute-start(f32[4,3296]{1,0:T(4,128)} %get-tuple-element.36), channel_id=1, source_target_pairs={{0,16},{16,32},{32,48},{48,64},{64,80},{80,96},{96,112},{112,128},... | collective-permute-start | bytes 158216 | tf_op jit(solution)/shard_map/ppermute | solution.py:29
  5.9 8.3 %collective-permute-start.3 = (f32[4,3296]{1,0:T(4,128)S(1)}, f32[4,3296]{1,0:T(4,128)S(1)}, u32[]{:S(2)}, u32[]{:S(2)}) collective-permute-start(f32[4,3296]{1,0:T(4,128)S(1)} %get-tuple-element.37), channel_id=1, source_target_pairs={{16,0},{32,16},{48,32},{64,48},{80,64},{96,80},{112,96},{128,112},... | collective-permute-start | bytes 158216 | tf_op jit(solution)/shard_map/ppermute | solution.py:31
  13.3 3.9 %copy-start.1 = (f32[64,8,8,128]{3,2,1,0:T(8,128)}, f32[64,8,8,128]{3,2,1,0:T(8,128)S(1)}, u32[]{:S(2)}) copy-start(f32[64,8,8,128]{3,2,1,0:T(8,128)S(1)} %copy.10) | copy-start | bytes 6291460
  14.6 4.3 %collective-permute-start.4 = (f32[2,24,64]{2,1,0:T(8,128)S(1)}, f32[2,24,64]{2,1,0:T(8,128)S(1)}, u32[]{:S(2)}, u32[]{:S(2)}) collective-permute-start(f32[2,24,64]{2,1,0:T(8,128)S(1)} %pad_maximum_fusion.1), channel_id=1, source_target_pairs={{0,8},{1,9},{2,10},{3,11},{4,12},{5,13},{6,14},{7,15},{8,0},{9,1},... | collective-permute-start | bytes 36872 | tf_op jit(solution)/shard_map/ppermute | solution.py:45
  17.6 12.3 %copy-start.5 = (f32[16,2,4,8,128]{4,3,2,1,0:T(8,128)S(1)}, f32[16,2,4,8,128]{4,3,2,1,0:T(8,128)}, u32[]{:S(2)}) copy-start(f32[16,2,4,8,128]{4,3,2,1,0:T(8,128)} %get-tuple-element.24) | copy-start | bytes 1572868
  18.9 7.2 %collective-permute-start.11 = (f32[2,24,64]{2,1,0:T(8,128)S(1)}, f32[2,24,64]{2,1,0:T(8,128)S(1)}, u32[]{:S(2)}, u32[]{:S(2)}) collective-permute-start(f32[2,24,64]{2,1,0:T(8,128)S(1)} %broadcast_select_fusion), channel_id=1, source_target_pairs={{0,1},{1,0},{2,3},{3,2},{4,5},{5,4},{6,7},{7,6},{8,9},{9,8},{10,11... | collective-permute-start | bytes 36872 | tf_op jit(solution)/shard_map/ppermute | solution.py:50
  21.0 7.9 %collective-permute-start.10 = (f32[2,24,64]{2,1,0:T(8,128)S(1)}, f32[2,24,64]{2,1,0:T(8,128)S(1)}, u32[]{:S(2)}, u32[]{:S(2)}) collective-permute-start(f32[2,24,64]{2,1,0:T(8,128)S(1)} %broadcast_select_fusion), channel_id=1, source_target_pairs={{0,2},{1,3},{2,0},{3,1},{4,6},{5,7},{6,4},{7,5},{8,10},{9,11},{10,... | collective-permute-start | bytes 36872 | tf_op jit(solution)/shard_map/ppermute | solution.py:50
  22.3 7.5 %collective-permute-start.9 = (f32[2,24,64]{2,1,0:T(8,128)S(1)}, f32[2,24,64]{2,1,0:T(8,128)S(1)}, u32[]{:S(2)}, u32[]{:S(2)}) collective-permute-start(f32[2,24,64]{2,1,0:T(8,128)S(1)} %broadcast_select_fusion), channel_id=1, source_target_pairs={{0,3},{1,2},{2,1},{3,0},{4,7},{5,6},{6,5},{7,4},{8,11},{9,10},{10,... | collective-permute-start | bytes 36872 | tf_op jit(solution)/shard_map/ppermute | solution.py:50
  22.8 9.9 %collective-permute-start.8 = (f32[2,24,64]{2,1,0:T(8,128)S(1)}, f32[2,24,64]{2,1,0:T(8,128)S(1)}, u32[]{:S(2)}, u32[]{:S(2)}) collective-permute-start(f32[2,24,64]{2,1,0:T(8,128)S(1)} %broadcast_select_fusion), channel_id=1, source_target_pairs={{0,4},{1,5},{2,6},{3,7},{4,0},{5,1},{6,2},{7,3},{8,12},{9,13},{10,... | collective-permute-start | bytes 36872 | tf_op jit(solution)/shard_map/ppermute | solution.py:50
  25.8 7.0 %collective-permute-start.7 = (f32[2,24,64]{2,1,0:T(8,128)S(1)}, f32[2,24,64]{2,1,0:T(8,128)S(1)}, u32[]{:S(2)}, u32[]{:S(2)}) collective-permute-start(f32[2,24,64]{2,1,0:T(8,128)S(1)} %broadcast_select_fusion), channel_id=1, source_target_pairs={{0,5},{1,4},{2,7},{3,6},{4,1},{5,0},{6,3},{7,2},{8,13},{9,12},{10,... | collective-permute-start | bytes 36872 | tf_op jit(solution)/shard_map/ppermute | solution.py:50
  26.1 6.7 %collective-permute-start.6 = (f32[2,24,64]{2,1,0:T(8,128)S(1)}, f32[2,24,64]{2,1,0:T(8,128)S(1)}, u32[]{:S(2)}, u32[]{:S(2)}) collective-permute-start(f32[2,24,64]{2,1,0:T(8,128)S(1)} %broadcast_select_fusion), channel_id=1, source_target_pairs={{0,6},{1,7},{2,4},{3,5},{4,2},{5,3},{6,0},{7,1},{8,14},{9,15},{10,... | collective-permute-start | bytes 36872 | tf_op jit(solution)/shard_map/ppermute | solution.py:50
  28.9 4.5 %collective-permute-start.5 = (f32[2,24,64]{2,1,0:T(8,128)S(1)}, f32[2,24,64]{2,1,0:T(8,128)S(1)}, u32[]{:S(2)}, u32[]{:S(2)}) collective-permute-start(f32[2,24,64]{2,1,0:T(8,128)S(1)} %broadcast_select_fusion), channel_id=1, source_target_pairs={{0,7},{1,6},{2,5},{3,4},{4,3},{5,2},{6,1},{7,0},{8,15},{9,14},{10,... | collective-permute-start | bytes 36872 | tf_op jit(solution)/shard_map/ppermute | solution.py:50
  29.1 25.2 %copy-start.2 = (f32[8,24,8,128]{3,2,1,0:T(8,128)}, f32[8,24,8,128]{3,2,1,0:T(8,128)S(1)}, u32[]{:S(2)}) copy-start(f32[8,24,8,128]{3,2,1,0:T(8,128)S(1)} %bitcast_dynamic-update-slice_fusion.w_ref) | copy-start | bytes 2359300
  29.9 24.4 %collective-permute-start.1 = (f32[16,2,4,8,128]{4,3,2,1,0:T(8,128)S(1)}, f32[16,2,4,8,128]{4,3,2,1,0:T(8,128)S(1)}, u32[]{:S(2)}, u32[]{:S(2)}) collective-permute-start(f32[16,2,4,8,128]{4,3,2,1,0:T(8,128)S(1)} %copy-done.5), channel_id=1, source_target_pairs={{16,0},{32,16},{48,32},{64,48},{80,64},{96,80},{112,96},{128,112},... | collective-permute-start | bytes 1572872 | tf_op jit(solution)/shard_map/ppermute | solution.py:148
  32.8 21.5 %collective-permute-start = (f32[16,2,4,8,128]{4,3,2,1,0:T(8,128)S(1)}, f32[16,2,4,8,128]{4,3,2,1,0:T(8,128)S(1)}, u32[]{:S(2)}, u32[]{:S(2)}) collective-permute-start(f32[16,2,4,8,128]{4,3,2,1,0:T(8,128)S(1)} %get-tuple-element.25), channel_id=1, source_target_pairs={{0,16},{16,32},{32,48},{48,64},{64,80},{80,96},{96,112},{112,128},... | collective-permute-start | bytes 1572872 | tf_op jit(solution)/shard_map/ppermute | solution.py:147
  54.3 0.8 %copy-start.3 = (f32[16,2,4,8,128]{4,3,2,1,0:T(8,128)}, f32[16,2,4,8,128]{4,3,2,1,0:T(8,128)S(1)}, u32[]{:S(2)}) copy-start(f32[16,2,4,8,128]{4,3,2,1,0:T(8,128)S(1)} %collective-permute-done.1.east_ref) | copy-start | bytes 1572868
  54.3 1.0 %copy-start.4 = (f32[16,2,4,8,128]{4,3,2,1,0:T(8,128)}, f32[16,2,4,8,128]{4,3,2,1,0:T(8,128)S(1)}, u32[]{:S(2)}) copy-start(f32[16,2,4,8,128]{4,3,2,1,0:T(8,128)S(1)} %collective-permute-done.west_ref) | copy-start | bytes 1572868

commit v10 on v9

--- a/solution.py
+++ b/solution.py
@@ -199,9 +199,11 @@
         for k in range(2, 2 * rim + local - 2):
             for t, value in enumerate(step(e_ref, k, 0, o)):
                 f_ref[t, k] = value
-        for k in range(rim, rim + local):
-            for t, value in enumerate(step(f_ref, k, 1, o)):
-                out_ref[o, t, k - rim] = value
+        for q in range(0, local, 8):
+            rows = [step(f_ref, rim + q + i, 1, o) for i in range(8)]
+            for t in range(tracers):
+                stacked = jnp.stack([row[t] for row in rows])
+                out_ref[o, t, q : q + 8, :] = stacked.reshape(8, stacked.shape[1] * stacked.shape[2])
 
 
 def two_retreats(center, west, east, stencil, slopes, seeds):
@@ -211,7 +213,7 @@
     pack = 4 if groups % 4 == 0 else 1
     return pl.pallas_call(
         retreat_kernel,
-        out_shape=jax.ShapeDtypeStruct(center.shape, center.dtype),
+        out_shape=jax.ShapeDtypeStruct((groups, tracers, local, sub * lanes), center.dtype),
         grid=(groups // pack,),
         in_specs=[
             pl.BlockSpec((pack, tracers, local, sub, lanes), lambda g: (g, 0, 0, 0, 0)),
@@ -221,7 +223,7 @@
             pl.BlockSpec(slopes.shape, lambda g: (0, 0, 0, 0, 0)),
             pl.BlockSpec((pack,) + seeds.shape[1:], lambda g: (g, 0, 0, 0)),
         ],
-        out_specs=pl.BlockSpec((pack, tracers, local, sub, lanes), lambda g: (g, 0, 0, 0, 0)),
+        out_specs=pl.BlockSpec((pack, tracers, local, sub * lanes), lambda g: (g, 0, 0, 0)),
         scratch_shapes=[
             pltpu.VMEM((tracers, span, sub, lanes), jnp.float32),
             pltpu.VMEM((tracers, span, sub, lanes), jnp.float32),
@@ -243,10 +245,16 @@
     owner_index = interval[0] % owners
     band = 2 * ROWS
     stored = lax.dynamic_index_in_dim(checkpoint_store, interval[0] // owners, 0, keepdims=False)
+    band_wide = padded(
+        jnp.concatenate([stored[0, :, :band], stored[1, :, :band]], axis=1),
+        (("tile", 0),),
+        rim_depth,
+    )
+    initial_wide = spread(
+        jnp.stack([band_wide[:, :band], band_wide[:, band : 2 * band]]), "obj", owner_index
+    )
     statics = jnp.concatenate(
         [
-            stored[0, :, :band],
-            stored[1, :, :band],
             sea_mask.astype(jnp.float32),
             zonal_speed,
             mixing,
@@ -257,10 +265,6 @@
         axis=1,
     )
     widened = padded(statics, (("tile", 0),), rim_depth)
-    initial_wide = spread(
-        jnp.stack([widened[:, :band], widened[:, band : 2 * band]]), "obj", owner_index
-    )
-    widened = widened[:, 2 * band :]
     sea_wide = widened[:, :cell_count]
     speed_wide = widened[:, cell_count : 2 * cell_count]
     mixing_wide = widened[:, 2 * cell_count : 3 * cell_count]
@@ -336,8 +340,7 @@
         )
     )
     seeds = lanes_to(objective_seeds, 128)[:, :, None, :]
-    out = two_retreats(as_tiles(adjoint_in), west, east, stencil, slopes, seeds)
-    return out.reshape(adjoint_in.shape)
+    return two_retreats(as_tiles(adjoint_in), west, east, stencil, slopes, seeds)
 
 
 def solution(mesh):

time: 66 us -> 67.5 us (1.023)
  other arithmetic: 2.72 us -> 5.95 us
  local copies, waits for them, and re-layouts: 10.8 us -> 8.47 us
  starting transfers between devices: 22.9 us -> 25 us
  waiting for transfers between devices: 20.5 us -> 18.5 us
    ppermute x1 -> x2, starting transfers between devices: 5.3 us -> 8.94 us  [padded(): lax.ppermute(head, axis, [((i + 1) % count, i) for i in range(count)])]
    reshape x1 -> x0, local copies, waits for them, and re-layouts: 2.7 us -> none  [staged(): return out.reshape(adjoint_in.shape)]
    ppermute x1, starting transfers between devices: 2.92 us -> 0.57 us  [halves(): lax.ppermute(head, axis, [((i + 1) % count, i) for i in range(count)])]
    ppermute x1, waiting for transfers between devices: 19.1 us -> 17.3 us  [halves(): lax.ppermute(head, axis, [((i + 1) % count, i) for i in range(count)])]
    ppermute x1, starting transfers between devices: 0.01 us -> 0.89 us  [halves(): lax.ppermute(tail, axis, [(i, (i + 1) % count) for i in range(count)])]
    select_n x1, other arithmetic: 0.02 us -> 0.77 us  [spread(): received = jnp.where(low == mask, moved, received)]
    unnamed x34 -> x40, local copies, waits for them, and re-layouts: 4.34 us -> 5.02 us
    div x1, other arithmetic: 0.08 us -> 0.77 us  [zonal_weights(): opened * (magnitude - velocity) / 12.0]
  transfers between devices with their start and end apart: 12 -> 14, of which waited for: 3 -> 2; matrix products, arithmetic and copies ran while one was open for 10% -> 19% of each run, Pallas kernels for 0% -> 0%
where the time goes in v10:
time: 67.5 us; the launch traced here: 66.9 us
  starting transfers between devices  25 us (37%)
  waiting for transfers between devices  18.5 us (27%)
  local copies, waits for them, and re-layouts  8.47 us (13%)
  Pallas kernels  7.87 us (12%)
  other arithmetic  5.95 us (9%)
  between operations  1.16 us (2%)
    ppermute x1, waiting for transfers between devices, halves(): lax.ppermute(head, axis, [((i + 1) % count, i) for i in range(count)])  17.3 us
    ppermute x7, starting transfers between devices, spread(): moved = lax.ppermute(value, axis, [(i, i ^ mask) for i in range(count)])  10 us
    ppermute x2, starting transfers between devices, padded(): lax.ppermute(head, axis, [((i + 1) % count, i) for i in range(count)])  8.94 us
    pallas_call x1, Pallas kernels, two_retreats(): pl.pallas_call(retreat_kernel, out_shape=jax.ShapeDtypeStruct((groups, tr...  7.87 us
    unnamed x40, local copies, waits for them, and re-layouts  5.02 us
    ppermute x1, starting transfers between devices, spread(): moved = lax.ppermute(value, axis, [(i, i ^ top) for i in range(count)])  2.48 us
    ppermute x2, starting transfers between devices, padded(): lax.ppermute(tail, axis, [(i, (i + 1) % count) for i in range(count)])  2.05 us
  transfers between devices with their start and end apart: 14, of which 2 were waited for; matrix products, arithmetic and copies ran while one was open for 19% of the time, Pallas kernels for 0%

profile of v10, /device:TPU:1, one launch (start us, length us, event | category | flops | bytes accessed | tf_op | source)
XLA Modules:
  0.0 66.9 jit_solution(6091285160538738624)
XLA Ops:
  1.2 2.0 %collective-permute-start.4 = (f32[4,128]{1,0:T(4,128)S(1)}, f32[4,128]{1,0:T(4,128)S(1)}, u32[]{:S(2)}, u32[]{:S(2)}) collective-permute-start(f32[4,128]{1,0:T(4,128)S(1)} %get-tuple-element.40), channel_id=1, source_target_pairs={{0,16},{16,32},{32,48},{48,64},{64,80},{80,96},{96,112},{112,128},... | collective-permute-start | bytes 6152 | tf_op jit(solution)/shard_map/ppermute | solution.py:29
  3.2 5.4 %collective-permute-start.5 = (f32[4,128]{1,0:T(4,128)S(1)}, f32[4,128]{1,0:T(4,128)S(1)}, u32[]{:S(2)}, u32[]{:S(2)}) collective-permute-start(f32[4,128]{1,0:T(4,128)S(1)} %get-tuple-element.41), channel_id=1, source_target_pairs={{16,0},{32,16},{48,32},{64,48},{80,64},{96,80},{112,96},{128,112},... | collective-permute-start | bytes 6152 | tf_op jit(solution)/shard_map/ppermute | solution.py:31
  8.6 0.7 %convert_element_type.37 = f32[16,32]{1,0:T(8,128)S(1)} convert(s32[16,32]{1,0:T(8,128)} %param.17) | non-fusion elementwise | flops 512 | bytes 4096 | tf_op jit(solution)/shard_map/convert_element_type | solution.py:263
  9.3 0.8 %convert_element_type.36 = f32[16,1024]{1,0:T(8,128)S(1)} convert(s32[16,1024]{1,0:T(8,128)} %param.12) | non-fusion elementwise | flops 16384 | bytes 131072 | tf_op jit(solution)/shard_map/convert_element_type | solution.py:258
  10.1 1.0 %concatenate.43 = f32[16,3168]{1,0:T(8,128)S(1)} concatenate(f32[16,1024]{1,0:T(8,128)S(1)} %convert_element_type.36, f32[16,1024]{1,0:T(8,128)} %param.13, f32[16,1024]{1,0:T(8,128)} %param.14, f32[16,32]{1,0:T(8,128)} %param.15, f32[16,32]{1,0:T(8,128)} %param.16, f32[16,32]{1,0:T(8,128)S(1)} %convert_element_type.37), dimensions={1} | concatenate | bytes 405504 | tf_op jit(solution)/shard_map/concatenate | solution.py:256
  11.1 2.1 %copy.10 = f32[64,8,8,128]{3,2,1,0:T(8,128)S(1)} copy(f32[64,8,8,128]{3,1,2,0:T(8,128)} %bitcast.407) | data formatting | bytes 4194304
  13.2 1.2 %fusion.51 = (f32[16,2,4,8,128]{4,3,2,1,0:T(8,128)}, f32[16,2,4,8,128]{4,3,2,1,0:T(8,128)}) fusion(f32[16,2,16,8,128]{4,3,2,1,0:T(8,128)S(1)} %bitcast.405), kind=kLoop, calls=%fused_computation.207 | loop fusion | bytes 2097152 | tf_op jit(solution)/shard_map/slice | solution.py:145
  14.6 2.5 %collective-permute-start.6 = (f32[2,24,64]{2,1,0:T(8,128)S(1)}, f32[2,24,64]{2,1,0:T(8,128)S(1)}, u32[]{:S(2)}, u32[]{:S(2)}) collective-permute-start(f32[2,24,64]{2,1,0:T(8,128)S(1)} %pad_maximum_fusion.1), channel_id=1, source_target_pairs={{0,8},{1,9},{2,10},{3,11},{4,12},{5,13},{6,14},{7,15},{8,0},{9,1},... | collective-permute-start | bytes 36872 | tf_op jit(solution)/shard_map/ppermute | solution.py:45
  17.6 1.1 %collective-permute-done.6 = f32[2,24,64]{2,1,0:T(8,128)S(1)} collective-permute-done((f32[2,24,64]{2,1,0:T(8,128)S(1)}, f32[2,24,64]{2,1,0:T(8,128)S(1)}, u32[]{:S(2)}, u32[]{:S(2)}) %collective-permute-start.6) | collective-permute-done | bytes 12320 | tf_op jit(solution)/shard_map/ppermute | solution.py:45
  18.8 2.1 %collective-permute-start.13 = (f32[2,24,64]{2,1,0:T(8,128)S(1)}, f32[2,24,64]{2,1,0:T(8,128)S(1)}, u32[]{:S(2)}, u32[]{:S(2)}) collective-permute-start(f32[2,24,64]{2,1,0:T(8,128)S(1)} %broadcast_select_fusion), channel_id=1, source_target_pairs={{0,1},{1,0},{2,3},{3,2},{4,5},{5,4},{6,7},{7,6},{8,9},{9,8},{10,11... | collective-permute-start | bytes 36872 | tf_op jit(solution)/shard_map/ppermute | solution.py:50
  20.9 1.3 %collective-permute-start.12 = (f32[2,24,64]{2,1,0:T(8,128)S(1)}, f32[2,24,64]{2,1,0:T(8,128)S(1)}, u32[]{:S(2)}, u32[]{:S(2)}) collective-permute-start(f32[2,24,64]{2,1,0:T(8,128)S(1)} %broadcast_select_fusion), channel_id=1, source_target_pairs={{0,2},{1,3},{2,0},{3,1},{4,6},{5,7},{6,4},{7,5},{8,10},{9,11},{10,... | collective-permute-start | bytes 36872 | tf_op jit(solution)/shard_map/ppermute | solution.py:50
  22.2 0.6 fusion.45
  23.2 2.9 %collective-permute-start.10 = (f32[2,24,64]{2,1,0:T(8,128)S(1)}, f32[2,24,64]{2,1,0:T(8,128)S(1)}, u32[]{:S(2)}, u32[]{:S(2)}) collective-permute-start(f32[2,24,64]{2,1,0:T(8,128)S(1)} %broadcast_select_fusion), channel_id=1, source_target_pairs={{0,4},{1,5},{2,6},{3,7},{4,0},{5,1},{6,2},{7,3},{8,12},{9,13},{10,... | collective-permute-start | bytes 36872 | tf_op jit(solution)/shard_map/ppermute | solution.py:50
  26.5 2.7 %collective-permute-start.8 = (f32[2,24,64]{2,1,0:T(8,128)S(1)}, f32[2,24,64]{2,1,0:T(8,128)}, u32[]{:S(2)}, u32[]{:S(2)}) collective-permute-start(f32[2,24,64]{2,1,0:T(8,128)S(1)} %broadcast_select_fusion), channel_id=1, source_target_pairs={{0,6},{1,7},{2,4},{3,5},{4,2},{5,3},{6,0},{7,1},{8,14},{9,15},{10,... | collective-permute-start | bytes 36872 | tf_op jit(solution)/shard_map/ppermute | solution.py:50
  30.0 3.6 %collective-permute-start.3 = (f32[4,3168]{1,0:T(4,128)S(1)}, f32[4,3168]{1,0:T(4,128)S(1)}, u32[]{:S(2)}, u32[]{:S(2)}) collective-permute-start(f32[4,3168]{1,0:T(4,128)S(1)} %get-tuple-element.35), channel_id=1, source_target_pairs={{16,0},{32,16},{48,32},{64,48},{80,64},{96,80},{112,96},{128,112},... | collective-permute-start | bytes 152072 | tf_op jit(solution)/shard_map/ppermute | solution.py:31
  33.6 0.6 copy-done.7
  34.8 0.9 %collective-permute-start = (f32[16,2,4,8,128]{4,3,2,1,0:T(8,128)}, f32[16,2,4,8,128]{4,3,2,1,0:T(8,128)}, u32[]{:S(2)}, u32[]{:S(2)}) collective-permute-start(f32[16,2,4,8,128]{4,3,2,1,0:T(8,128)} %get-tuple-element.25), channel_id=1, source_target_pairs={{0,16},{16,32},{32,48},{48,64},{64,80},{80,96},{96,112},{112,128},... | collective-permute-start | bytes 1572872 | tf_op jit(solution)/shard_map/ppermute | solution.py:147
  35.7 0.8 %select_select_fusion = f32[2,24,64]{2,1,0:T(8,128)S(1)} fusion(f32[2,24,64]{2,1,0:T(8,128)} %collective-permute-done.7, f32[2,24,64]{2,1,0:T(8,128)} %collective-permute-done.8, f32[2,24,64]{2,1,0:T(8,128)} %copy-done.7, f32[2,24,64]{2,1,0:T(8,128)} %copy-done.6, f32[2,24,64]{2,1,0:T(8,128)} %copy-done.5, f32[2,24,64]{2,1,0:T(8,128)} %copy-done.4, ...), kind=kLoop, calls=%fused_computation.49 | loop fusion | flops 27648 | bytes 122888 | tf_op jit(solution)/shard_map/jit(_where)/select_n | solution.py:51
  36.9 0.8 %fusion.3 = (f32[24,1024]{1,0:T(8,128)S(1)}, f32[24,1024]{1,0:T(8,128)S(1)}, f32[3,8,8,128]{3,1,2,0:T(8,128)S(1)}, f32[24,1024]{1,0:T(8,128)S(1)}, f32[24,1024]{1,0:T(8,128)S(1)}, /*index=5*/f32[24,1024]{1,0:T(8,128)S(1)}) fusion(f32[24,1024]{1,0:T(8,128)S(1)} %get-tuple-element.19, f32[24,3168]{1,0:T(8,128)S(1)} %pad_maximum_fusion, ...), kind=kLoop, calls=%fused_computation.11 | loop fusion | flops 516096 | bytes 1184672 | tf_op jit(solution)/shard_map/div | solution.py:105
  39.1 0.8 %copy.19 = f32[12,8,8,128]{3,2,1,0:T(8,128)} copy(f32[12,8,8,128]{3,1,2,0:T(8,128)S(1)} %bitcast.409) | data formatting | bytes 786432
  40.1 0.7 %pad.43 = f32[16,24,128]{2,1,0:T(8,128)} pad(f32[16,24,32]{2,1,0:T(8,128)S(1)} %compare_select_fusion, f32[]{:T(128)} %constant.123.clone.1), padding=0_0x0_0x0_96 | pad | bytes 245764 | tf_op jit(solution)/shard_map/jit(_pad)/pad | solution.py:155
  40.9 17.3 %collective-permute-done.1.east_ref = f32[16,2,4,8,128]{4,3,2,1,0:T(8,128)S(1)} collective-permute-done((f32[16,2,4,8,128]{4,3,2,1,0:T(8,128)}, f32[16,2,4,8,128]{4,3,2,1,0:T(8,128)S(1)}, u32[]{:S(2)}, u32[]{:S(2)}) %collective-permute-start.1) | collective-permute-done | bytes 524320 | tf_op jit(solution)/shard_map/ppermute | solution.py:148
  58.3 0.8 %copy-done.3 = f32[16,2,4,8,128]{4,3,2,1,0:T(8,128)} copy-done((f32[16,2,4,8,128]{4,3,2,1,0:T(8,128)}, f32[16,2,4,8,128]{4,3,2,1,0:T(8,128)S(1)}, u32[]{:S(2)}) %copy-start.3) | copy-done | bytes 524312
  59.1 7.9 %shard_map.91 = f32[16,2,16,1024]{3,2,1,0:T(8,128)} custom-call(f32[16,2,16,8,128]{4,3,2,1,0:T(8,128)} %bitcast.406, f32[16,2,4,8,128]{4,3,2,1,0:T(8,128)} %collective-permute-done.west_ref, f32[16,2,4,8,128]{4,3,2,1,0:T(8,128)} %copy-done.3, f32[8,24,8,128]{3,2,1,0:T(8,128)} %copy-done.2, f32[2,2,24,8,128]{4,3,2,1,0:T(8,128)} %bitcast.408, ...), custom_call_target="tpu_custom_call" | custom-call | tf_op jit(solution)/shard_map/pallas_call | solution.py:214
  (92 shorter events, 5.2 us)
Async XLA Ops:
  0.0 1.1 %copy-start = (f32[4,2,16,1024]{3,2,1,0:T(8,128)S(1)}, f32[4,2,16,1024]{3,2,1,0:T(8,128)}, u32[]{:S(2)}) copy-start(f32[4,2,16,1024]{3,2,1,0:T(8,128)} %param.10) | copy-start | bytes 1572868
  1.2 13.2 %collective-permute-start.4 = (f32[4,128]{1,0:T(4,128)S(1)}, f32[4,128]{1,0:T(4,128)S(1)}, u32[]{:S(2)}, u32[]{:S(2)}) collective-permute-start(f32[4,128]{1,0:T(4,128)S(1)} %get-tuple-element.40), channel_id=1, source_target_pairs={{0,16},{16,32},{32,48},{48,64},{64,80},{80,96},{96,112},{112,128},... | collective-permute-start | bytes 6152 | tf_op jit(solution)/shard_map/ppermute | solution.py:29
  3.2 11.2 %collective-permute-start.5 = (f32[4,128]{1,0:T(4,128)S(1)}, f32[4,128]{1,0:T(4,128)S(1)}, u32[]{:S(2)}, u32[]{:S(2)}) collective-permute-start(f32[4,128]{1,0:T(4,128)S(1)} %get-tuple-element.41), channel_id=1, source_target_pairs={{16,0},{32,16},{48,32},{64,48},{80,64},{96,80},{112,96},{128,112},... | collective-permute-start | bytes 6152 | tf_op jit(solution)/shard_map/ppermute | solution.py:31
  13.2 23.7 %copy-start.1 = (f32[64,8,8,128]{3,2,1,0:T(8,128)}, f32[64,8,8,128]{3,2,1,0:T(8,128)S(1)}, u32[]{:S(2)}) copy-start(f32[64,8,8,128]{3,2,1,0:T(8,128)S(1)} %copy.10) | copy-start | bytes 6291460
  14.6 4.2 %collective-permute-start.6 = (f32[2,24,64]{2,1,0:T(8,128)S(1)}, f32[2,24,64]{2,1,0:T(8,128)S(1)}, u32[]{:S(2)}, u32[]{:S(2)}) collective-permute-start(f32[2,24,64]{2,1,0:T(8,128)S(1)} %pad_maximum_fusion.1), channel_id=1, source_target_pairs={{0,8},{1,9},{2,10},{3,11},{4,12},{5,13},{6,14},{7,15},{8,0},{9,1},... | collective-permute-start | bytes 36872 | tf_op jit(solution)/shard_map/ppermute | solution.py:45
  18.8 7.7 %collective-permute-start.13 = (f32[2,24,64]{2,1,0:T(8,128)S(1)}, f32[2,24,64]{2,1,0:T(8,128)S(1)}, u32[]{:S(2)}, u32[]{:S(2)}) collective-permute-start(f32[2,24,64]{2,1,0:T(8,128)S(1)} %broadcast_select_fusion), channel_id=1, source_target_pairs={{0,1},{1,0},{2,3},{3,2},{4,5},{5,4},{6,7},{7,6},{8,9},{9,8},{10,11... | collective-permute-start | bytes 36872 | tf_op jit(solution)/shard_map/ppermute | solution.py:50
  20.9 8.3 %collective-permute-start.12 = (f32[2,24,64]{2,1,0:T(8,128)S(1)}, f32[2,24,64]{2,1,0:T(8,128)S(1)}, u32[]{:S(2)}, u32[]{:S(2)}) collective-permute-start(f32[2,24,64]{2,1,0:T(8,128)S(1)} %broadcast_select_fusion), channel_id=1, source_target_pairs={{0,2},{1,3},{2,0},{3,1},{4,6},{5,7},{6,4},{7,5},{8,10},{9,11},{10,... | collective-permute-start | bytes 36872 | tf_op jit(solution)/shard_map/ppermute | solution.py:50
  22.8 7.2 %collective-permute-start.11 = (f32[2,24,64]{2,1,0:T(8,128)S(1)}, f32[2,24,64]{2,1,0:T(8,128)S(1)}, u32[]{:S(2)}, u32[]{:S(2)}) collective-permute-start(f32[2,24,64]{2,1,0:T(8,128)S(1)} %broadcast_select_fusion), channel_id=1, source_target_pairs={{0,3},{1,2},{2,1},{3,0},{4,7},{5,6},{6,5},{7,4},{8,11},{9,10},{10,... | collective-permute-start | bytes 36872 | tf_op jit(solution)/shard_map/ppermute | solution.py:50
  23.2 6.8 %collective-permute-start.10 = (f32[2,24,64]{2,1,0:T(8,128)S(1)}, f32[2,24,64]{2,1,0:T(8,128)S(1)}, u32[]{:S(2)}, u32[]{:S(2)}) collective-permute-start(f32[2,24,64]{2,1,0:T(8,128)S(1)} %broadcast_select_fusion), channel_id=1, source_target_pairs={{0,4},{1,5},{2,6},{3,7},{4,0},{5,1},{6,2},{7,3},{8,12},{9,13},{10,... | collective-permute-start | bytes 36872 | tf_op jit(solution)/shard_map/ppermute | solution.py:50
  26.1 7.4 %collective-permute-start.9 = (f32[2,24,64]{2,1,0:T(8,128)S(1)}, f32[2,24,64]{2,1,0:T(8,128)S(1)}, u32[]{:S(2)}, u32[]{:S(2)}) collective-permute-start(f32[2,24,64]{2,1,0:T(8,128)S(1)} %broadcast_select_fusion), channel_id=1, source_target_pairs={{0,5},{1,4},{2,7},{3,6},{4,1},{5,0},{6,3},{7,2},{8,13},{9,12},{10,... | collective-permute-start | bytes 36872 | tf_op jit(solution)/shard_map/ppermute | solution.py:50
  26.5 8.3 %collective-permute-start.8 = (f32[2,24,64]{2,1,0:T(8,128)S(1)}, f32[2,24,64]{2,1,0:T(8,128)}, u32[]{:S(2)}, u32[]{:S(2)}) collective-permute-start(f32[2,24,64]{2,1,0:T(8,128)S(1)} %broadcast_select_fusion), channel_id=1, source_target_pairs={{0,6},{1,7},{2,4},{3,5},{4,2},{5,3},{6,0},{7,1},{8,14},{9,15},{10,... | collective-permute-start | bytes 36872 | tf_op jit(solution)/shard_map/ppermute | solution.py:50
  29.2 4.3 %copy-start.4 = (f32[2,24,64]{2,1,0:T(8,128)}, f32[2,24,64]{2,1,0:T(8,128)S(1)}, u32[]{:S(2)}) copy-start(f32[2,24,64]{2,1,0:T(8,128)S(1)} %collective-permute-done.12) | copy-start | bytes 36868
  29.2 6.4 %collective-permute-start.7 = (f32[2,24,64]{2,1,0:T(8,128)S(1)}, f32[2,24,64]{2,1,0:T(8,128)}, u32[]{:S(2)}, u32[]{:S(2)}) collective-permute-start(f32[2,24,64]{2,1,0:T(8,128)S(1)} %broadcast_select_fusion), channel_id=1, source_target_pairs={{0,7},{1,6},{2,5},{3,4},{4,3},{5,2},{6,1},{7,0},{8,15},{9,14},{10,... | collective-permute-start | bytes 36872 | tf_op jit(solution)/shard_map/ppermute | solution.py:50
  30.0 3.6 %copy-start.5 = (f32[2,24,64]{2,1,0:T(8,128)}, f32[2,24,64]{2,1,0:T(8,128)S(1)}, u32[]{:S(2)}) copy-start(f32[2,24,64]{2,1,0:T(8,128)S(1)} %collective-permute-done.11) | copy-start | bytes 36868
  30.0 6.6 %collective-permute-start.2 = (f32[4,3168]{1,0:T(4,128)S(1)}, f32[4,3168]{1,0:T(4,128)S(1)}, u32[]{:S(2)}, u32[]{:S(2)}) collective-permute-start(f32[4,3168]{1,0:T(4,128)S(1)} %get-tuple-element.34), channel_id=1, source_target_pairs={{0,16},{16,32},{32,48},{48,64},{64,80},{80,96},{96,112},{112,128},... | collective-permute-start | bytes 152072 | tf_op jit(solution)/shard_map/ppermute | solution.py:29
  30.0 3.6 %copy-start.6 = (f32[2,24,64]{2,1,0:T(8,128)}, f32[2,24,64]{2,1,0:T(8,128)S(1)}, u32[]{:S(2)}) copy-start(f32[2,24,64]{2,1,0:T(8,128)S(1)} %collective-permute-done.10) | copy-start | bytes 36868
  30.0 6.6 %collective-permute-start.3 = (f32[4,3168]{1,0:T(4,128)S(1)}, f32[4,3168]{1,0:T(4,128)S(1)}, u32[]{:S(2)}, u32[]{:S(2)}) collective-permute-start(f32[4,3168]{1,0:T(4,128)S(1)} %get-tuple-element.35), channel_id=1, source_target_pairs={{16,0},{32,16},{48,32},{64,48},{80,64},{96,80},{112,96},{128,112},... | collective-permute-start | bytes 152072 | tf_op jit(solution)/shard_map/ppermute | solution.py:31
  33.6 0.6 copy-start.7
  34.2 24.1 %collective-permute-start.1 = (f32[16,2,4,8,128]{4,3,2,1,0:T(8,128)}, f32[16,2,4,8,128]{4,3,2,1,0:T(8,128)S(1)}, u32[]{:S(2)}, u32[]{:S(2)}) collective-permute-start(f32[16,2,4,8,128]{4,3,2,1,0:T(8,128)} %get-tuple-element.24), channel_id=1, source_target_pairs={{16,0},{32,16},{48,32},{64,48},{80,64},{96,80},{112,96},{128,112},... | collective-permute-start | bytes 1572872 | tf_op jit(solution)/shard_map/ppermute | solution.py:148
  34.8 23.5 %collective-permute-start = (f32[16,2,4,8,128]{4,3,2,1,0:T(8,128)}, f32[16,2,4,8,128]{4,3,2,1,0:T(8,128)}, u32[]{:S(2)}, u32[]{:S(2)}) collective-permute-start(f32[16,2,4,8,128]{4,3,2,1,0:T(8,128)} %get-tuple-element.25), channel_id=1, source_target_pairs={{0,16},{16,32},{32,48},{48,64},{64,80},{80,96},{96,112},{112,128},... | collective-permute-start | bytes 1572872 | tf_op jit(solution)/shard_map/ppermute | solution.py:147
  38.3 1.8 %copy-start.8 = (f32[16]{0:T(128)S(1)}, f32[16]{0:T(128)}, u32[]{:S(2)}) copy-start(f32[16]{0:T(128)} %add_convert_fusion) | copy-start | bytes 196
  40.9 17.4 %copy-start.2 = (f32[8,24,8,128]{3,2,1,0:T(8,128)}, f32[8,24,8,128]{3,2,1,0:T(8,128)S(1)}, u32[]{:S(2)}) copy-start(f32[8,24,8,128]{3,2,1,0:T(8,128)S(1)} %bitcast_dynamic-update-slice_fusion.w_ref) | copy-start | bytes 2359300
  58.3 0.8 %copy-start.3 = (f32[16,2,4,8,128]{4,3,2,1,0:T(8,128)}, f32[16,2,4,8,128]{4,3,2,1,0:T(8,128)S(1)}, u32[]{:S(2)}) copy-start(f32[16,2,4,8,128]{4,3,2,1,0:T(8,128)S(1)} %collective-permute-done.1.east_ref) | copy-start | bytes 1572868

commit v11 on v10

--- a/solution.py
+++ b/solution.py
@@ -210,7 +210,7 @@
     groups, tracers, local, sub, lanes = center.shape
     rim = west.shape[2]
     span = local + 2 * rim
-    pack = 4 if groups % 4 == 0 else 1
+    pack = 8 if groups % 8 == 0 else 1
     return pl.pallas_call(
         retreat_kernel,
         out_shape=jax.ShapeDtypeStruct((groups, tracers, local, sub * lanes), center.dtype),
@@ -245,16 +245,10 @@
     owner_index = interval[0] % owners
     band = 2 * ROWS
     stored = lax.dynamic_index_in_dim(checkpoint_store, interval[0] // owners, 0, keepdims=False)
-    band_wide = padded(
-        jnp.concatenate([stored[0, :, :band], stored[1, :, :band]], axis=1),
-        (("tile", 0),),
-        rim_depth,
-    )
-    initial_wide = spread(
-        jnp.stack([band_wide[:, :band], band_wide[:, band : 2 * band]]), "obj", owner_index
-    )
     statics = jnp.concatenate(
         [
+            stored[0, :, :band],
+            stored[1, :, :band],
             sea_mask.astype(jnp.float32),
             zonal_speed,
             mixing,
@@ -265,6 +259,10 @@
         axis=1,
     )
     widened = padded(statics, (("tile", 0),), rim_depth)
+    initial_wide = spread(
+        jnp.stack([widened[:, :band], widened[:, band : 2 * band]]), "obj", owner_index
+    )
+    widened = widened[:, 2 * band :]
     sea_wide = widened[:, :cell_count]
     speed_wide = widened[:, cell_count : 2 * cell_count]
     mixing_wide = widened[:, 2 * cell_count : 3 * cell_count]

time: 67.5 us -> 63.7 us (0.944)
  other arithmetic: 5.95 us -> 2.72 us
  starting transfers between devices: 25 us -> 22.9 us
  waiting for transfers between devices: 18.5 us -> 20.4 us
    ppermute x2 -> x1, starting transfers between devices: 8.94 us -> 5.3 us  [padded(): lax.ppermute(head, axis, [((i + 1) % count, i) for i in range(count)])]
    ppermute x1, starting transfers between devices: 0.57 us -> 2.93 us  [halves(): lax.ppermute(head, axis, [((i + 1) % count, i) for i in range(count)])]
    ppermute x1, waiting for transfers between devices: 17.3 us -> 19.1 us  [halves(): lax.ppermute(head, axis, [((i + 1) % count, i) for i in range(count)])]
    ppermute x1, starting transfers between devices: 0.89 us -> 0.01 us  [halves(): lax.ppermute(tail, axis, [(i, (i + 1) % count) for i in range(count)])]
    select_n x1, other arithmetic: 0.77 us -> 0.02 us  [spread(): received = jnp.where(low == mask, moved, received)]
    unnamed x40 -> x34, local copies, waits for them, and re-layouts: 5.02 us -> 4.34 us
    div x1, other arithmetic: 0.77 us -> 0.08 us  [zonal_weights(): opened * (magnitude - velocity) / 12.0]
    ppermute x2 -> x1, starting transfers between devices: 2.05 us -> 2.03 us  [padded(): lax.ppermute(tail, axis, [(i, (i + 1) % count) for i in range(count)])]
  transfers between devices with their start and end apart: 14 -> 12, of which waited for: 2 -> 3; matrix products, arithmetic and copies ran while one was open for 19% -> 10% of each run, Pallas kernels for 0% -> 0%
where the time goes in v11:
time: 63.7 us; the launch traced here: 63.4 us
  starting transfers between devices  22.9 us (36%)
  waiting for transfers between devices  20.4 us (32%)
  Pallas kernels  8.14 us (13%)
  local copies, waits for them, and re-layouts  8.11 us (13%)
  other arithmetic  2.72 us (4%)
  between operations  1.13 us (2%)
    ppermute x1, waiting for transfers between devices, halves(): lax.ppermute(head, axis, [((i + 1) % count, i) for i in range(count)])  19.1 us
    ppermute x7, starting transfers between devices, spread(): moved = lax.ppermute(value, axis, [(i, i ^ mask) for i in range(count)])  10.1 us
    pallas_call x1, Pallas kernels, two_retreats(): pl.pallas_call(retreat_kernel, out_shape=jax.ShapeDtypeStruct((groups, tr...  8.14 us
    ppermute x1, starting transfers between devices, padded(): lax.ppermute(head, axis, [((i + 1) % count, i) for i in range(count)])  5.3 us
    unnamed x34, local copies, waits for them, and re-layouts  4.34 us
    ppermute x1, starting transfers between devices, halves(): lax.ppermute(head, axis, [((i + 1) % count, i) for i in range(count)])  2.93 us
    ppermute x1, starting transfers between devices, spread(): moved = lax.ppermute(value, axis, [(i, i ^ top) for i in range(count)])  2.53 us
    ppermute x1, starting transfers between devices, padded(): lax.ppermute(tail, axis, [(i, (i + 1) % count) for i in range(count)])  2.03 us
  transfers between devices with their start and end apart: 12, of which 3 were waited for; matrix products, arithmetic and copies ran while one was open for 10% of the time, Pallas kernels for 0%

profile of v11, /device:TPU:1, one launch (start us, length us, event | category | flops | bytes accessed | tf_op | source)
XLA Modules:
  0.0 63.4 jit_solution(12203276732175294651)
XLA Ops:
  0.7 0.7 %convert_element_type.37 = f32[16,32]{1,0:T(8,128)S(1)} convert(s32[16,32]{1,0:T(8,128)} %param.17) | non-fusion elementwise | flops 512 | bytes 4096 | tf_op jit(solution)/shard_map/convert_element_type | solution.py:257
  1.4 0.8 %convert_element_type.36 = f32[16,1024]{1,0:T(8,128)S(1)} convert(s32[16,1024]{1,0:T(8,128)} %param.12) | non-fusion elementwise | flops 16384 | bytes 131072 | tf_op jit(solution)/shard_map/convert_element_type | solution.py:252
  2.3 1.0 %concatenate.37 = f32[16,3296]{1,0:T(8,128)S(1)} concatenate(f32[16,64]{1,0:T(8,128)S(1)} %get-tuple-element.39, f32[16,64]{1,0:T(8,128)S(1)} %get-tuple-element.38, f32[16,1024]{1,0:T(8,128)S(1)} %convert_element_type.36, f32[16,1024]{1,0:T(8,128)} %param.13, f32[16,1024]{1,0:T(8,128)} %param.14, f32[16,32]{1,0:T(8,128)} %param.15, f32[16,32]{1,0:T(8,128)} %param.16, ...), dimensions={1} | concatenate | bytes 421888 | tf_op jit(solution)/shard_map/concatenate | solution.py:248
  3.3 0.6 %fusion.52 = (f32[4,3296]{1,0:T(4,128)}, f32[4,3296]{1,0:T(4,128)S(1)}) fusion(f32[16,3296]{1,0:T(8,128)S(1)} %concatenate.37), kind=kLoop, calls=%fused_computation.205 | loop fusion | bytes 210944 | tf_op jit(solution)/shard_map/slice | solution.py:26
  3.9 2.0 %collective-permute-start.2 = (f32[4,3296]{1,0:T(4,128)}, f32[4,3296]{1,0:T(4,128)S(1)}, u32[]{:S(2)}, u32[]{:S(2)}) collective-permute-start(f32[4,3296]{1,0:T(4,128)} %get-tuple-element.36), channel_id=1, source_target_pairs={{0,16},{16,32},{32,48},{48,64},{64,80},{80,96},{96,112},{112,128},... | collective-permute-start | bytes 158216 | tf_op jit(solution)/shard_map/ppermute | solution.py:29
  6.0 5.3 %collective-permute-start.3 = (f32[4,3296]{1,0:T(4,128)S(1)}, f32[4,3296]{1,0:T(4,128)S(1)}, u32[]{:S(2)}, u32[]{:S(2)}) collective-permute-start(f32[4,3296]{1,0:T(4,128)S(1)} %get-tuple-element.37), channel_id=1, source_target_pairs={{16,0},{32,16},{48,32},{64,48},{80,64},{96,80},{112,96},{128,112},... | collective-permute-start | bytes 158216 | tf_op jit(solution)/shard_map/ppermute | solution.py:31
  11.3 2.1 %copy.10 = f32[64,8,8,128]{3,2,1,0:T(8,128)S(1)} copy(f32[64,8,8,128]{3,1,2,0:T(8,128)} %bitcast.407) | data formatting | bytes 4194304
  13.3 0.9 %fusion.51 = (f32[16,2,4,8,128]{4,3,2,1,0:T(8,128)}, f32[16,2,4,8,128]{4,3,2,1,0:T(8,128)S(1)}) fusion(f32[16,2,16,8,128]{4,3,2,1,0:T(8,128)S(1)} %bitcast.405), kind=kLoop, calls=%fused_computation.204 | loop fusion | bytes 2097152 | tf_op jit(solution)/shard_map/slice | solution.py:145
  14.6 2.5 %collective-permute-start.4 = (f32[2,24,64]{2,1,0:T(8,128)S(1)}, f32[2,24,64]{2,1,0:T(8,128)S(1)}, u32[]{:S(2)}, u32[]{:S(2)}) collective-permute-start(f32[2,24,64]{2,1,0:T(8,128)S(1)} %pad_maximum_fusion.1), channel_id=1, source_target_pairs={{0,8},{1,9},{2,10},{3,11},{4,12},{5,13},{6,14},{7,15},{8,0},{9,1},... | collective-permute-start | bytes 36872 | tf_op jit(solution)/shard_map/ppermute | solution.py:45
  18.1 0.8 %collective-permute-done.4 = f32[2,24,64]{2,1,0:T(8,128)S(1)} collective-permute-done((f32[2,24,64]{2,1,0:T(8,128)S(1)}, f32[2,24,64]{2,1,0:T(8,128)S(1)}, u32[]{:S(2)}, u32[]{:S(2)}) %collective-permute-start.4) | collective-permute-done | bytes 12320 | tf_op jit(solution)/shard_map/ppermute | solution.py:45
  18.9 2.1 %collective-permute-start.11 = (f32[2,24,64]{2,1,0:T(8,128)S(1)}, f32[2,24,64]{2,1,0:T(8,128)S(1)}, u32[]{:S(2)}, u32[]{:S(2)}) collective-permute-start(f32[2,24,64]{2,1,0:T(8,128)S(1)} %broadcast_select_fusion), channel_id=1, source_target_pairs={{0,1},{1,0},{2,3},{3,2},{4,5},{5,4},{6,7},{7,6},{8,9},{9,8},{10,11... | collective-permute-start | bytes 36872 | tf_op jit(solution)/shard_map/ppermute | solution.py:50
  21.0 1.3 %collective-permute-start.10 = (f32[2,24,64]{2,1,0:T(8,128)S(1)}, f32[2,24,64]{2,1,0:T(8,128)S(1)}, u32[]{:S(2)}, u32[]{:S(2)}) collective-permute-start(f32[2,24,64]{2,1,0:T(8,128)S(1)} %broadcast_select_fusion), channel_id=1, source_target_pairs={{0,2},{1,3},{2,0},{3,1},{4,6},{5,7},{6,4},{7,5},{8,10},{9,11},{10,... | collective-permute-start | bytes 36872 | tf_op jit(solution)/shard_map/ppermute | solution.py:50
  22.3 0.5 collective-permute-start.9
  22.9 2.9 %collective-permute-start.8 = (f32[2,24,64]{2,1,0:T(8,128)S(1)}, f32[2,24,64]{2,1,0:T(8,128)S(1)}, u32[]{:S(2)}, u32[]{:S(2)}) collective-permute-start(f32[2,24,64]{2,1,0:T(8,128)S(1)} %broadcast_select_fusion), channel_id=1, source_target_pairs={{0,4},{1,5},{2,6},{3,7},{4,0},{5,1},{6,2},{7,3},{8,12},{9,13},{10,... | collective-permute-start | bytes 36872 | tf_op jit(solution)/shard_map/ppermute | solution.py:50
  25.8 0.4 collective-permute-start.7
  26.1 2.7 %collective-permute-start.6 = (f32[2,24,64]{2,1,0:T(8,128)S(1)}, f32[2,24,64]{2,1,0:T(8,128)S(1)}, u32[]{:S(2)}, u32[]{:S(2)}) collective-permute-start(f32[2,24,64]{2,1,0:T(8,128)S(1)} %broadcast_select_fusion), channel_id=1, source_target_pairs={{0,6},{1,7},{2,4},{3,5},{4,2},{5,3},{6,0},{7,1},{8,14},{9,15},{10,... | collective-permute-start | bytes 36872 | tf_op jit(solution)/shard_map/ppermute | solution.py:50
  29.1 0.7 %pad.43 = f32[16,24,128]{2,1,0:T(8,128)} pad(f32[16,24,32]{2,1,0:T(8,128)S(1)} %compare_select_fusion, f32[]{:T(128)} %constant.128.clone.1), padding=0_0x0_0x0_96 | pad | bytes 245764 | tf_op jit(solution)/shard_map/jit(_pad)/pad | solution.py:155
  29.9 2.9 %collective-permute-start.1 = (f32[16,2,4,8,128]{4,3,2,1,0:T(8,128)S(1)}, f32[16,2,4,8,128]{4,3,2,1,0:T(8,128)S(1)}, u32[]{:S(2)}, u32[]{:S(2)}) collective-permute-start(f32[16,2,4,8,128]{4,3,2,1,0:T(8,128)S(1)} %copy-done.5), channel_id=1, source_target_pairs={{16,0},{32,16},{48,32},{64,48},{80,64},{96,80},{112,96},{128,112},... | collective-permute-start | bytes 1572872 | tf_op jit(solution)/shard_map/ppermute | solution.py:148
  32.8 0.5 collective-permute-done.5
  33.9 0.3 add_bitcast_fusion.3
  34.4 0.8 %copy.19 = f32[12,8,8,128]{3,2,1,0:T(8,128)} copy(f32[12,8,8,128]{3,1,2,0:T(8,128)S(1)} %bitcast.409) | data formatting | bytes 786432
  35.2 19.1 %collective-permute-done.1.east_ref = f32[16,2,4,8,128]{4,3,2,1,0:T(8,128)S(1)} collective-permute-done((f32[16,2,4,8,128]{4,3,2,1,0:T(8,128)S(1)}, f32[16,2,4,8,128]{4,3,2,1,0:T(8,128)S(1)}, u32[]{:S(2)}, u32[]{:S(2)}) %collective-permute-start.1) | collective-permute-done | bytes 524320 | tf_op jit(solution)/shard_map/ppermute | solution.py:148
  54.3 0.8 %copy-done.3 = f32[16,2,4,8,128]{4,3,2,1,0:T(8,128)} copy-done((f32[16,2,4,8,128]{4,3,2,1,0:T(8,128)}, f32[16,2,4,8,128]{4,3,2,1,0:T(8,128)S(1)}, u32[]{:S(2)}) %copy-start.3) | copy-done | bytes 524312
  55.3 8.1 %shard_map.91 = f32[16,2,16,1024]{3,2,1,0:T(8,128)} custom-call(f32[16,2,16,8,128]{4,3,2,1,0:T(8,128)} %bitcast.406, f32[16,2,4,8,128]{4,3,2,1,0:T(8,128)} %copy-done.4, f32[16,2,4,8,128]{4,3,2,1,0:T(8,128)} %copy-done.3, f32[8,24,8,128]{3,2,1,0:T(8,128)} %copy-done.2, f32[2,2,24,8,128]{4,3,2,1,0:T(8,128)} %bitcast.408, f32[16,24,1,128]{3,2,1,0:T(1,128)} %bitcast.414), custom_call_target="tpu_custom_call" | custom-call | tf_op jit(solution)/shard_map/pallas_call | solution.py:214
  (80 shorter events, 2.3 us)
Async XLA Ops:
  0.0 2.3 %copy-start = (f32[4,2,16,1024]{3,2,1,0:T(8,128)S(1)}, f32[4,2,16,1024]{3,2,1,0:T(8,128)}, u32[]{:S(2)}) copy-start(f32[4,2,16,1024]{3,2,1,0:T(8,128)} %param.10) | copy-start | bytes 1572868
  3.9 10.4 %collective-permute-start.2 = (f32[4,3296]{1,0:T(4,128)}, f32[4,3296]{1,0:T(4,128)S(1)}, u32[]{:S(2)}, u32[]{:S(2)}) collective-permute-start(f32[4,3296]{1,0:T(4,128)} %get-tuple-element.36), channel_id=1, source_target_pairs={{0,16},{16,32},{32,48},{48,64},{64,80},{80,96},{96,112},{112,128},... | collective-permute-start | bytes 158216 | tf_op jit(solution)/shard_map/ppermute | solution.py:29
  6.0 8.3 %collective-permute-start.3 = (f32[4,3296]{1,0:T(4,128)S(1)}, f32[4,3296]{1,0:T(4,128)S(1)}, u32[]{:S(2)}, u32[]{:S(2)}) collective-permute-start(f32[4,3296]{1,0:T(4,128)S(1)} %get-tuple-element.37), channel_id=1, source_target_pairs={{16,0},{32,16},{48,32},{64,48},{80,64},{96,80},{112,96},{128,112},... | collective-permute-start | bytes 158216 | tf_op jit(solution)/shard_map/ppermute | solution.py:31
  13.3 3.9 %copy-start.1 = (f32[64,8,8,128]{3,2,1,0:T(8,128)}, f32[64,8,8,128]{3,2,1,0:T(8,128)S(1)}, u32[]{:S(2)}) copy-start(f32[64,8,8,128]{3,2,1,0:T(8,128)S(1)} %copy.10) | copy-start | bytes 6291460
  14.6 4.3 %collective-permute-start.4 = (f32[2,24,64]{2,1,0:T(8,128)S(1)}, f32[2,24,64]{2,1,0:T(8,128)S(1)}, u32[]{:S(2)}, u32[]{:S(2)}) collective-permute-start(f32[2,24,64]{2,1,0:T(8,128)S(1)} %pad_maximum_fusion.1), channel_id=1, source_target_pairs={{0,8},{1,9},{2,10},{3,11},{4,12},{5,13},{6,14},{7,15},{8,0},{9,1},... | collective-permute-start | bytes 36872 | tf_op jit(solution)/shard_map/ppermute | solution.py:45
  17.6 12.3 %copy-start.5 = (f32[16,2,4,8,128]{4,3,2,1,0:T(8,128)S(1)}, f32[16,2,4,8,128]{4,3,2,1,0:T(8,128)}, u32[]{:S(2)}) copy-start(f32[16,2,4,8,128]{4,3,2,1,0:T(8,128)} %get-tuple-element.24) | copy-start | bytes 1572868
  18.9 7.2 %collective-permute-start.11 = (f32[2,24,64]{2,1,0:T(8,128)S(1)}, f32[2,24,64]{2,1,0:T(8,128)S(1)}, u32[]{:S(2)}, u32[]{:S(2)}) collective-permute-start(f32[2,24,64]{2,1,0:T(8,128)S(1)} %broadcast_select_fusion), channel_id=1, source_target_pairs={{0,1},{1,0},{2,3},{3,2},{4,5},{5,4},{6,7},{7,6},{8,9},{9,8},{10,11... | collective-permute-start | bytes 36872 | tf_op jit(solution)/shard_map/ppermute | solution.py:50
  21.0 7.9 %collective-permute-start.10 = (f32[2,24,64]{2,1,0:T(8,128)S(1)}, f32[2,24,64]{2,1,0:T(8,128)S(1)}, u32[]{:S(2)}, u32[]{:S(2)}) collective-permute-start(f32[2,24,64]{2,1,0:T(8,128)S(1)} %broadcast_select_fusion), channel_id=1, source_target_pairs={{0,2},{1,3},{2,0},{3,1},{4,6},{5,7},{6,4},{7,5},{8,10},{9,11},{10,... | collective-permute-start | bytes 36872 | tf_op jit(solution)/shard_map/ppermute | solution.py:50
  22.3 7.5 %collective-permute-start.9 = (f32[2,24,64]{2,1,0:T(8,128)S(1)}, f32[2,24,64]{2,1,0:T(8,128)S(1)}, u32[]{:S(2)}, u32[]{:S(2)}) collective-permute-start(f32[2,24,64]{2,1,0:T(8,128)S(1)} %broadcast_select_fusion), channel_id=1, source_target_pairs={{0,3},{1,2},{2,1},{3,0},{4,7},{5,6},{6,5},{7,4},{8,11},{9,10},{10,... | collective-permute-start | bytes 36872 | tf_op jit(solution)/shard_map/ppermute | solution.py:50
  22.9 9.9 %collective-permute-start.8 = (f32[2,24,64]{2,1,0:T(8,128)S(1)}, f32[2,24,64]{2,1,0:T(8,128)S(1)}, u32[]{:S(2)}, u32[]{:S(2)}) collective-permute-start(f32[2,24,64]{2,1,0:T(8,128)S(1)} %broadcast_select_fusion), channel_id=1, source_target_pairs={{0,4},{1,5},{2,6},{3,7},{4,0},{5,1},{6,2},{7,3},{8,12},{9,13},{10,... | collective-permute-start | bytes 36872 | tf_op jit(solution)/shard_map/ppermute | solution.py:50
  25.8 7.0 %collective-permute-start.7 = (f32[2,24,64]{2,1,0:T(8,128)S(1)}, f32[2,24,64]{2,1,0:T(8,128)S(1)}, u32[]{:S(2)}, u32[]{:S(2)}) collective-permute-start(f32[2,24,64]{2,1,0:T(8,128)S(1)} %broadcast_select_fusion), channel_id=1, source_target_pairs={{0,5},{1,4},{2,7},{3,6},{4,1},{5,0},{6,3},{7,2},{8,13},{9,12},{10,... | collective-permute-start | bytes 36872 | tf_op jit(solution)/shard_map/ppermute | solution.py:50
  26.1 6.7 %collective-permute-start.6 = (f32[2,24,64]{2,1,0:T(8,128)S(1)}, f32[2,24,64]{2,1,0:T(8,128)S(1)}, u32[]{:S(2)}, u32[]{:S(2)}) collective-permute-start(f32[2,24,64]{2,1,0:T(8,128)S(1)} %broadcast_select_fusion), channel_id=1, source_target_pairs={{0,6},{1,7},{2,4},{3,5},{4,2},{5,3},{6,0},{7,1},{8,14},{9,15},{10,... | collective-permute-start | bytes 36872 | tf_op jit(solution)/shard_map/ppermute | solution.py:50
  28.9 4.5 %collective-permute-start.5 = (f32[2,24,64]{2,1,0:T(8,128)S(1)}, f32[2,24,64]{2,1,0:T(8,128)S(1)}, u32[]{:S(2)}, u32[]{:S(2)}) collective-permute-start(f32[2,24,64]{2,1,0:T(8,128)S(1)} %broadcast_select_fusion), channel_id=1, source_target_pairs={{0,7},{1,6},{2,5},{3,4},{4,3},{5,2},{6,1},{7,0},{8,15},{9,14},{10,... | collective-permute-start | bytes 36872 | tf_op jit(solution)/shard_map/ppermute | solution.py:50
  29.1 25.2 %copy-start.2 = (f32[8,24,8,128]{3,2,1,0:T(8,128)}, f32[8,24,8,128]{3,2,1,0:T(8,128)S(1)}, u32[]{:S(2)}) copy-start(f32[8,24,8,128]{3,2,1,0:T(8,128)S(1)} %bitcast_dynamic-update-slice_fusion.w_ref) | copy-start | bytes 2359300
  29.9 24.4 %collective-permute-start.1 = (f32[16,2,4,8,128]{4,3,2,1,0:T(8,128)S(1)}, f32[16,2,4,8,128]{4,3,2,1,0:T(8,128)S(1)}, u32[]{:S(2)}, u32[]{:S(2)}) collective-permute-start(f32[16,2,4,8,128]{4,3,2,1,0:T(8,128)S(1)} %copy-done.5), channel_id=1, source_target_pairs={{16,0},{32,16},{48,32},{64,48},{80,64},{96,80},{112,96},{128,112},... | collective-permute-start | bytes 1572872 | tf_op jit(solution)/shard_map/ppermute | solution.py:148
  32.8 21.5 %collective-permute-start = (f32[16,2,4,8,128]{4,3,2,1,0:T(8,128)S(1)}, f32[16,2,4,8,128]{4,3,2,1,0:T(8,128)S(1)}, u32[]{:S(2)}, u32[]{:S(2)}) collective-permute-start(f32[16,2,4,8,128]{4,3,2,1,0:T(8,128)S(1)} %get-tuple-element.25), channel_id=1, source_target_pairs={{0,16},{16,32},{32,48},{48,64},{64,80},{80,96},{96,112},{112,128},... | collective-permute-start | bytes 1572872 | tf_op jit(solution)/shard_map/ppermute | solution.py:147
  54.3 0.8 %copy-start.3 = (f32[16,2,4,8,128]{4,3,2,1,0:T(8,128)}, f32[16,2,4,8,128]{4,3,2,1,0:T(8,128)S(1)}, u32[]{:S(2)}) copy-start(f32[16,2,4,8,128]{4,3,2,1,0:T(8,128)S(1)} %collective-permute-done.1.east_ref) | copy-start | bytes 1572868
  54.3 1.0 %copy-start.4 = (f32[16,2,4,8,128]{4,3,2,1,0:T(8,128)}, f32[16,2,4,8,128]{4,3,2,1,0:T(8,128)S(1)}, u32[]{:S(2)}) copy-start(f32[16,2,4,8,128]{4,3,2,1,0:T(8,128)S(1)} %collective-permute-done.west_ref) | copy-start | bytes 1572868

commit v12 on v11

--- a/solution.py
+++ b/solution.py
@@ -210,7 +210,7 @@
     groups, tracers, local, sub, lanes = center.shape
     rim = west.shape[2]
     span = local + 2 * rim
-    pack = 8 if groups % 8 == 0 else 1
+    pack = 4 if groups % 4 == 0 else 1
     return pl.pallas_call(
         retreat_kernel,
         out_shape=jax.ShapeDtypeStruct((groups, tracers, local, sub * lanes), center.dtype),
@@ -297,7 +297,8 @@
     _, slopes_second = surface_slopes(
         following[0, :, :ROWS], following[1, :, :ROWS], piston_inner, sea_inner
     )
-    west, east = halves(as_tiles(adjoint_in), "tile", 2, rim_depth)
+    west, east = halves(adjoint_in, "tile", 2, rim_depth)
+    west, east = as_tiles(west), as_tiles(east)
     span = adjoint_in.shape[2] + 2 * rim_depth
 
     def along(source, lead):
@@ -338,7 +339,8 @@
         )
     )
     seeds = lanes_to(objective_seeds, 128)[:, :, None, :]
-    return two_retreats(as_tiles(adjoint_in), west, east, stencil, slopes, seeds)
+    center = as_tiles(adjoint_in)
+    return two_retreats(center, west, east, stencil, slopes, seeds)
 
 
 def solution(mesh):

time: 63.7 us -> 66.9 us (1.050)
  local copies, waits for them, and re-layouts: 8.11 us -> 12.2 us
  waiting for transfers between devices: 20.4 us -> 19.1 us
  starting transfers between devices: 22.9 us -> 23.6 us
    ppermute x1, waiting for transfers between devices: 19.1 us -> 0.92 us  [halves(): lax.ppermute(head, axis, [((i + 1) % count, i) for i in range(count)])]
    ppermute x1, waiting for transfers between devices: 0.01 us -> 17.3 us  [halves(): lax.ppermute(tail, axis, [(i, (i + 1) % count) for i in range(count)])]
    slice x1, local copies, waits for them, and re-layouts: 0.94 us -> 2.74 us  [halves(): head = lax.slice_in_dim(cells, 0, width, axis=dim)]
    reshape x0 -> x2, local copies, waits for them, and re-layouts: none -> 1.72 us  [as_tiles(): return source.reshape(source.shape[:-1] + (source.shape[-1] // 128, 128))]
    unnamed x34 -> x32, local copies, waits for them, and re-layouts: 4.34 us -> 4.9 us
  transfers between devices with their start and end apart: 12 -> 12, of which waited for: 3 -> 3; matrix products, arithmetic and copies ran while one was open for 10% -> 16% of each run, Pallas kernels for 0% -> 0%
where the time goes in v12:
time: 66.9 us; the launch traced here: 66.6 us
  starting transfers between devices  23.6 us (35%)
  waiting for transfers between devices  19.1 us (29%)
  local copies, waits for them, and re-layouts  12.2 us (18%)
  Pallas kernels  7.87 us (12%)
  other arithmetic  2.73 us (4%)
  between operations  1.12 us (2%)
    ppermute x1, waiting for transfers between devices, halves(): lax.ppermute(tail, axis, [(i, (i + 1) % count) for i in range(count)])  17.3 us
    ppermute x7, starting transfers between devices, spread(): moved = lax.ppermute(value, axis, [(i, i ^ mask) for i in range(count)])  10.1 us
    pallas_call x1, Pallas kernels, two_retreats(): pl.pallas_call(retreat_kernel, out_shape=jax.ShapeDtypeStruct((groups, tr...  7.87 us
    ppermute x1, starting transfers between devices, padded(): lax.ppermute(head, axis, [((i + 1) % count, i) for i in range(count)])  5.3 us
    unnamed x32, local copies, waits for them, and re-layouts  4.9 us
    ppermute x1, starting transfers between devices, halves(): lax.ppermute(head, axis, [((i + 1) % count, i) for i in range(count)])  3.57 us
    slice x1, local copies, waits for them, and re-layouts, halves(): head = lax.slice_in_dim(cells, 0, width, axis=dim)  2.74 us
    ppermute x1, starting transfers between devices, spread(): moved = lax.ppermute(value, axis, [(i, i ^ top) for i in range(count)])  2.53 us
  transfers between devices with their start and end apart: 12, of which 3 were waited for; matrix products, arithmetic and copies ran while one was open for 16% of the time, Pallas kernels for 0%

profile of v12, /device:TPU:1, one launch (start us, length us, event | category | flops | bytes accessed | tf_op | source)
XLA Modules:
  0.0 66.6 jit_solution(18067588221868676903)
XLA Ops:
  0.7 0.7 %convert_element_type.37 = f32[16,32]{1,0:T(8,128)S(1)} convert(s32[16,32]{1,0:T(8,128)} %param.17) | non-fusion elementwise | flops 512 | bytes 4096 | tf_op jit(solution)/shard_map/convert_element_type | solution.py:257
  1.4 0.8 %convert_element_type.36 = f32[16,1024]{1,0:T(8,128)S(1)} convert(s32[16,1024]{1,0:T(8,128)} %param.12) | non-fusion elementwise | flops 16384 | bytes 131072 | tf_op jit(solution)/shard_map/convert_element_type | solution.py:252
  2.3 1.0 %concatenate.37 = f32[16,3296]{1,0:T(8,128)S(1)} concatenate(f32[16,64]{1,0:T(8,128)S(1)} %get-tuple-element.39, f32[16,64]{1,0:T(8,128)S(1)} %get-tuple-element.38, f32[16,1024]{1,0:T(8,128)S(1)} %convert_element_type.36, f32[16,1024]{1,0:T(8,128)} %param.13, f32[16,1024]{1,0:T(8,128)} %param.14, f32[16,32]{1,0:T(8,128)} %param.15, f32[16,32]{1,0:T(8,128)} %param.16, ...), dimensions={1} | concatenate | bytes 421888 | tf_op jit(solution)/shard_map/concatenate | solution.py:248
  3.3 0.6 fusion.52
  3.9 2.0 %collective-permute-start.2 = (f32[4,3296]{1,0:T(4,128)}, f32[4,3296]{1,0:T(4,128)S(1)}, u32[]{:S(2)}, u32[]{:S(2)}) collective-permute-start(f32[4,3296]{1,0:T(4,128)} %get-tuple-element.36), channel_id=1, source_target_pairs={{0,16},{16,32},{32,48},{48,64},{64,80},{80,96},{96,112},{112,128},... | collective-permute-start | bytes 158216 | tf_op jit(solution)/shard_map/ppermute | solution.py:29
  5.9 5.3 %collective-permute-start.3 = (f32[4,3296]{1,0:T(4,128)S(1)}, f32[4,3296]{1,0:T(4,128)S(1)}, u32[]{:S(2)}, u32[]{:S(2)}) collective-permute-start(f32[4,3296]{1,0:T(4,128)S(1)} %get-tuple-element.37), channel_id=1, source_target_pairs={{16,0},{32,16},{48,32},{64,48},{80,64},{96,80},{112,96},{128,112},... | collective-permute-start | bytes 158216 | tf_op jit(solution)/shard_map/ppermute | solution.py:31
  11.3 2.7 %fusion.51 = (f32[16,2,4,1024]{3,2,1,0:T(4,128)}, f32[16,2,4,1024]{3,2,1,0:T(4,128)S(1)}) fusion(f32[16,2,16,1024]{3,2,1,0:T(8,128)} %param.9), kind=kLoop, calls=%fused_computation.204 | loop fusion | bytes 2097152 | tf_op jit(solution)/shard_map/slice | solution.py:145
  14.0 1.3 %copy.19 = f32[16,2,4,1024]{3,0,2,1:T(8,128)S(1)} copy(f32[16,2,4,1024]{3,2,1,0:T(4,128)} %get-tuple-element.24) | data formatting | bytes 1048576
  15.7 1.8 %copy.20 = f32[64,8,8,128]{3,2,1,0:T(8,128)} copy(f32[64,8,8,128]{3,1,2,0:T(8,128)S(1)} %bitcast.420) | data formatting | bytes 4194304
  17.8 2.5 %collective-permute-start.4 = (f32[2,24,64]{2,1,0:T(8,128)S(1)}, f32[2,24,64]{2,1,0:T(8,128)S(1)}, u32[]{:S(2)}, u32[]{:S(2)}) collective-permute-start(f32[2,24,64]{2,1,0:T(8,128)S(1)} %pad_maximum_fusion.1), channel_id=1, source_target_pairs={{0,8},{1,9},{2,10},{3,11},{4,12},{5,13},{6,14},{7,15},{8,0},{9,1},... | collective-permute-start | bytes 36872 | tf_op jit(solution)/shard_map/ppermute | solution.py:45
  21.2 0.8 %collective-permute-done.4 = f32[2,24,64]{2,1,0:T(8,128)S(1)} collective-permute-done((f32[2,24,64]{2,1,0:T(8,128)S(1)}, f32[2,24,64]{2,1,0:T(8,128)S(1)}, u32[]{:S(2)}, u32[]{:S(2)}) %collective-permute-start.4) | collective-permute-done | bytes 12320 | tf_op jit(solution)/shard_map/ppermute | solution.py:45
  22.1 2.1 %collective-permute-start.11 = (f32[2,24,64]{2,1,0:T(8,128)S(1)}, f32[2,24,64]{2,1,0:T(8,128)S(1)}, u32[]{:S(2)}, u32[]{:S(2)}) collective-permute-start(f32[2,24,64]{2,1,0:T(8,128)S(1)} %broadcast_select_fusion), channel_id=1, source_target_pairs={{0,1},{1,0},{2,3},{3,2},{4,5},{5,4},{6,7},{7,6},{8,9},{9,8},{10,11... | collective-permute-start | bytes 36872 | tf_op jit(solution)/shard_map/ppermute | solution.py:50
  24.2 1.3 %collective-permute-start.10 = (f32[2,24,64]{2,1,0:T(8,128)S(1)}, f32[2,24,64]{2,1,0:T(8,128)S(1)}, u32[]{:S(2)}, u32[]{:S(2)}) collective-permute-start(f32[2,24,64]{2,1,0:T(8,128)S(1)} %broadcast_select_fusion), channel_id=1, source_target_pairs={{0,2},{1,3},{2,0},{3,1},{4,6},{5,7},{6,4},{7,5},{8,10},{9,11},{10,... | collective-permute-start | bytes 36872 | tf_op jit(solution)/shard_map/ppermute | solution.py:50
  25.5 0.5 collective-permute-start.9
  26.0 2.9 %collective-permute-start.8 = (f32[2,24,64]{2,1,0:T(8,128)S(1)}, f32[2,24,64]{2,1,0:T(8,128)S(1)}, u32[]{:S(2)}, u32[]{:S(2)}) collective-permute-start(f32[2,24,64]{2,1,0:T(8,128)S(1)} %broadcast_select_fusion), channel_id=1, source_target_pairs={{0,4},{1,5},{2,6},{3,7},{4,0},{5,1},{6,2},{7,3},{8,12},{9,13},{10,... | collective-permute-start | bytes 36872 | tf_op jit(solution)/shard_map/ppermute | solution.py:50
  29.3 2.7 %collective-permute-start.6 = (f32[2,24,64]{2,1,0:T(8,128)S(1)}, f32[2,24,64]{2,1,0:T(8,128)S(1)}, u32[]{:S(2)}, u32[]{:S(2)}) collective-permute-start(f32[2,24,64]{2,1,0:T(8,128)S(1)} %broadcast_select_fusion), channel_id=1, source_target_pairs={{0,6},{1,7},{2,4},{3,5},{4,2},{5,3},{6,0},{7,1},{8,14},{9,15},{10,... | collective-permute-start | bytes 36872 | tf_op jit(solution)/shard_map/ppermute | solution.py:50
  32.3 0.8 %pad.43 = f32[16,24,128]{2,1,0:T(8,128)} pad(f32[16,24,32]{2,1,0:T(8,128)S(1)} %compare_select_fusion, f32[]{:T(128)} %constant.128.clone.1), padding=0_0x0_0x0_96 | pad | bytes 245764 | tf_op jit(solution)/shard_map/jit(_pad)/pad | solution.py:155
  33.1 3.6 %collective-permute-start.1 = (f32[16,2,4,1024]{3,0,2,1:T(8,128)S(1)}, f32[16,2,4,1024]{3,0,2,1:T(8,128)S(1)}, u32[]{:S(2)}, u32[]{:S(2)}) collective-permute-start(f32[16,2,4,1024]{3,0,2,1:T(8,128)S(1)} %copy.19), channel_id=1, source_target_pairs={{16,0},{32,16},{48,32},{64,48},{80,64},{96,80},{112,96},{128,112},... | collective-permute-start | bytes 1572872 | tf_op jit(solution)/shard_map/ppermute | solution.py:148
  37.7 0.8 %copy.31 = f32[12,8,8,128]{3,2,1,0:T(8,128)} copy(f32[12,8,8,128]{3,1,2,0:T(8,128)S(1)} %bitcast.424) | data formatting | bytes 786432
  38.5 17.3 %collective-permute-done = f32[16,2,4,1024]{3,0,2,1:T(8,128)S(1)} collective-permute-done((f32[16,2,4,1024]{3,0,2,1:T(8,128)S(1)}, f32[16,2,4,1024]{3,0,2,1:T(8,128)S(1)}, u32[]{:S(2)}, u32[]{:S(2)}) %collective-permute-start) | collective-permute-done | bytes 524320 | tf_op jit(solution)/shard_map/ppermute | solution.py:147
  56.0 0.9 %copy.16.west_ref = f32[16,2,4,8,128]{4,3,2,1,0:T(8,128)} copy(f32[16,2,4,8,128]{4,3,0,2,1:T(8,128)S(1)} %bitcast.421) | data formatting | bytes 1048576 | tf_op jit(solution)/shard_map/reshape | solution.py:235
  56.8 0.9 %collective-permute-done.1 = f32[16,2,4,1024]{3,0,2,1:T(8,128)S(1)} collective-permute-done((f32[16,2,4,1024]{3,0,2,1:T(8,128)S(1)}, f32[16,2,4,1024]{3,0,2,1:T(8,128)S(1)}, u32[]{:S(2)}, u32[]{:S(2)}) %collective-permute-start.1) | collective-permute-done | bytes 524320 | tf_op jit(solution)/shard_map/ppermute | solution.py:148
  57.9 0.9 %copy.17.east_ref = f32[16,2,4,8,128]{4,3,2,1,0:T(8,128)} copy(f32[16,2,4,8,128]{4,3,0,2,1:T(8,128)S(1)} %bitcast.422) | data formatting | bytes 1048576 | tf_op jit(solution)/shard_map/reshape | solution.py:235
  58.7 7.9 %shard_map.91 = f32[16,2,16,1024]{3,2,1,0:T(8,128)} custom-call(f32[16,2,16,8,128]{4,3,2,1,0:T(8,128)} %bitcast.419, f32[16,2,4,8,128]{4,3,2,1,0:T(8,128)} %copy.16.west_ref, f32[16,2,4,8,128]{4,3,2,1,0:T(8,128)} %copy.17.east_ref, f32[8,24,8,128]{3,2,1,0:T(8,128)} %copy-done.2, f32[2,2,24,8,128]{4,3,2,1,0:T(8,128)} %bitcast.423, f32[16,24,1,128]{3,2,1,0:T(1,128)} %bitcast.429), custom_call_target="tpu_custom_call" | custom-call | tf_op jit(solution)/shard_map/pallas_call | solution.py:214
  (80 shorter events, 3.2 us)
Async XLA Ops:
  0.0 2.3 %copy-start = (f32[4,2,16,1024]{3,2,1,0:T(8,128)S(1)}, f32[4,2,16,1024]{3,2,1,0:T(8,128)}, u32[]{:S(2)}) copy-start(f32[4,2,16,1024]{3,2,1,0:T(8,128)} %param.10) | copy-start | bytes 1572868
  3.9 13.6 %collective-permute-start.2 = (f32[4,3296]{1,0:T(4,128)}, f32[4,3296]{1,0:T(4,128)S(1)}, u32[]{:S(2)}, u32[]{:S(2)}) collective-permute-start(f32[4,3296]{1,0:T(4,128)} %get-tuple-element.36), channel_id=1, source_target_pairs={{0,16},{16,32},{32,48},{48,64},{64,80},{80,96},{96,112},{112,128},... | collective-permute-start | bytes 158216 | tf_op jit(solution)/shard_map/ppermute | solution.py:29
  5.9 11.5 %collective-permute-start.3 = (f32[4,3296]{1,0:T(4,128)S(1)}, f32[4,3296]{1,0:T(4,128)S(1)}, u32[]{:S(2)}, u32[]{:S(2)}) collective-permute-start(f32[4,3296]{1,0:T(4,128)S(1)} %get-tuple-element.37), channel_id=1, source_target_pairs={{16,0},{32,16},{48,32},{64,48},{80,64},{96,80},{112,96},{128,112},... | collective-permute-start | bytes 158216 | tf_op jit(solution)/shard_map/ppermute | solution.py:31
  11.3 4.4 %copy-start.1 = (f32[16,2,16,1024]{3,2,1,0:T(8,128)S(1)}, f32[16,2,16,1024]{3,2,1,0:T(8,128)}, u32[]{:S(2)}) copy-start(f32[16,2,16,1024]{3,2,1,0:T(8,128)} %param.9) | copy-start | bytes 6291460
  17.8 4.3 %collective-permute-start.4 = (f32[2,24,64]{2,1,0:T(8,128)S(1)}, f32[2,24,64]{2,1,0:T(8,128)S(1)}, u32[]{:S(2)}, u32[]{:S(2)}) collective-permute-start(f32[2,24,64]{2,1,0:T(8,128)S(1)} %pad_maximum_fusion.1), channel_id=1, source_target_pairs={{0,8},{1,9},{2,10},{3,11},{4,12},{5,13},{6,14},{7,15},{8,0},{9,1},... | collective-permute-start | bytes 36872 | tf_op jit(solution)/shard_map/ppermute | solution.py:45
  22.1 7.2 %collective-permute-start.11 = (f32[2,24,64]{2,1,0:T(8,128)S(1)}, f32[2,24,64]{2,1,0:T(8,128)S(1)}, u32[]{:S(2)}, u32[]{:S(2)}) collective-permute-start(f32[2,24,64]{2,1,0:T(8,128)S(1)} %broadcast_select_fusion), channel_id=1, source_target_pairs={{0,1},{1,0},{2,3},{3,2},{4,5},{5,4},{6,7},{7,6},{8,9},{9,8},{10,11... | collective-permute-start | bytes 36872 | tf_op jit(solution)/shard_map/ppermute | solution.py:50
  24.2 7.9 %collective-permute-start.10 = (f32[2,24,64]{2,1,0:T(8,128)S(1)}, f32[2,24,64]{2,1,0:T(8,128)S(1)}, u32[]{:S(2)}, u32[]{:S(2)}) collective-permute-start(f32[2,24,64]{2,1,0:T(8,128)S(1)} %broadcast_select_fusion), channel_id=1, source_target_pairs={{0,2},{1,3},{2,0},{3,1},{4,6},{5,7},{6,4},{7,5},{8,10},{9,11},{10,... | collective-permute-start | bytes 36872 | tf_op jit(solution)/shard_map/ppermute | solution.py:50
  25.5 7.5 %collective-permute-start.9 = (f32[2,24,64]{2,1,0:T(8,128)S(1)}, f32[2,24,64]{2,1,0:T(8,128)S(1)}, u32[]{:S(2)}, u32[]{:S(2)}) collective-permute-start(f32[2,24,64]{2,1,0:T(8,128)S(1)} %broadcast_select_fusion), channel_id=1, source_target_pairs={{0,3},{1,2},{2,1},{3,0},{4,7},{5,6},{6,5},{7,4},{8,11},{9,10},{10,... | collective-permute-start | bytes 36872 | tf_op jit(solution)/shard_map/ppermute | solution.py:50
  26.0 7.0 %collective-permute-start.8 = (f32[2,24,64]{2,1,0:T(8,128)S(1)}, f32[2,24,64]{2,1,0:T(8,128)S(1)}, u32[]{:S(2)}, u32[]{:S(2)}) collective-permute-start(f32[2,24,64]{2,1,0:T(8,128)S(1)} %broadcast_select_fusion), channel_id=1, source_target_pairs={{0,4},{1,5},{2,6},{3,7},{4,0},{5,1},{6,2},{7,3},{8,12},{9,13},{10,... | collective-permute-start | bytes 36872 | tf_op jit(solution)/shard_map/ppermute | solution.py:50
  29.0 7.7 %collective-permute-start.7 = (f32[2,24,64]{2,1,0:T(8,128)S(1)}, f32[2,24,64]{2,1,0:T(8,128)S(1)}, u32[]{:S(2)}, u32[]{:S(2)}) collective-permute-start(f32[2,24,64]{2,1,0:T(8,128)S(1)} %broadcast_select_fusion), channel_id=1, source_target_pairs={{0,5},{1,4},{2,7},{3,6},{4,1},{5,0},{6,3},{7,2},{8,13},{9,12},{10,... | collective-permute-start | bytes 36872 | tf_op jit(solution)/shard_map/ppermute | solution.py:50
  29.3 7.3 %collective-permute-start.6 = (f32[2,24,64]{2,1,0:T(8,128)S(1)}, f32[2,24,64]{2,1,0:T(8,128)S(1)}, u32[]{:S(2)}, u32[]{:S(2)}) collective-permute-start(f32[2,24,64]{2,1,0:T(8,128)S(1)} %broadcast_select_fusion), channel_id=1, source_target_pairs={{0,6},{1,7},{2,4},{3,5},{4,2},{5,3},{6,0},{7,1},{8,14},{9,15},{10,... | collective-permute-start | bytes 36872 | tf_op jit(solution)/shard_map/ppermute | solution.py:50
  32.1 4.6 %collective-permute-start.5 = (f32[2,24,64]{2,1,0:T(8,128)S(1)}, f32[2,24,64]{2,1,0:T(8,128)S(1)}, u32[]{:S(2)}, u32[]{:S(2)}) collective-permute-start(f32[2,24,64]{2,1,0:T(8,128)S(1)} %broadcast_select_fusion), channel_id=1, source_target_pairs={{0,7},{1,6},{2,5},{3,4},{4,3},{5,2},{6,1},{7,0},{8,15},{9,14},{10,... | collective-permute-start | bytes 36872 | tf_op jit(solution)/shard_map/ppermute | solution.py:50
  32.3 23.7 %copy-start.2 = (f32[8,24,8,128]{3,2,1,0:T(8,128)}, f32[8,24,8,128]{3,2,1,0:T(8,128)S(1)}, u32[]{:S(2)}) copy-start(f32[8,24,8,128]{3,2,1,0:T(8,128)S(1)} %bitcast_dynamic-update-slice_fusion.w_ref) | copy-start | bytes 2359300
  33.1 22.8 %collective-permute-start = (f32[16,2,4,1024]{3,0,2,1:T(8,128)S(1)}, f32[16,2,4,1024]{3,0,2,1:T(8,128)S(1)}, u32[]{:S(2)}, u32[]{:S(2)}) collective-permute-start(f32[16,2,4,1024]{3,0,2,1:T(8,128)S(1)} %copy.18), channel_id=1, source_target_pairs={{0,16},{16,32},{32,48},{48,64},{64,80},{80,96},{96,112},{112,128},... | collective-permute-start | bytes 1572872 | tf_op jit(solution)/shard_map/ppermute | solution.py:147
  33.1 24.7 %collective-permute-start.1 = (f32[16,2,4,1024]{3,0,2,1:T(8,128)S(1)}, f32[16,2,4,1024]{3,0,2,1:T(8,128)S(1)}, u32[]{:S(2)}, u32[]{:S(2)}) collective-permute-start(f32[16,2,4,1024]{3,0,2,1:T(8,128)S(1)} %copy.19), channel_id=1, source_target_pairs={{16,0},{32,16},{48,32},{64,48},{80,64},{96,80},{112,96},{128,112},... | collective-permute-start | bytes 1572872 | tf_op jit(solution)/shard_map/ppermute | solution.py:148

commit v13 on v11

--- a/solution.py
+++ b/solution.py
@@ -210,7 +210,7 @@
     groups, tracers, local, sub, lanes = center.shape
     rim = west.shape[2]
     span = local + 2 * rim
-    pack = 8 if groups % 8 == 0 else 1
+    pack = 4 if groups % 4 == 0 else 1
     return pl.pallas_call(
         retreat_kernel,
         out_shape=jax.ShapeDtypeStruct((groups, tracers, local, sub * lanes), center.dtype),
@@ -245,16 +245,17 @@
     owner_index = interval[0] % owners
     band = 2 * ROWS
     stored = lax.dynamic_index_in_dim(checkpoint_store, interval[0] // owners, 0, keepdims=False)
+    whole = jnp.concatenate([sea_mask, region], axis=1).astype(jnp.float32)
     statics = jnp.concatenate(
         [
             stored[0, :, :band],
             stored[1, :, :band],
-            sea_mask.astype(jnp.float32),
+            whole[:, :cell_count],
             zonal_speed,
             mixing,
             piston,
             cell_area,
-            region.astype(jnp.float32),
+            whole[:, cell_count:],
         ],
         axis=1,
     )

time: 63.7 us -> 63.5 us (level)
    slice x0 -> x1, other arithmetic: none -> 0.71 us  [staged(): whole[:, cell_count:]]
    convert_element_type x2 -> x1, other arithmetic: 1.54 us -> 0.86 us  [staged(): whole = jnp.concatenate([sea_mask, region], axis=1).astype(jnp.float32)]
where the time goes in v13:
time: 63.5 us; the launch traced here: 63.2 us
  starting transfers between devices  22.9 us (36%)
  waiting for transfers between devices  20.4 us (32%)
  local copies, waits for them, and re-layouts  8.12 us (13%)
  Pallas kernels  7.87 us (12%)
  other arithmetic  2.75 us (4%)
  between operations  1.14 us (2%)
    ppermute x1, waiting for transfers between devices, halves(): lax.ppermute(head, axis, [((i + 1) % count, i) for i in range(count)])  19.1 us
    ppermute x7, starting transfers between devices, spread(): moved = lax.ppermute(value, axis, [(i, i ^ mask) for i in range(count)])  10.1 us
    pallas_call x1, Pallas kernels, two_retreats(): pl.pallas_call(retreat_kernel, out_shape=jax.ShapeDtypeStruct((groups, tr...  7.87 us
    ppermute x1, starting transfers between devices, padded(): lax.ppermute(head, axis, [((i + 1) % count, i) for i in range(count)])  5.3 us
    unnamed x34, local copies, waits for them, and re-layouts  4.34 us
    ppermute x1, starting transfers between devices, halves(): lax.ppermute(head, axis, [((i + 1) % count, i) for i in range(count)])  2.93 us
    ppermute x1, starting transfers between devices, spread(): moved = lax.ppermute(value, axis, [(i, i ^ top) for i in range(count)])  2.53 us
    ppermute x1, starting transfers between devices, padded(): lax.ppermute(tail, axis, [(i, (i + 1) % count) for i in range(count)])  2.03 us
  transfers between devices with their start and end apart: 12, of which 3 were waited for; matrix products, arithmetic and copies ran while one was open for 10% of the time, Pallas kernels for 0%

profile of v13, /device:TPU:1, one launch (start us, length us, event | category | flops | bytes accessed | tf_op | source)
XLA Modules:
  0.0 63.2 jit_solution(13777997571335272503)
XLA Ops:
  0.7 0.7 %add_convert_fusion.1 = f32[16,32]{1,0:T(8,128)S(1)} fusion(s32[16,32]{1,0:T(8,128)} %param.17, s32[16,1024]{1,0:T(8,128)} %param.12), kind=kLoop, calls=%fused_computation.184 | loop fusion | flops 1024 | bytes 69632 | tf_op jit(solution)/shard_map/slice | solution.py:258
  1.4 0.9 %add_convert_fusion = f32[16,1056]{1,0:T(8,128)S(1)} fusion(s32[16,32]{1,0:T(8,128)} %param.17, s32[16,1024]{1,0:T(8,128)} %param.12), kind=kLoop, calls=%fused_computation.32 | loop fusion | flops 33792 | bytes 135168 | tf_op jit(solution)/shard_map/convert_element_type | solution.py:248
  2.4 1.0 %concatenate.41 = f32[16,3296]{1,0:T(8,128)S(1)} concatenate(f32[16,64]{1,0:T(8,128)S(1)} %get-tuple-element.39, f32[16,64]{1,0:T(8,128)S(1)} %get-tuple-element.38, f32[16,1024]{1,0:T(8,128)S(1)} %slice.235, f32[16,1024]{1,0:T(8,128)} %param.13, f32[16,1024]{1,0:T(8,128)} %param.14, f32[16,32]{1,0:T(8,128)} %param.15, f32[16,32]{1,0:T(8,128)} %param.16, ...), dimensions={1} | concatenate | bytes 421888 | tf_op jit(solution)/shard_map/concatenate | solution.py:249
  3.3 0.6 %fusion.52 = (f32[4,3296]{1,0:T(4,128)}, f32[4,3296]{1,0:T(4,128)S(1)}) fusion(f32[16,3296]{1,0:T(8,128)S(1)} %concatenate.41), kind=kLoop, calls=%fused_computation.207 | loop fusion | bytes 210944 | tf_op jit(solution)/shard_map/slice | solution.py:26
  4.0 2.0 %collective-permute-start.2 = (f32[4,3296]{1,0:T(4,128)}, f32[4,3296]{1,0:T(4,128)S(1)}, u32[]{:S(2)}, u32[]{:S(2)}) collective-permute-start(f32[4,3296]{1,0:T(4,128)} %get-tuple-element.36), channel_id=1, source_target_pairs={{0,16},{16,32},{32,48},{48,64},{64,80},{80,96},{96,112},{112,128},... | collective-permute-start | bytes 158216 | tf_op jit(solution)/shard_map/ppermute | solution.py:29
  6.0 5.3 %collective-permute-start.3 = (f32[4,3296]{1,0:T(4,128)S(1)}, f32[4,3296]{1,0:T(4,128)S(1)}, u32[]{:S(2)}, u32[]{:S(2)}) collective-permute-start(f32[4,3296]{1,0:T(4,128)S(1)} %get-tuple-element.37), channel_id=1, source_target_pairs={{16,0},{32,16},{48,32},{64,48},{80,64},{96,80},{112,96},{128,112},... | collective-permute-start | bytes 158216 | tf_op jit(solution)/shard_map/ppermute | solution.py:31
  11.3 2.1 %copy.10 = f32[64,8,8,128]{3,2,1,0:T(8,128)S(1)} copy(f32[64,8,8,128]{3,1,2,0:T(8,128)} %bitcast.407) | data formatting | bytes 4194304
  13.4 0.9 %fusion.51 = (f32[16,2,4,8,128]{4,3,2,1,0:T(8,128)}, f32[16,2,4,8,128]{4,3,2,1,0:T(8,128)S(1)}) fusion(f32[16,2,16,8,128]{4,3,2,1,0:T(8,128)S(1)} %bitcast.405), kind=kLoop, calls=%fused_computation.206 | loop fusion | bytes 2097152 | tf_op jit(solution)/shard_map/slice | solution.py:145
  14.7 2.5 %collective-permute-start.4 = (f32[2,24,64]{2,1,0:T(8,128)S(1)}, f32[2,24,64]{2,1,0:T(8,128)S(1)}, u32[]{:S(2)}, u32[]{:S(2)}) collective-permute-start(f32[2,24,64]{2,1,0:T(8,128)S(1)} %pad_maximum_fusion.1), channel_id=1, source_target_pairs={{0,8},{1,9},{2,10},{3,11},{4,12},{5,13},{6,14},{7,15},{8,0},{9,1},... | collective-permute-start | bytes 36872 | tf_op jit(solution)/shard_map/ppermute | solution.py:45
  18.1 0.8 %collective-permute-done.4 = f32[2,24,64]{2,1,0:T(8,128)S(1)} collective-permute-done((f32[2,24,64]{2,1,0:T(8,128)S(1)}, f32[2,24,64]{2,1,0:T(8,128)S(1)}, u32[]{:S(2)}, u32[]{:S(2)}) %collective-permute-start.4) | collective-permute-done | bytes 12320 | tf_op jit(solution)/shard_map/ppermute | solution.py:45
  18.9 2.1 %collective-permute-start.11 = (f32[2,24,64]{2,1,0:T(8,128)S(1)}, f32[2,24,64]{2,1,0:T(8,128)S(1)}, u32[]{:S(2)}, u32[]{:S(2)}) collective-permute-start(f32[2,24,64]{2,1,0:T(8,128)S(1)} %broadcast_select_fusion), channel_id=1, source_target_pairs={{0,1},{1,0},{2,3},{3,2},{4,5},{5,4},{6,7},{7,6},{8,9},{9,8},{10,11... | collective-permute-start | bytes 36872 | tf_op jit(solution)/shard_map/ppermute | solution.py:50
  21.0 1.3 %collective-permute-start.10 = (f32[2,24,64]{2,1,0:T(8,128)S(1)}, f32[2,24,64]{2,1,0:T(8,128)S(1)}, u32[]{:S(2)}, u32[]{:S(2)}) collective-permute-start(f32[2,24,64]{2,1,0:T(8,128)S(1)} %broadcast_select_fusion), channel_id=1, source_target_pairs={{0,2},{1,3},{2,0},{3,1},{4,6},{5,7},{6,4},{7,5},{8,10},{9,11},{10,... | collective-permute-start | bytes 36872 | tf_op jit(solution)/shard_map/ppermute | solution.py:50
  22.4 0.5 collective-permute-start.9
  22.9 2.9 %collective-permute-start.8 = (f32[2,24,64]{2,1,0:T(8,128)S(1)}, f32[2,24,64]{2,1,0:T(8,128)S(1)}, u32[]{:S(2)}, u32[]{:S(2)}) collective-permute-start(f32[2,24,64]{2,1,0:T(8,128)S(1)} %broadcast_select_fusion), channel_id=1, source_target_pairs={{0,4},{1,5},{2,6},{3,7},{4,0},{5,1},{6,2},{7,3},{8,12},{9,13},{10,... | collective-permute-start | bytes 36872 | tf_op jit(solution)/shard_map/ppermute | solution.py:50
  25.8 0.4 collective-permute-start.7
  26.2 2.7 %collective-permute-start.6 = (f32[2,24,64]{2,1,0:T(8,128)S(1)}, f32[2,24,64]{2,1,0:T(8,128)S(1)}, u32[]{:S(2)}, u32[]{:S(2)}) collective-permute-start(f32[2,24,64]{2,1,0:T(8,128)S(1)} %broadcast_select_fusion), channel_id=1, source_target_pairs={{0,6},{1,7},{2,4},{3,5},{4,2},{5,3},{6,0},{7,1},{8,14},{9,15},{10,... | collective-permute-start | bytes 36872 | tf_op jit(solution)/shard_map/ppermute | solution.py:50
  29.2 0.7 %pad.43 = f32[16,24,128]{2,1,0:T(8,128)} pad(f32[16,24,32]{2,1,0:T(8,128)S(1)} %compare_select_fusion, f32[]{:T(128)} %constant.128.clone.1), padding=0_0x0_0x0_96 | pad | bytes 245764 | tf_op jit(solution)/shard_map/jit(_pad)/pad | solution.py:155
  29.9 2.9 %collective-permute-start.1 = (f32[16,2,4,8,128]{4,3,2,1,0:T(8,128)S(1)}, f32[16,2,4,8,128]{4,3,2,1,0:T(8,128)S(1)}, u32[]{:S(2)}, u32[]{:S(2)}) collective-permute-start(f32[16,2,4,8,128]{4,3,2,1,0:T(8,128)S(1)} %copy-done.5), channel_id=1, source_target_pairs={{16,0},{32,16},{48,32},{64,48},{80,64},{96,80},{112,96},{128,112},... | collective-permute-start | bytes 1572872 | tf_op jit(solution)/shard_map/ppermute | solution.py:148
  32.9 0.5 collective-permute-done.5
  33.9 0.3 add_bitcast_fusion.3
  34.4 0.8 %copy.19 = f32[12,8,8,128]{3,2,1,0:T(8,128)} copy(f32[12,8,8,128]{3,1,2,0:T(8,128)S(1)} %bitcast.409) | data formatting | bytes 786432
  35.3 19.1 %collective-permute-done.1.east_ref = f32[16,2,4,8,128]{4,3,2,1,0:T(8,128)S(1)} collective-permute-done((f32[16,2,4,8,128]{4,3,2,1,0:T(8,128)S(1)}, f32[16,2,4,8,128]{4,3,2,1,0:T(8,128)S(1)}, u32[]{:S(2)}, u32[]{:S(2)}) %collective-permute-start.1) | collective-permute-done | bytes 524320 | tf_op jit(solution)/shard_map/ppermute | solution.py:148
  54.4 0.8 %copy-done.3 = f32[16,2,4,8,128]{4,3,2,1,0:T(8,128)} copy-done((f32[16,2,4,8,128]{4,3,2,1,0:T(8,128)}, f32[16,2,4,8,128]{4,3,2,1,0:T(8,128)S(1)}, u32[]{:S(2)}) %copy-start.3) | copy-done | bytes 524312
  55.4 7.9 %shard_map.91 = f32[16,2,16,1024]{3,2,1,0:T(8,128)} custom-call(f32[16,2,16,8,128]{4,3,2,1,0:T(8,128)} %bitcast.406, f32[16,2,4,8,128]{4,3,2,1,0:T(8,128)} %copy-done.4, f32[16,2,4,8,128]{4,3,2,1,0:T(8,128)} %copy-done.3, f32[8,24,8,128]{3,2,1,0:T(8,128)} %copy-done.2, f32[2,2,24,8,128]{4,3,2,1,0:T(8,128)} %bitcast.408, f32[16,24,1,128]{3,2,1,0:T(1,128)} %bitcast.414), custom_call_target="tpu_custom_call" | custom-call | tf_op jit(solution)/shard_map/pallas_call | solution.py:214
  (81 shorter events, 2.3 us)
Async XLA Ops:
  0.0 2.3 %copy-start = (f32[4,2,16,1024]{3,2,1,0:T(8,128)S(1)}, f32[4,2,16,1024]{3,2,1,0:T(8,128)}, u32[]{:S(2)}) copy-start(f32[4,2,16,1024]{3,2,1,0:T(8,128)} %param.10) | copy-start | bytes 1572868
  4.0 10.4 %collective-permute-start.2 = (f32[4,3296]{1,0:T(4,128)}, f32[4,3296]{1,0:T(4,128)S(1)}, u32[]{:S(2)}, u32[]{:S(2)}) collective-permute-start(f32[4,3296]{1,0:T(4,128)} %get-tuple-element.36), channel_id=1, source_target_pairs={{0,16},{16,32},{32,48},{48,64},{64,80},{80,96},{96,112},{112,128},... | collective-permute-start | bytes 158216 | tf_op jit(solution)/shard_map/ppermute | solution.py:29
  6.0 8.3 %collective-permute-start.3 = (f32[4,3296]{1,0:T(4,128)S(1)}, f32[4,3296]{1,0:T(4,128)S(1)}, u32[]{:S(2)}, u32[]{:S(2)}) collective-permute-start(f32[4,3296]{1,0:T(4,128)S(1)} %get-tuple-element.37), channel_id=1, source_target_pairs={{16,0},{32,16},{48,32},{64,48},{80,64},{96,80},{112,96},{128,112},... | collective-permute-start | bytes 158216 | tf_op jit(solution)/shard_map/ppermute | solution.py:31
  13.4 3.9 %copy-start.1 = (f32[64,8,8,128]{3,2,1,0:T(8,128)}, f32[64,8,8,128]{3,2,1,0:T(8,128)S(1)}, u32[]{:S(2)}) copy-start(f32[64,8,8,128]{3,2,1,0:T(8,128)S(1)} %copy.10) | copy-start | bytes 6291460
  14.7 4.3 %collective-permute-start.4 = (f32[2,24,64]{2,1,0:T(8,128)S(1)}, f32[2,24,64]{2,1,0:T(8,128)S(1)}, u32[]{:S(2)}, u32[]{:S(2)}) collective-permute-start(f32[2,24,64]{2,1,0:T(8,128)S(1)} %pad_maximum_fusion.1), channel_id=1, source_target_pairs={{0,8},{1,9},{2,10},{3,11},{4,12},{5,13},{6,14},{7,15},{8,0},{9,1},... | collective-permute-start | bytes 36872 | tf_op jit(solution)/shard_map/ppermute | solution.py:45
  17.7 12.3 %copy-start.5 = (f32[16,2,4,8,128]{4,3,2,1,0:T(8,128)S(1)}, f32[16,2,4,8,128]{4,3,2,1,0:T(8,128)}, u32[]{:S(2)}) copy-start(f32[16,2,4,8,128]{4,3,2,1,0:T(8,128)} %get-tuple-element.24) | copy-start | bytes 1572868
  18.9 7.2 %collective-permute-start.11 = (f32[2,24,64]{2,1,0:T(8,128)S(1)}, f32[2,24,64]{2,1,0:T(8,128)S(1)}, u32[]{:S(2)}, u32[]{:S(2)}) collective-permute-start(f32[2,24,64]{2,1,0:T(8,128)S(1)} %broadcast_select_fusion), channel_id=1, source_target_pairs={{0,1},{1,0},{2,3},{3,2},{4,5},{5,4},{6,7},{7,6},{8,9},{9,8},{10,11... | collective-permute-start | bytes 36872 | tf_op jit(solution)/shard_map/ppermute | solution.py:50
  21.0 7.9 %collective-permute-start.10 = (f32[2,24,64]{2,1,0:T(8,128)S(1)}, f32[2,24,64]{2,1,0:T(8,128)S(1)}, u32[]{:S(2)}, u32[]{:S(2)}) collective-permute-start(f32[2,24,64]{2,1,0:T(8,128)S(1)} %broadcast_select_fusion), channel_id=1, source_target_pairs={{0,2},{1,3},{2,0},{3,1},{4,6},{5,7},{6,4},{7,5},{8,10},{9,11},{10,... | collective-permute-start | bytes 36872 | tf_op jit(solution)/shard_map/ppermute | solution.py:50
  22.4 7.5 %collective-permute-start.9 = (f32[2,24,64]{2,1,0:T(8,128)S(1)}, f32[2,24,64]{2,1,0:T(8,128)S(1)}, u32[]{:S(2)}, u32[]{:S(2)}) collective-permute-start(f32[2,24,64]{2,1,0:T(8,128)S(1)} %broadcast_select_fusion), channel_id=1, source_target_pairs={{0,3},{1,2},{2,1},{3,0},{4,7},{5,6},{6,5},{7,4},{8,11},{9,10},{10,... | collective-permute-start | bytes 36872 | tf_op jit(solution)/shard_map/ppermute | solution.py:50
  22.9 9.9 %collective-permute-start.8 = (f32[2,24,64]{2,1,0:T(8,128)S(1)}, f32[2,24,64]{2,1,0:T(8,128)S(1)}, u32[]{:S(2)}, u32[]{:S(2)}) collective-permute-start(f32[2,24,64]{2,1,0:T(8,128)S(1)} %broadcast_select_fusion), channel_id=1, source_target_pairs={{0,4},{1,5},{2,6},{3,7},{4,0},{5,1},{6,2},{7,3},{8,12},{9,13},{10,... | collective-permute-start | bytes 36872 | tf_op jit(solution)/shard_map/ppermute | solution.py:50
  25.8 7.0 %collective-permute-start.7 = (f32[2,24,64]{2,1,0:T(8,128)S(1)}, f32[2,24,64]{2,1,0:T(8,128)S(1)}, u32[]{:S(2)}, u32[]{:S(2)}) collective-permute-start(f32[2,24,64]{2,1,0:T(8,128)S(1)} %broadcast_select_fusion), channel_id=1, source_target_pairs={{0,5},{1,4},{2,7},{3,6},{4,1},{5,0},{6,3},{7,2},{8,13},{9,12},{10,... | collective-permute-start | bytes 36872 | tf_op jit(solution)/shard_map/ppermute | solution.py:50
  26.2 6.7 %collective-permute-start.6 = (f32[2,24,64]{2,1,0:T(8,128)S(1)}, f32[2,24,64]{2,1,0:T(8,128)S(1)}, u32[]{:S(2)}, u32[]{:S(2)}) collective-permute-start(f32[2,24,64]{2,1,0:T(8,128)S(1)} %broadcast_select_fusion), channel_id=1, source_target_pairs={{0,6},{1,7},{2,4},{3,5},{4,2},{5,3},{6,0},{7,1},{8,14},{9,15},{10,... | collective-permute-start | bytes 36872 | tf_op jit(solution)/shard_map/ppermute | solution.py:50
  28.9 4.5 %collective-permute-start.5 = (f32[2,24,64]{2,1,0:T(8,128)S(1)}, f32[2,24,64]{2,1,0:T(8,128)S(1)}, u32[]{:S(2)}, u32[]{:S(2)}) collective-permute-start(f32[2,24,64]{2,1,0:T(8,128)S(1)} %broadcast_select_fusion), channel_id=1, source_target_pairs={{0,7},{1,6},{2,5},{3,4},{4,3},{5,2},{6,1},{7,0},{8,15},{9,14},{10,... | collective-permute-start | bytes 36872 | tf_op jit(solution)/shard_map/ppermute | solution.py:50
  29.1 25.2 %copy-start.2 = (f32[8,24,8,128]{3,2,1,0:T(8,128)}, f32[8,24,8,128]{3,2,1,0:T(8,128)S(1)}, u32[]{:S(2)}) copy-start(f32[8,24,8,128]{3,2,1,0:T(8,128)S(1)} %bitcast_dynamic-update-slice_fusion.w_ref) | copy-start | bytes 2359300
  29.9 24.4 %collective-permute-start.1 = (f32[16,2,4,8,128]{4,3,2,1,0:T(8,128)S(1)}, f32[16,2,4,8,128]{4,3,2,1,0:T(8,128)S(1)}, u32[]{:S(2)}, u32[]{:S(2)}) collective-permute-start(f32[16,2,4,8,128]{4,3,2,1,0:T(8,128)S(1)} %copy-done.5), channel_id=1, source_target_pairs={{16,0},{32,16},{48,32},{64,48},{80,64},{96,80},{112,96},{128,112},... | collective-permute-start | bytes 1572872 | tf_op jit(solution)/shard_map/ppermute | solution.py:148
  32.9 21.5 %collective-permute-start = (f32[16,2,4,8,128]{4,3,2,1,0:T(8,128)S(1)}, f32[16,2,4,8,128]{4,3,2,1,0:T(8,128)S(1)}, u32[]{:S(2)}, u32[]{:S(2)}) collective-permute-start(f32[16,2,4,8,128]{4,3,2,1,0:T(8,128)S(1)} %get-tuple-element.25), channel_id=1, source_target_pairs={{0,16},{16,32},{32,48},{48,64},{64,80},{80,96},{96,112},{112,128},... | collective-permute-start | bytes 1572872 | tf_op jit(solution)/shard_map/ppermute | solution.py:147
  54.4 0.8 %copy-start.3 = (f32[16,2,4,8,128]{4,3,2,1,0:T(8,128)}, f32[16,2,4,8,128]{4,3,2,1,0:T(8,128)S(1)}, u32[]{:S(2)}) copy-start(f32[16,2,4,8,128]{4,3,2,1,0:T(8,128)S(1)} %collective-permute-done.1.east_ref) | copy-start | bytes 1572868
  54.4 1.0 %copy-start.4 = (f32[16,2,4,8,128]{4,3,2,1,0:T(8,128)}, f32[16,2,4,8,128]{4,3,2,1,0:T(8,128)S(1)}, u32[]{:S(2)}) copy-start(f32[16,2,4,8,128]{4,3,2,1,0:T(8,128)S(1)} %collective-permute-done.west_ref) | copy-start | bytes 1572868
